TPU v7x, 256 devices: a whole 4x4x8 slice. The times are simulated.
256 devices in a mesh: lon: 32 (over x_hi, z, core), lat: 8 (over x_lo, y).
Axes of the slice: x: 4 (x_hi: 2, x_lo: 2; x = x_hi * 2 + x_lo), y: 4, z: 8, core: 2. Of those that a mesh axis runs over, the one named last changes fastest.
Arguments:
- tracer_start: float32 [3, 16, 128, 4096], P(None, None, 'lat', 'lon'), may hold values from -6 to 6
- source: float32 [3, 16, 128, 4096], P(None, None, 'lat', 'lon'), may hold values from -3 to 3
- target: float32 [3, 16, 128, 4096], P(None, None, 'lat', 'lon'), may hold values from -27 to 27
- east_vel: float32 [16, 128, 4096], P(None, 'lat', 'lon'), may hold values from -0.12 to 0.12
- north_vel: float32 [16, 128, 4096], P(None, 'lat', 'lon'), may hold values from -0.12 to 0.12
- vertical_vel: float32 [16, 128, 4096], P(None, 'lat', 'lon'), may hold values from -0.12 to 0.12
- diffusivity: float32 [16, 128, 4096], P(None, 'lat', 'lon'), may hold values from 0.01 to 0.04
- sea_mask: int32 [16, 128, 4096], P(None, 'lat', 'lon'), may hold values 0 or 1
- reaction_rate: float32 [3, 16], replicated, may hold values from 0.05 to 0.5
- fold_partner: int32 [4096], P('lon'), may hold values from 0 to 4095, as said below
Outputs:
- source_grad: float32 [3, 16, 128, 4096], P(None, None, 'lat', 'lon')
- grad_norm: float32 [], replicated
Inputs may be any that keep to these rules, and one draw needn't show every extreme that they name: fold_partner[fold_partner[i]] = i; column i meets column (s - i) mod 4096 across the fold, for one s of each draw.
All inputs are finite; a program needn't handle non-finite values. No bound on the sum of `sea_mask` on one device may be relied on, other than what follows from the above.
Results may differ from a plain program's by a relative error of at most 0.00002.
Values sent between devices are 32-bit elements; how exact they have to be, the bound alone decides.
No kernel may reach another device: no remote copies, remote signals or barrier semaphores. Data moves between devices by JAX's collectives and lax.ppermute only.
A program may use at most 64 MiB of HBM per device.

v0:
```python
import jax
import jax.numpy as jnp
from jax import lax
from jax.sharding import PartitionSpec as P

STEPS = 4


def with_halo(block, sides, width, periodic):
    for axis, dim in sides:
        count = lax.axis_size(axis)
        forward = [(i, i + 1) for i in range(count - 1)]
        if periodic:
            forward.append((count - 1, 0))
        backward = [(target, source) for source, target in forward]
        low = lax.ppermute(
            lax.slice_in_dim(block, block.shape[dim] - width, None, axis=dim), axis, forward
        )
        high = lax.ppermute(lax.slice_in_dim(block, 0, width, axis=dim), axis, backward)
        block = jnp.concatenate([low, block, high], axis=dim)
    return block


def upwind_pair(velocity, mixing, face_sea):
    flow_rate = velocity * face_sea
    mixing_part = mixing * face_sea
    return (jnp.maximum(flow_rate, 0.0) + mixing_part, jnp.minimum(flow_rate, 0.0) - mixing_part)


def on_device(
    tracer_start,
    source,
    target,
    east_vel,
    north_vel,
    vertical_vel,
    diffusivity,
    sea_mask,
    reaction_rate,
    fold_partner,
):
    ocean = sea_mask.astype(jnp.float32)
    statics = jnp.stack([east_vel, north_vel, diffusivity, ocean])
    wide_static = with_halo(statics, (("lon", 3),), 1, True)
    tall_static = with_halo(statics, (("lat", 2),), 1, False)
    west_cell = wide_static[..., :-1]
    east_cell = wide_static[..., 1:]
    east_own, east_next = upwind_pair(
        west_cell[0], 0.5 * (west_cell[2] + east_cell[2]), west_cell[3] * east_cell[3]
    )
    below_row = tall_static[:, :, :-1, :]
    above_row = tall_static[:, :, 1:, :]
    north_own, north_next = upwind_pair(
        below_row[1], 0.5 * (below_row[2] + above_row[2]), below_row[3] * above_row[3]
    )
    up_own, up_next = upwind_pair(
        vertical_vel[:-1], 0.5 * (diffusivity[:-1] + diffusivity[1:]), ocean[:-1] * ocean[1:]
    )
    top_static = jnp.stack([north_vel[:, -1, :], diffusivity[:, -1, :], ocean[:, -1, :]])
    fold_all = lax.all_gather(top_static, "lon", axis=2, tiled=True)
    across = jnp.take(fold_all, fold_partner, axis=2)
    north_top = (lax.axis_index("lat") == lax.axis_size("lat") - 1).astype(jnp.float32)
    fold_own, fold_next = upwind_pair(
        0.5 * (top_static[0] - across[0]),
        0.5 * (top_static[1] + across[1]),
        top_static[2] * across[2] * north_top,
    )
    decay_rate = reaction_rate[:, :, None, None]

    def neighbours(quantity):
        east_west = with_halo(quantity, (("lon", 3),), 1, True)
        south_north = with_halo(quantity, (("lat", 2),), 1, False)
        top_row = quantity[:, :, -1, :]
        whole_top = lax.all_gather(top_row, "lon", axis=2, tiled=True)
        partner_row = jnp.take(whole_top, fold_partner, axis=2)
        return (east_west, south_north, partner_row)

    kept_states = [tracer_start]
    for repeat in range(STEPS):
        advance_quantity = kept_states[-1]
        uptake = decay_rate * advance_quantity / jnp.sqrt(1.0 + advance_quantity * advance_quantity)
        divergence_east_west, divergence_south_north, divergence_partner_row = neighbours(
            advance_quantity
        )
        east_flux = (
            east_own * divergence_east_west[..., :-1] + east_next * divergence_east_west[..., 1:]
        )
        north_flux = (
            north_own * divergence_south_north[:, :, :-1, :]
            + north_next * divergence_south_north[:, :, 1:, :]
        )
        divergence_top_row = advance_quantity[:, :, -1, :]
        fold_flux = fold_own * divergence_top_row + fold_next * divergence_partner_row
        north_flux = north_flux.at[:, :, -1, :].add(fold_flux)
        up_flux = up_own * advance_quantity[:, :-1] + up_next * advance_quantity[:, 1:]
        zero_level = jnp.zeros_like(advance_quantity[:, :1])
        vertical_part = jnp.concatenate([up_flux, zero_level], 1) - jnp.concatenate(
            [zero_level, up_flux], 1
        )
        kept_states.append(
            ocean
            * (
                advance_quantity
                - (
                    east_flux[..., 1:]
                    - east_flux[..., :-1]
                    + (north_flux[:, :, 1:, :] - north_flux[:, :, :-1, :])
                    + vertical_part
                )
                - uptake
                + source
            )
        )
    last_state = kept_states[-1]
    adjoint = ocean * (last_state - target)
    source_grad = ocean * adjoint
    for backward in range(STEPS - 1, 0, -1):
        current = kept_states[backward]
        weight = ocean * adjoint
        transposed_east_west, transposed_south_north, transposed_partner_row = neighbours(weight)
        east_diff = transposed_east_west[..., :-1] - transposed_east_west[..., 1:]
        north_diff = transposed_south_north[:, :, :-1, :] - transposed_south_north[:, :, 1:, :]
        up_diff = weight[:, :-1] - weight[:, 1:]
        result = east_own[..., 1:] * east_diff[..., 1:] + east_next[..., :-1] * east_diff[..., :-1]
        result = result + (
            north_own[:, 1:, :] * north_diff[:, :, 1:, :]
            + north_next[:, :-1, :] * north_diff[:, :, :-1, :]
        )
        result = result.at[:, :, -1, :].add(
            fold_own * (weight[:, :, -1, :] - transposed_partner_row)
        )
        transposed_zero_level = jnp.zeros_like(weight[:, :1])
        result = result + (
            jnp.concatenate([up_own * up_diff, transposed_zero_level], 1)
            + jnp.concatenate([transposed_zero_level, up_next * up_diff], 1)
        )
        spread = 1.0 + current * current
        adjoint = weight - result - decay_rate / (spread * jnp.sqrt(spread)) * weight
        source_grad = source_grad + ocean * adjoint
    squares = lax.psum(jnp.sum(source_grad * source_grad), ("lon", "lat"))
    return (source_grad, jnp.sqrt(squares))


def solution(mesh):
    return jax.shard_map(
        on_device,
        mesh=mesh,
        in_specs=(
            P(None, None, "lat", "lon"),
            P(None, None, "lat", "lon"),
            P(None, None, "lat", "lon"),
            P(None, "lat", "lon"),
            P(None, "lat", "lon"),
            P(None, "lat", "lon"),
            P(None, "lat", "lon"),
            P(None, "lat", "lon"),
            P(),
            P("lon"),
        ),
        out_specs=(P(None, None, "lat", "lon"), P()),
        check_vma=False,
    )
```

profile of v0, /device:TPU:2, one launch (start us, length us, event | category | flops | bytes accessed | tf_op | source)
XLA Modules:
  0.0 697.5 jit_solution(13284979570440464098)
XLA Ops:
  0.6 1.9 fusion.105
  3.1 3.5 collective-permute-start.6
  6.6 4.5 collective-permute-start.7
  13.9 2.8 collective-permute-start.5
  17.8 6.3 collective-permute-start.1
  27.1 2.2 fusion.104
  30.4 43.1 %all-gather = f32[3,16,1,4096]{3,1,2,0:T(8,128)} all-gather(f32[3,16,1,128]{3,1,2,0:T(8,128)S(1)} %get-tuple-element.158), channel_id=2, replica_groups=mesh['lon'=32,'lat'=8] {'lon'}, dimensions={3}, use_global_device_ids=true | all-gather | bytes 811008 | tf_op jit(solution)/shard_map/all_gather | solution.py:74
  73.5 38.9 %all_gather.24 = f32[3,16,4096]{2,1,0:T(8,128)S(1)} all-gather(f32[3,16,128]{2,1,0:T(8,128)S(1)} %pad_maximum_fusion.12), channel_id=1, replica_groups=mesh['lon'=32,'lat'=8] {'lon'}, dimensions={2}, use_global_device_ids=true | all-gather | bytes 811008 | tf_op jit(solution)/shard_map/all_gather | solution.py:60
  112.3 5.8 copy.549
  118.2 4.2 gather_fusion
  124.5 6.9 copy.552
  131.4 4.1 gather_fusion.1
  136.6 5.0 collective-permute-start.3
  141.6 1.4 add_bitcast_fusion
  143.1 4.2 collective-permute-done.2
  147.3 2.8 collective-permute-start.4
  150.6 4.8 collective-permute-done.4
  157.6 2.5 multiply_add_fusion.2
  161.2 1.9 collective-permute-start.10
  163.1 6.0 collective-permute-start.11
  169.3 5.3 collective-permute-start.9
  175.4 44.4 %all-gather.1 = f32[3,16,1,4096]{3,1,2,0:T(8,128)} all-gather(f32[3,16,1,128]{3,1,2,0:T(8,128)S(1)} %get-tuple-element.153), channel_id=3, replica_groups=mesh['lon'=32,'lat'=8] {'lon'}, dimensions={3}, use_global_device_ids=true | all-gather | bytes 811008 | tf_op jit(solution)/shard_map/all_gather | solution.py:74
  219.8 6.8 copy.567
  226.6 4.3 gather_fusion.2
  233.4 2.9 fusion.11
  236.3 1.8 fusion.31
  239.2 1.9 collective-permute-start.14
  241.1 6.0 collective-permute-start.15
  247.2 5.3 collective-permute-start.13
  252.6 45.2 %all-gather.2 = f32[3,16,1,4096]{3,1,2,0:T(8,128)} all-gather(f32[3,16,1,128]{3,1,2,0:T(8,128)S(1)} %get-tuple-element.148), channel_id=4, replica_groups=mesh['lon'=32,'lat'=8] {'lon'}, dimensions={3}, use_global_device_ids=true | all-gather | bytes 811008 | tf_op jit(solution)/shard_map/all_gather | solution.py:74
  297.8 6.8 copy.585
  304.6 4.9 gather_fusion.3
  313.4 2.6 fusion.17
  318.9 1.9 collective-permute-start.18
  320.8 6.0 collective-permute-start.19
  326.9 5.3 collective-permute-start.17
  332.3 45.2 %all-gather.3 = f32[3,16,1,4096]{3,1,2,0:T(8,128)} all-gather(f32[3,16,1,128]{3,1,2,0:T(8,128)S(1)} %get-tuple-element.143), channel_id=5, replica_groups=mesh['lon'=32,'lat'=8] {'lon'}, dimensions={3}, use_global_device_ids=true | all-gather | bytes 811008 | tf_op jit(solution)/shard_map/all_gather | solution.py:74
  377.5 6.8 copy.597
  384.3 4.9 gather_fusion.4
  394.2 1.6 fusion.16
  398.1 2.0 collective-permute-start.22
  400.1 6.0 collective-permute-start.23
  406.5 5.3 collective-permute-start.21
  411.8 45.0 %all-gather.4 = f32[3,16,1,4096]{3,1,2,0:T(8,128)} all-gather(f32[3,16,1,128]{3,1,2,0:T(8,128)S(1)} %get-tuple-element.137), channel_id=6, replica_groups=mesh['lon'=32,'lat'=8] {'lon'}, dimensions={3}, use_global_device_ids=true | all-gather | bytes 811008 | tf_op jit(solution)/shard_map/all_gather | solution.py:74
  456.8 6.9 copy.618
  463.7 4.9 gather_fusion.5
  472.7 1.4 fusion.58
  475.4 1.9 collective-permute-start.26
  477.3 6.0 collective-permute-start.27
  483.4 5.3 collective-permute-start.25
  488.8 45.0 %all-gather.5 = f32[3,16,1,4096]{3,1,2,0:T(8,128)} all-gather(f32[3,16,1,128]{3,1,2,0:T(8,128)S(1)} %get-tuple-element.130), channel_id=7, replica_groups=mesh['lon'=32,'lat'=8] {'lon'}, dimensions={3}, use_global_device_ids=true | all-gather | bytes 811008 | tf_op jit(solution)/shard_map/all_gather | solution.py:74
  533.7 6.8 copy.631
  540.6 4.9 gather_fusion.6
  546.6 1.4 maximum_subtract_fusion.1
  548.3 1.5 fusion.55
  551.9 1.9 collective-permute-start.30
  553.8 6.0 collective-permute-start.31
  559.9 5.3 collective-permute-start.29
  565.2 42.5 %all-gather.6 = f32[3,16,1,4096]{3,1,2,0:T(8,128)S(1)} all-gather(f32[3,16,1,128]{3,1,2,0:T(8,128)S(1)} %get-tuple-element.120), channel_id=8, replica_groups=mesh['lon'=32,'lat'=8] {'lon'}, dimensions={3}, use_global_device_ids=true | all-gather | bytes 811008 | tf_op jit(solution)/shard_map/all_gather | solution.py:74
  607.8 5.8 copy.645
  613.6 4.3 gather_fusion.7
  618.0 1.4 maximum_subtract_fusion.2
  619.7 3.0 multiply_reduce_fusion
  622.8 72.8 %psum.7 = f32[]{:T(128)} all-reduce(f32[]{:T(128)} %get-tuple-element.93), channel_id=1, replica_groups=mesh['lon'=32,'lat'=8] {'lon','lat'}, use_global_device_ids=true, to_apply=%region_1.3 | all-reduce | flops 1 | bytes 8 | tf_op jit(solution)/shard_map/psum | solution.py:140
  (171 shorter events, 43.5 us)
Async XLA Ops:
  3.1 153.5 %collective-permute-start.6 = (f32[3,16,1,128]{3,1,0,2:T(8,128)}, f32[3,16,1,128]{3,1,0,2:T(8,128)}, u32[]{:S(2)}, u32[]{:S(2)}) collective-permute-start(f32[3,16,1,128]{3,1,0,2:T(8,128)} %get-tuple-element.160), channel_id=1, source_target_pairs={{0,1},{1,2},{2,3},{3,4},{4,5},{5,6},{6,7},{8,9},{9,10},{10,11},{11... | collective-permute-start | bytes 73736 | tf_op jit(solution)/shard_map/ppermute | solution.py:16
  6.6 150.0 %collective-permute-start.7 = (f32[3,16,1,128]{3,1,0,2:T(8,128)}, f32[3,16,1,128]{3,1,0,2:T(8,128)}, u32[]{:S(2)}, u32[]{:S(2)}) collective-permute-start(f32[3,16,1,128]{3,1,0,2:T(8,128)} %get-tuple-element.159), channel_id=1, source_target_pairs={{1,0},{2,1},{3,2},{4,3},{5,4},{6,5},{7,6},{9,8},{10,9},{11,10},{12... | collective-permute-start | bytes 73736 | tf_op jit(solution)/shard_map/ppermute | solution.py:19
  12.0 110.4 %copy-start = (f32[3,16,16,128]{3,2,1,0:T(8,128)S(1)}, f32[3,16,16,128]{3,2,1,0:T(8,128)}, u32[]{:S(2)}) copy-start(f32[3,16,16,128]{3,2,1,0:T(8,128)} %param.26) | copy-start | bytes 1179652
  13.9 136.7 %collective-permute-start.5 = (f32[4,16,1,128]{3,2,1,0:T(1,128)}, f32[4,16,1,128]{3,2,1,0:T(1,128)}, u32[]{:S(2)}, u32[]{:S(2)}) collective-permute-start(f32[4,16,1,128]{3,2,1,0:T(1,128)} %get-tuple-element.119), channel_id=1, source_target_pairs={{1,0},{2,1},{3,2},{4,3},{5,4},{6,5},{7,6},{9,8},{10,9},{11,10},{12... | collective-permute-start | bytes 98312 | tf_op jit(solution)/shard_map/ppermute | solution.py:19
  17.8 118.5 %collective-permute-start.1 = (f32[4,16,16,1]{3,2,1,0:T(8,128)}, f32[4,16,16,1]{3,2,1,0:T(8,128)}, u32[]{:S(2)}, u32[]{:S(2)}) collective-permute-start(f32[4,16,16,1]{3,2,1,0:T(8,128)} %get-tuple-element.117), channel_id=1, source_target_pairs={{8,0},{16,8},{24,16},{32,24},{40,32},{48,40},{56,48},{64,56},{72,6... | collective-permute-start | bytes 12296 | tf_op jit(solution)/shard_map/ppermute | solution.py:19
  24.1 112.5 %collective-permute-start = (f32[4,16,16,1]{3,2,1,0:T(8,128)}, f32[4,16,16,1]{3,2,1,0:T(8,128)}, u32[]{:S(2)}, u32[]{:S(2)}) collective-permute-start(f32[4,16,16,1]{3,2,1,0:T(8,128)} %get-tuple-element.116), channel_id=1, source_target_pairs={{0,8},{8,16},{16,24},{24,32},{32,40},{40,48},{48,56},{56,64},{64,7... | collective-permute-start | bytes 12296 | tf_op jit(solution)/shard_map/ppermute | solution.py:16
  27.1 97.3 %copy-start.12 = (pred[128]{0:T(512)(128)(4,1)}, pred[128]{0:T(512)(128)(4,1)S(1)}, u32[]{:S(2)}) copy-start(pred[128]{0:T(512)(128)(4,1)S(1)} %compare_and_fusion) | copy-start | bytes 388
  73.5 57.9 %copy-start.16 = (s32[1024]{0:T(1024)}, s32[1024]{0:T(1024)S(1)}, u32[]{:S(2)}) copy-start(s32[1024]{0:T(1024)S(1)} %pad_clamp_fusion) | copy-start | bytes 12292
  118.2 23.4 %copy-start.4 = (f32[16,16,128]{2,1,0:T(8,128)S(1)}, f32[16,16,128]{2,1,0:T(8,128)}, u32[]{:S(2)}) copy-start(f32[16,16,128]{2,1,0:T(8,128)} %param.32) | copy-start | bytes 393220
  118.2 23.4 %copy-start.6 = (f32[16,16,128]{2,1,0:T(8,128)S(1)}, f32[16,16,128]{2,1,0:T(8,128)}, u32[]{:S(2)}) copy-start(f32[16,16,128]{2,1,0:T(8,128)} %param.30) | copy-start | bytes 393220
  118.2 23.4 %copy-start.7 = (f32[16,16,128]{2,1,0:T(8,128)S(1)}, f32[16,16,128]{2,1,0:T(8,128)}, u32[]{:S(2)}) copy-start(f32[16,16,128]{2,1,0:T(8,128)} %param.29) | copy-start | bytes 393220
  124.3 50.3 %copy-start.2 = (f32[15,16,128]{2,0,1:T(8,128)}, f32[15,16,128]{2,0,1:T(8,128)S(1)}, u32[]{:S(2)}) copy-start(f32[15,16,128]{2,0,1:T(8,128)S(1)} %copy.662) | copy-start | bytes 368644
  124.4 50.2 %copy-start.3 = (f32[15,16,128]{2,0,1:T(8,128)}, f32[15,16,128]{2,0,1:T(8,128)S(1)}, u32[]{:S(2)}) copy-start(f32[15,16,128]{2,0,1:T(8,128)S(1)} %copy.661) | copy-start | bytes 368644
  124.5 33.1 %copy-start.1 = (f32[3,16,16,128]{3,2,1,0:T(8,128)S(1)}, f32[3,16,16,128]{3,2,1,0:T(8,128)}, u32[]{:S(2)}) copy-start(f32[3,16,16,128]{3,2,1,0:T(8,128)} %param.27) | copy-start | bytes 1179652
  136.2 21.3 %copy-start.9 = (f32[128,3,16]{0,2,1:T(8,128)S(1)}, f32[128,3,16]{0,2,1:T(8,128)}, u32[]{:S(2)}) copy-start(f32[128,3,16]{0,2,1:T(8,128)} %copy.553) | copy-start | bytes 73732
  136.2 21.3 %copy-start.13 = (pred[128]{0:T(512)(128)(4,1)S(1)}, pred[128]{0:T(512)(128)(4,1)}, u32[]{:S(2)}) copy-start(pred[128]{0:T(512)(128)(4,1)} %copy-done.12) | copy-start | bytes 388
  136.2 11.0 %collective-permute-start.2 = (f32[3,16,16,1]{3,2,1,0:T(8,128)}, f32[3,16,16,1]{3,2,1,0:T(8,128)S(1)}, u32[]{:S(2)}, u32[]{:S(2)}) collective-permute-start(f32[3,16,16,1]{3,2,1,0:T(8,128)} %get-tuple-element.157), channel_id=1, source_target_pairs={{0,8},{8,16},{16,24},{24,32},{32,40},{40,48},{48,56},{56,64},{64,7... | collective-permute-start | bytes 9224 | tf_op jit(solution)/shard_map/ppermute | solution.py:16
  136.6 13.4 %collective-permute-start.3 = (f32[3,16,16,1]{3,2,1,0:T(8,128)}, f32[3,16,16,1]{3,2,1,0:T(8,128)S(1)}, u32[]{:S(2)}, u32[]{:S(2)}) collective-permute-start(f32[3,16,16,1]{3,2,1,0:T(8,128)} %get-tuple-element.156), channel_id=1, source_target_pairs={{8,0},{16,8},{24,16},{32,24},{40,32},{48,40},{56,48},{64,56},{72,6... | collective-permute-start | bytes 9224 | tf_op jit(solution)/shard_map/ppermute | solution.py:19
  147.3 8.1 %collective-permute-start.4 = (f32[4,16,1,128]{3,2,1,0:T(1,128)}, f32[4,16,1,128]{3,2,1,0:T(1,128)S(1)}, u32[]{:S(2)}, u32[]{:S(2)}) collective-permute-start(f32[4,16,1,128]{3,2,1,0:T(1,128)} %get-tuple-element.118), channel_id=1, source_target_pairs={{0,1},{1,2},{2,3},{3,4},{4,5},{5,6},{6,7},{8,9},{9,10},{10,11},{11... | collective-permute-start | bytes 98312 | tf_op jit(solution)/shard_map/ppermute | solution.py:16
  161.2 72.1 %collective-permute-start.10 = (f32[3,16,1,128]{3,1,0,2:T(8,128)S(1)}, f32[3,16,1,128]{3,1,0,2:T(8,128)S(1)}, u32[]{:S(2)}, u32[]{:S(2)}) collective-permute-start(f32[3,16,1,128]{3,1,0,2:T(8,128)S(1)} %get-tuple-element.155), channel_id=1, source_target_pairs={{0,1},{1,2},{2,3},{3,4},{4,5},{5,6},{6,7},{8,9},{9,10},{10,11},{11... | collective-permute-start | bytes 73736 | tf_op jit(solution)/shard_map/ppermute | solution.py:16
  163.1 70.2 %collective-permute-start.11 = (f32[3,16,1,128]{3,1,0,2:T(8,128)S(1)}, f32[3,16,1,128]{3,1,0,2:T(8,128)S(1)}, u32[]{:S(2)}, u32[]{:S(2)}) collective-permute-start(f32[3,16,1,128]{3,1,0,2:T(8,128)S(1)} %get-tuple-element.154), channel_id=1, source_target_pairs={{1,0},{2,1},{3,2},{4,3},{5,4},{6,5},{7,6},{9,8},{10,9},{11,10},{12... | collective-permute-start | bytes 73736 | tf_op jit(solution)/shard_map/ppermute | solution.py:19
  169.2 62.5 %collective-permute-start.8 = (f32[3,16,16,1]{3,2,1,0:T(8,128)}, f32[3,16,16,1]{3,2,1,0:T(8,128)}, u32[]{:S(2)}, u32[]{:S(2)}) collective-permute-start(f32[3,16,16,1]{3,2,1,0:T(8,128)} %get-tuple-element.152), channel_id=1, source_target_pairs={{0,8},{8,16},{16,24},{24,32},{32,40},{40,48},{48,56},{56,64},{64,7... | collective-permute-start | bytes 9224 | tf_op jit(solution)/shard_map/ppermute | solution.py:16
  169.3 64.1 %copy-start.14 = (pred[128]{0:T(512)(128)(4,1)S(1)}, pred[128]{0:T(512)(128)(4,1)}, u32[]{:S(2)}) copy-start(pred[128]{0:T(512)(128)(4,1)} %copy-done.12) | copy-start | bytes 388
  169.3 64.1 %copy-start.10 = (f32[3,16]{1,0:T(4,128)S(1)}, f32[3,16]{1,0:T(4,128)}, u32[]{:S(2)}) copy-start(f32[3,16]{1,0:T(4,128)} %param.34) | copy-start | bytes 580
  169.3 62.4 %collective-permute-start.9 = (f32[3,16,16,1]{3,2,1,0:T(8,128)}, f32[3,16,16,1]{3,2,1,0:T(8,128)}, u32[]{:S(2)}, u32[]{:S(2)}) collective-permute-start(f32[3,16,16,1]{3,2,1,0:T(8,128)} %get-tuple-element.151), channel_id=1, source_target_pairs={{8,0},{16,8},{24,16},{32,24},{40,32},{48,40},{56,48},{64,56},{72,6... | collective-permute-start | bytes 9224 | tf_op jit(solution)/shard_map/ppermute | solution.py:19
  239.2 74.1 %collective-permute-start.14 = (f32[3,16,1,128]{3,1,0,2:T(8,128)S(1)}, f32[3,16,1,128]{3,1,0,2:T(8,128)S(1)}, u32[]{:S(2)}, u32[]{:S(2)}) collective-permute-start(f32[3,16,1,128]{3,1,0,2:T(8,128)S(1)} %get-tuple-element.150), channel_id=1, source_target_pairs={{0,1},{1,2},{2,3},{3,4},{4,5},{5,6},{6,7},{8,9},{9,10},{10,11},{11... | collective-permute-start | bytes 73736 | tf_op jit(solution)/shard_map/ppermute | solution.py:16
  241.1 72.2 %collective-permute-start.15 = (f32[3,16,1,128]{3,1,0,2:T(8,128)S(1)}, f32[3,16,1,128]{3,1,0,2:T(8,128)S(1)}, u32[]{:S(2)}, u32[]{:S(2)}) collective-permute-start(f32[3,16,1,128]{3,1,0,2:T(8,128)S(1)} %get-tuple-element.149), channel_id=1, source_target_pairs={{1,0},{2,1},{3,2},{4,3},{5,4},{6,5},{7,6},{9,8},{10,9},{11,10},{12... | collective-permute-start | bytes 73736 | tf_op jit(solution)/shard_map/ppermute | solution.py:19
  247.1 63.4 %collective-permute-start.12 = (f32[3,16,16,1]{3,1,0,2:T(8,128)}, f32[3,16,16,1]{3,1,0,2:T(8,128)}, u32[]{:S(2)}, u32[]{:S(2)}) collective-permute-start(f32[3,16,16,1]{3,1,0,2:T(8,128)} %get-tuple-element.147), channel_id=1, source_target_pairs={{0,8},{8,16},{16,24},{24,32},{32,40},{40,48},{48,56},{56,64},{64,7... | collective-permute-start | bytes 9224 | tf_op jit(solution)/shard_map/ppermute | solution.py:16
  247.2 64.5 %collective-permute-start.13 = (f32[3,16,16,1]{3,1,0,2:T(8,128)}, f32[3,16,16,1]{3,1,0,2:T(8,128)}, u32[]{:S(2)}, u32[]{:S(2)}) collective-permute-start(f32[3,16,16,1]{3,1,0,2:T(8,128)} %get-tuple-element.146), channel_id=1, source_target_pairs={{8,0},{16,8},{24,16},{32,24},{40,32},{48,40},{56,48},{64,56},{72,6... | collective-permute-start | bytes 9224 | tf_op jit(solution)/shard_map/ppermute | solution.py:19
  318.9 75.3 %collective-permute-start.18 = (f32[3,16,1,128]{3,1,0,2:T(8,128)S(1)}, f32[3,16,1,128]{3,1,0,2:T(8,128)S(1)}, u32[]{:S(2)}, u32[]{:S(2)}) collective-permute-start(f32[3,16,1,128]{3,1,0,2:T(8,128)S(1)} %get-tuple-element.145), channel_id=1, source_target_pairs={{0,1},{1,2},{2,3},{3,4},{4,5},{5,6},{6,7},{8,9},{9,10},{10,11},{11... | collective-permute-start | bytes 73736 | tf_op jit(solution)/shard_map/ppermute | solution.py:16
  320.8 73.3 %collective-permute-start.19 = (f32[3,16,1,128]{3,1,0,2:T(8,128)S(1)}, f32[3,16,1,128]{3,1,0,2:T(8,128)S(1)}, u32[]{:S(2)}, u32[]{:S(2)}) collective-permute-start(f32[3,16,1,128]{3,1,0,2:T(8,128)S(1)} %get-tuple-element.144), channel_id=1, source_target_pairs={{1,0},{2,1},{3,2},{4,3},{5,4},{6,5},{7,6},{9,8},{10,9},{11,10},{12... | collective-permute-start | bytes 73736 | tf_op jit(solution)/shard_map/ppermute | solution.py:19
  326.9 63.4 %collective-permute-start.16 = (f32[3,16,16,1]{3,1,0,2:T(8,128)}, f32[3,16,16,1]{3,1,0,2:T(8,128)}, u32[]{:S(2)}, u32[]{:S(2)}) collective-permute-start(f32[3,16,16,1]{3,1,0,2:T(8,128)} %get-tuple-element.142), channel_id=1, source_target_pairs={{0,8},{8,16},{16,24},{24,32},{32,40},{40,48},{48,56},{56,64},{64,7... | collective-permute-start | bytes 9224 | tf_op jit(solution)/shard_map/ppermute | solution.py:16
  326.9 64.5 %collective-permute-start.17 = (f32[3,16,16,1]{3,1,0,2:T(8,128)}, f32[3,16,16,1]{3,1,0,2:T(8,128)}, u32[]{:S(2)}, u32[]{:S(2)}) collective-permute-start(f32[3,16,16,1]{3,1,0,2:T(8,128)} %get-tuple-element.141), channel_id=1, source_target_pairs={{8,0},{16,8},{24,16},{32,24},{40,32},{48,40},{56,48},{64,56},{72,6... | collective-permute-start | bytes 9224 | tf_op jit(solution)/shard_map/ppermute | solution.py:19
  398.1 74.2 %copy-start.8 = (f32[16,16,128]{2,1,0:T(8,128)S(1)}, f32[16,16,128]{2,1,0:T(8,128)}, u32[]{:S(2)}) copy-start(f32[16,16,128]{2,1,0:T(8,128)} %copy.663) | copy-start | bytes 393220
  398.1 73.2 %collective-permute-start.22 = (f32[3,16,1,128]{3,1,0,2:T(8,128)S(1)}, f32[3,16,1,128]{3,1,0,2:T(8,128)S(1)}, u32[]{:S(2)}, u32[]{:S(2)}) collective-permute-start(f32[3,16,1,128]{3,1,0,2:T(8,128)S(1)} %get-tuple-element.138), channel_id=1, source_target_pairs={{0,1},{1,2},{2,3},{3,4},{4,5},{5,6},{6,7},{8,9},{9,10},{10,11},{11... | collective-permute-start | bytes 73736 | tf_op jit(solution)/shard_map/ppermute | solution.py:16
  400.1 71.2 %collective-permute-start.23 = (f32[3,16,1,128]{3,2,1,0:T(1,128)S(1)}, f32[3,16,1,128]{3,2,1,0:T(1,128)}, u32[]{:S(2)}, u32[]{:S(2)}) collective-permute-start(f32[3,16,1,128]{3,2,1,0:T(1,128)S(1)} %slice.756), channel_id=1, source_target_pairs={{1,0},{2,1},{3,2},{4,3},{5,4},{6,5},{7,6},{9,8},{10,9},{11,10},{12... | collective-permute-start | bytes 73736 | tf_op jit(solution)/shard_map/ppermute | solution.py:19
  406.1 63.5 %collective-permute-start.20 = (f32[3,16,16,1]{3,1,0,2:T(8,128)}, f32[3,16,16,1]{3,1,0,2:T(8,128)}, u32[]{:S(2)}, u32[]{:S(2)}) collective-permute-start(f32[3,16,16,1]{3,1,0,2:T(8,128)} %get-tuple-element.140), channel_id=1, source_target_pairs={{0,8},{8,16},{16,24},{24,32},{32,40},{40,48},{48,56},{56,64},{64,7... | collective-permute-start | bytes 9224 | tf_op jit(solution)/shard_map/ppermute | solution.py:16
  406.5 63.2 %collective-permute-start.21 = (f32[3,16,16,1]{3,1,0,2:T(8,128)S(1)}, f32[3,16,16,1]{3,1,0,2:T(8,128)}, u32[]{:S(2)}, u32[]{:S(2)}) collective-permute-start(f32[3,16,16,1]{3,1,0,2:T(8,128)S(1)} %get-tuple-element.139), channel_id=1, source_target_pairs={{8,0},{16,8},{24,16},{32,24},{40,32},{48,40},{56,48},{64,56},{72,6... | collective-permute-start | bytes 9224 | tf_op jit(solution)/shard_map/ppermute | solution.py:19
  456.8 15.9 %copy-start.5 = (f32[3,16,16,128]{3,1,0,2:T(8,128)S(1)}, f32[3,16,16,128]{3,1,0,2:T(8,128)}, u32[]{:S(2)}) copy-start(f32[3,16,16,128]{3,1,0,2:T(8,128)} %get-tuple-element.97) | copy-start | bytes 1179652
  475.4 72.6 %collective-permute-start.26 = (f32[3,16,1,128]{3,1,0,2:T(8,128)S(1)}, f32[3,16,1,128]{3,1,0,2:T(8,128)S(1)}, u32[]{:S(2)}, u32[]{:S(2)}) collective-permute-start(f32[3,16,1,128]{3,1,0,2:T(8,128)S(1)} %get-tuple-element.131), channel_id=1, source_target_pairs={{0,1},{1,2},{2,3},{3,4},{4,5},{5,6},{6,7},{8,9},{9,10},{10,11},{11... | collective-permute-start | bytes 73736 | tf_op jit(solution)/shard_map/ppermute | solution.py:16
  477.3 70.7 %collective-permute-start.27 = (f32[3,16,1,128]{3,1,0,2:T(8,128)S(1)}, f32[3,16,1,128]{3,1,0,2:T(8,128)S(1)}, u32[]{:S(2)}, u32[]{:S(2)}) collective-permute-start(f32[3,16,1,128]{3,1,0,2:T(8,128)S(1)} %get-tuple-element.132), channel_id=1, source_target_pairs={{1,0},{2,1},{3,2},{4,3},{5,4},{6,5},{7,6},{9,8},{10,9},{11,10},{12... | collective-permute-start | bytes 73736 | tf_op jit(solution)/shard_map/ppermute | solution.py:19
  483.3 63.2 %collective-permute-start.24 = (f32[3,16,16,1]{3,1,0,2:T(8,128)S(1)}, f32[3,16,16,1]{3,1,0,2:T(8,128)}, u32[]{:S(2)}, u32[]{:S(2)}) collective-permute-start(f32[3,16,16,1]{3,1,0,2:T(8,128)S(1)} %get-tuple-element.134), channel_id=1, source_target_pairs={{0,8},{8,16},{16,24},{24,32},{32,40},{40,48},{48,56},{56,64},{64,7... | collective-permute-start | bytes 9224 | tf_op jit(solution)/shard_map/ppermute | solution.py:16
  483.4 63.1 %collective-permute-start.25 = (f32[3,16,16,1]{3,1,0,2:T(8,128)S(1)}, f32[3,16,16,1]{3,1,0,2:T(8,128)}, u32[]{:S(2)}, u32[]{:S(2)}) collective-permute-start(f32[3,16,16,1]{3,1,0,2:T(8,128)S(1)} %get-tuple-element.133), channel_id=1, source_target_pairs={{8,0},{16,8},{24,16},{32,24},{40,32},{48,40},{56,48},{64,56},{72,6... | collective-permute-start | bytes 9224 | tf_op jit(solution)/shard_map/ppermute | solution.py:19
  550.8 68.9 %copy-start.15 = (pred[128]{0:T(512)(128)(4,1)S(1)}, pred[128]{0:T(512)(128)(4,1)}, u32[]{:S(2)}) copy-start(pred[128]{0:T(512)(128)(4,1)} %copy-done.12) | copy-start | bytes 388
  550.9 68.9 %copy-start.11 = (f32[3,16]{1,0:T(4,128)S(1)}, f32[3,16]{1,0:T(4,128)}, u32[]{:S(2)}) copy-start(f32[3,16]{1,0:T(4,128)} %param.34) | copy-start | bytes 580
  551.9 67.5 %collective-permute-start.30 = (f32[3,16,1,128]{3,1,0,2:T(8,128)S(1)}, f32[3,16,1,128]{3,1,0,2:T(8,128)S(1)}, u32[]{:S(2)}, u32[]{:S(2)}) collective-permute-start(f32[3,16,1,128]{3,1,0,2:T(8,128)S(1)} %get-tuple-element.121), channel_id=1, source_target_pairs={{0,1},{1,2},{2,3},{3,4},{4,5},{5,6},{6,7},{8,9},{9,10},{10,11},{11... | collective-permute-start | bytes 73736 | tf_op jit(solution)/shard_map/ppermute | solution.py:16
  553.8 65.6 %collective-permute-start.31 = (f32[3,16,1,128]{3,1,0,2:T(8,128)S(1)}, f32[3,16,1,128]{3,1,0,2:T(8,128)S(1)}, u32[]{:S(2)}, u32[]{:S(2)}) collective-permute-start(f32[3,16,1,128]{3,1,0,2:T(8,128)S(1)} %get-tuple-element.122), channel_id=1, source_target_pairs={{1,0},{2,1},{3,2},{4,3},{5,4},{6,5},{7,6},{9,8},{10,9},{11,10},{12... | collective-permute-start | bytes 73736 | tf_op jit(solution)/shard_map/ppermute | solution.py:19
  559.8 58.2 %collective-permute-start.28 = (f32[3,16,16,1]{3,1,0,2:T(8,128)}, f32[3,16,16,1]{3,1,0,2:T(8,128)}, u32[]{:S(2)}, u32[]{:S(2)}) collective-permute-start(f32[3,16,16,1]{3,1,0,2:T(8,128)} %get-tuple-element.124), channel_id=1, source_target_pairs={{0,8},{8,16},{16,24},{24,32},{32,40},{40,48},{48,56},{56,64},{64,7... | collective-permute-start | bytes 9224 | tf_op jit(solution)/shard_map/ppermute | solution.py:16
  559.9 58.1 %collective-permute-start.29 = (f32[3,16,16,1]{3,1,0,2:T(8,128)}, f32[3,16,16,1]{3,1,0,2:T(8,128)}, u32[]{:S(2)}, u32[]{:S(2)}) collective-permute-start(f32[3,16,16,1]{3,1,0,2:T(8,128)} %get-tuple-element.123), channel_id=1, source_target_pairs={{8,0},{16,8},{24,16},{32,24},{40,32},{48,40},{56,48},{64,56},{72,6... | collective-permute-start | bytes 9224 | tf_op jit(solution)/shard_map/ppermute | solution.py:19
where the time goes:
time: 701 us; the launch traced here: 697 us
  blocking collectives  422 us (60%)
  local copies, waits for them, and re-layouts  115 us (16%)
  starting transfers between devices  106 us (15%)
  other arithmetic  42.6 us (6%)
  waiting for transfers between devices  9.06 us (1%)
    all_gather x7, blocking collectives, neighbours(): whole_top = lax.all_gather(top_row, 'lon', axis=2, tiled=True)  310 us
    ppermute x16, starting transfers between devices, with_halo(): lax.ppermute(lax.slice_in_dim(block, 0, width, axis=dim), axis, backward)  86.8 us
    psum x1, blocking collectives, on_device(): squares = lax.psum(jnp.sum(source_grad * source_grad), ('lon', 'lat'))  72.8 us
    all_gather x7, local copies, waits for them, and re-layouts, neighbours(): whole_top = lax.all_gather(top_row, 'lon', axis=2, tiled=True)  46.9 us
    all_gather x1, blocking collectives, on_device(): fold_all = lax.all_gather(top_static, 'lon', axis=2, tiled=True)  38.9 us
    gather x14, local copies, waits for them, and re-layouts, neighbours(): partner_row = jnp.take(whole_top, fold_partner, axis=2)  37.4 us
    ppermute x16, starting transfers between devices, with_halo(): lax.ppermute(lax.slice_in_dim(block, block.shape[dim] - width, None, axis...  18.9 us
  transfers between devices with their start and end apart: 32, of which 2 were waited for; matrix products, arithmetic and copies ran while one was open for 18% of the time, Pallas kernels for 0%

commit v1 on v0

--- a/solution.py
+++ b/solution.py
@@ -19,6 +19,37 @@
         high = lax.ppermute(lax.slice_in_dim(block, 0, width, axis=dim), axis, backward)
         block = jnp.concatenate([low, block, high], axis=dim)
     return block
+
+
+def fold_row(row, fold_partner):
+    count = lax.axis_size("lon")
+    width = row.shape[-1]
+    here = lax.axis_index("lon")
+    whole = width * count
+    offset = (fold_partner[0] + width * here) % whole
+    turns = offset // width
+    shift = offset % width
+    flipped = row[..., ::-1]
+    first = lax.ppermute(flipped, "lon", [((-d) % count, d) for d in range(count)])
+    second = lax.ppermute(flipped, "lon", [((-d - 1) % count, d) for d in range(count)])
+    pair = jnp.concatenate([first, second], axis=-1)
+    step = 1
+    while step < count:
+        moved = lax.ppermute(pair, "lon", [(d, (d + step) % count) for d in range(count)])
+        pair = jnp.where((turns // step) % 2 == 1, moved, pair)
+        step *= 2
+    return lax.dynamic_slice_in_dim(pair, width - 1 - shift, width, axis=pair.ndim - 1)
+
+
+def tree_sum(value, axis):
+    count = lax.axis_size(axis)
+    if count & (count - 1):
+        return lax.psum(value, axis)
+    step = 1
+    while step < count:
+        value = value + lax.ppermute(value, axis, [(d, d ^ step) for d in range(count)])
+        step *= 2
+    return value
 
 
 def upwind_pair(velocity, mixing, face_sea):
@@ -57,8 +88,7 @@
         vertical_vel[:-1], 0.5 * (diffusivity[:-1] + diffusivity[1:]), ocean[:-1] * ocean[1:]
     )
     top_static = jnp.stack([north_vel[:, -1, :], diffusivity[:, -1, :], ocean[:, -1, :]])
-    fold_all = lax.all_gather(top_static, "lon", axis=2, tiled=True)
-    across = jnp.take(fold_all, fold_partner, axis=2)
+    across = fold_row(top_static, fold_partner)
     north_top = (lax.axis_index("lat") == lax.axis_size("lat") - 1).astype(jnp.float32)
     fold_own, fold_next = upwind_pair(
         0.5 * (top_static[0] - across[0]),
@@ -71,8 +101,7 @@
         east_west = with_halo(quantity, (("lon", 3),), 1, True)
         south_north = with_halo(quantity, (("lat", 2),), 1, False)
         top_row = quantity[:, :, -1, :]
-        whole_top = lax.all_gather(top_row, "lon", axis=2, tiled=True)
-        partner_row = jnp.take(whole_top, fold_partner, axis=2)
+        partner_row = fold_row(top_row, fold_partner)
         return (east_west, south_north, partner_row)
 
     kept_states = [tracer_start]
@@ -137,7 +166,7 @@
         spread = 1.0 + current * current
         adjoint = weight - result - decay_rate / (spread * jnp.sqrt(spread)) * weight
         source_grad = source_grad + ocean * adjoint
-    squares = lax.psum(jnp.sum(source_grad * source_grad), ("lon", "lat"))
+    squares = tree_sum(tree_sum(jnp.sum(source_grad * source_grad), "lon"), "lat")
     return (source_grad, jnp.sqrt(squares))
 
 

time: 701 us -> 488 us (0.70)
  blocking collectives: 422 us -> 0 us
  waiting for transfers between devices: 9.06 us -> 273 us
  local copies, waits for them, and re-layouts: 115 us -> 15.1 us
  starting transfers between devices: 106 us -> 166 us
  other arithmetic: 42.6 us -> 15.5 us
    all_gather x8 -> x0, blocking collectives: 349 us -> none  [the longest x7 310 us: neighbours(): whole_top = lax.all_gather(top_row, 'lon', axis=2, tiled=True)]
    ppermute x0 -> x64, waiting for transfers between devices: none -> 219 us  [the longest x40 167 us: fold_row(): lax.ppermute(pair, 'lon', [(d, (d + step) % count) for d in range(count)])]
    psum x1 -> x0, blocking collectives: 72.8 us -> none  [on_device(): squares = lax.psum(jnp.sum(source_grad * source_grad), ('lon', 'lat'))]
    ppermute x0 -> x64, starting transfers between devices: none -> 64 us  [the longest x40 26.8 us: fold_row(): lax.ppermute(pair, 'lon', [(d, (d + step) % count) for d in range(count)])]
    all_gather x8 -> x0, local copies, waits for them, and re-layouts: 52.8 us -> none  [the longest x7 46.9 us: neighbours(): whole_top = lax.all_gather(top_row, 'lon', axis=2, tiled=True)]
    gather x16 -> x0, local copies, waits for them, and re-layouts: 41.7 us -> none  [the longest x14 37.4 us: neighbours(): partner_row = jnp.take(whole_top, fold_partner, axis=2)]
    ppermute x16, waiting for transfers between devices: 9.02 us -> 49.5 us  [with_halo(): lax.ppermute(lax.slice_in_dim(block, block.shape[dim] - width, None, axis...]
  transfers between devices with their start and end apart: 32 -> 96, of which waited for: 2 -> 57; matrix products, arithmetic and copies ran while one was open for 18% -> 3% of each run, Pallas kernels for 0% -> 0%
where the time goes in v1:
time: 488 us; the launch traced here: 478 us
  waiting for transfers between devices  273 us (56%)
  starting transfers between devices  166 us (34%)
  other arithmetic  15.5 us (3%)
  local copies, waits for them, and re-layouts  15.1 us (3%)
  between operations  8.69 us (2%)
    ppermute x40, waiting for transfers between devices, fold_row(): lax.ppermute(pair, 'lon', [(d, (d + step) % count) for d in range(count)])  167 us
    ppermute x16, starting transfers between devices, with_halo(): lax.ppermute(lax.slice_in_dim(block, 0, width, axis=dim), axis, backward)  82.5 us
    ppermute x16, waiting for transfers between devices, with_halo(): lax.ppermute(lax.slice_in_dim(block, block.shape[dim] - width, None, axis...  49.5 us
    ppermute x8, waiting for transfers between devices, fold_row(): lax.ppermute(flipped, 'lon', [((-d - 1) % count, d) for d in range(count)])  27.1 us
    ppermute x40, starting transfers between devices, fold_row(): lax.ppermute(pair, 'lon', [(d, (d + step) % count) for d in range(count)])  26.8 us
    ppermute x8, waiting for transfers between devices, tree_sum(): lax.ppermute(value, axis, [(d, d ^ step) for d in range(count)])  24.4 us
    ppermute x16, starting transfers between devices, with_halo(): lax.ppermute(lax.slice_in_dim(block, block.shape[dim] - width, None, axis...  19.4 us
    ppermute x8, starting transfers between devices, fold_row(): lax.ppermute(flipped, 'lon', [((-d - 1) % count, d) for d in range(count)])  18 us
  transfers between devices with their start and end apart: 96, of which 57 were waited for; matrix products, arithmetic and copies ran while one was open for 3% of the time, Pallas kernels for 0%

profile of v1, /device:TPU:2, one launch (start us, length us, event | category | flops | bytes accessed | tf_op | source)
XLA Modules:
  0.0 477.9 jit_solution(250853657726361019)
XLA Ops:
  5.2 6.9 %collective-permute-start.16 = (f32[3,16,128]{2,1,0:T(8,128)}, f32[3,16,128]{2,1,0:T(8,128)}, u32[]{:S(2)}, u32[]{:S(2)}) collective-permute-start(f32[3,16,128]{2,1,0:T(8,128)} %rev.25), channel_id=1, source_target_pairs={{248,0},{240,8},{232,16},{224,24},{216,32},{208,40},{200,48},{192,... | collective-permute-start | bytes 73736 | tf_op jit(solution)/shard_map/ppermute | solution.py:34
  16.8 5.6 %collective-permute-start.1 = (f32[4,16,16,1]{3,1,2,0:T(8,128)}, f32[4,16,16,1]{3,1,2,0:T(8,128)S(1)}, u32[]{:S(2)}, u32[]{:S(2)}) collective-permute-start(f32[4,16,16,1]{3,1,2,0:T(8,128)} %get-tuple-element.104), channel_id=1, source_target_pairs={{8,0},{16,8},{24,16},{32,24},{40,32},{48,40},{56,48},{64,56},{72,6... | collective-permute-start | bytes 12296 | tf_op jit(solution)/shard_map/ppermute | solution.py:19
  25.9 3.7 collective-permute-done.1
  31.3 3.5 collective-permute-done
  35.4 5.3 %collective-permute-done.2 = f32[3,16,16,1]{3,1,0,2:T(8,128)S(1)} collective-permute-done((f32[3,16,16,1]{3,1,0,2:T(8,128)}, f32[3,16,16,1]{3,1,0,2:T(8,128)S(1)}, u32[]{:S(2)}, u32[]{:S(2)}) %collective-permute-start.2) | collective-permute-done | bytes 3104 | tf_op jit(solution)/shard_map/ppermute | solution.py:16
  40.7 3.5 collective-permute-start.6
  45.0 4.5 collective-permute-start.7
  50.2 3.7 collective-permute-start.5
  58.8 3.8 collective-permute-done.4
  65.4 7.6 %collective-permute-done.11 = f32[3,16,256]{2,1,0:T(8,128)S(1)} collective-permute-done((f32[3,16,256]{2,1,0:T(8,128)S(1)}, f32[3,16,256]{2,1,0:T(8,128)S(1)}, u32[]{:S(2)}, u32[]{:S(2)}) %collective-permute-start.11) | collective-permute-done | bytes 49184 | tf_op jit(solution)/shard_map/ppermute | solution.py:38
  73.8 7.8 %collective-permute-done.12 = f32[3,16,256]{2,1,0:T(8,128)S(1)} collective-permute-done((f32[3,16,256]{2,1,0:T(8,128)S(1)}, f32[3,16,256]{2,1,0:T(8,128)S(1)}, u32[]{:S(2)}, u32[]{:S(2)}) %collective-permute-start.12) | collective-permute-done | bytes 49184 | tf_op jit(solution)/shard_map/ppermute | solution.py:38
  82.4 6.8 %collective-permute-start.20 = (f32[3,16,256]{2,1,0:T(8,128)S(1)}, f32[3,16,256]{2,1,0:T(8,128)S(1)}, u32[]{:S(2)}, u32[]{:S(2)}) collective-permute-start(f32[3,16,256]{2,1,0:T(8,128)S(1)} %broadcast_select_fusion.22), channel_id=1, source_target_pairs={{0,64},{8,72},{16,80},{24,88},{32,96},{40,104},{48,112},{56,120},{... | collective-permute-start | bytes 147464 | tf_op jit(solution)/shard_map/ppermute | solution.py:38
  89.3 2.9 collective-permute-done.13
  102.7 6.8 %collective-permute-done.27 = f32[3,16,128]{2,1,0:T(8,128)S(1)} collective-permute-done((f32[3,16,128]{2,1,0:T(8,128)S(1)}, f32[3,16,128]{2,1,0:T(8,128)S(1)}, u32[]{:S(2)}, u32[]{:S(2)}) %collective-permute-start.27) | collective-permute-done | bytes 24608 | tf_op jit(solution)/shard_map/ppermute | solution.py:34
  109.5 7.1 %collective-permute-done.28 = f32[3,16,256]{2,1,0:T(8,128)S(1)} collective-permute-done((f32[3,16,256]{2,1,0:T(8,128)S(1)}, f32[3,16,256]{2,1,0:T(8,128)S(1)}, u32[]{:S(2)}, u32[]{:S(2)}) %collective-permute-start.28) | collective-permute-done | bytes 49184 | tf_op jit(solution)/shard_map/ppermute | solution.py:38
  117.0 7.5 %collective-permute-done.29 = f32[3,16,256]{2,1,0:T(8,128)S(1)} collective-permute-done((f32[3,16,256]{2,1,0:T(8,128)S(1)}, f32[3,16,256]{2,1,0:T(8,128)S(1)}, u32[]{:S(2)}, u32[]{:S(2)}) %collective-permute-start.29) | collective-permute-done | bytes 49184 | tf_op jit(solution)/shard_map/ppermute | solution.py:38
  126.6 6.4 %collective-permute-start.25 = (f32[3,16,1,128]{3,1,0,2:T(8,128)S(1)}, f32[3,16,1,128]{3,1,0,2:T(8,128)S(1)}, u32[]{:S(2)}, u32[]{:S(2)}) collective-permute-start(f32[3,16,1,128]{3,1,0,2:T(8,128)S(1)} %get-tuple-element.140), channel_id=1, source_target_pairs={{1,0},{2,1},{3,2},{4,3},{5,4},{6,5},{7,6},{9,8},{10,9},{11,10},{12... | collective-permute-start | bytes 73736 | tf_op jit(solution)/shard_map/ppermute | solution.py:19
  133.1 5.3 %collective-permute-start.23 = (f32[3,16,16,1]{3,1,0,2:T(8,128)S(1)}, f32[3,16,16,1]{3,1,0,2:T(8,128)S(1)}, u32[]{:S(2)}, u32[]{:S(2)}) collective-permute-start(f32[3,16,16,1]{3,1,0,2:T(8,128)S(1)} %get-tuple-element.137), channel_id=1, source_target_pairs={{8,0},{16,8},{24,16},{32,24},{40,32},{48,40},{56,48},{64,56},{72,6... | collective-permute-start | bytes 9224 | tf_op jit(solution)/shard_map/ppermute | solution.py:19
  138.6 6.9 %collective-permute-done.22 = f32[3,16,16,1]{3,1,0,2:T(8,128)S(1)} collective-permute-done((f32[3,16,16,1]{3,1,0,2:T(8,128)S(1)}, f32[3,16,16,1]{3,1,0,2:T(8,128)S(1)}, u32[]{:S(2)}, u32[]{:S(2)}) %collective-permute-start.22) | collective-permute-done | bytes 3104 | tf_op jit(solution)/shard_map/ppermute | solution.py:16
  145.8 3.2 collective-permute-done.31
  151.0 3.7 collective-permute-done.32
  159.4 5.3 %collective-permute-done.38 = f32[3,16,128]{2,1,0:T(8,128)S(1)} collective-permute-done((f32[3,16,128]{2,1,0:T(8,128)S(1)}, f32[3,16,128]{2,1,0:T(8,128)S(1)}, u32[]{:S(2)}, u32[]{:S(2)}) %collective-permute-start.38) | collective-permute-done | bytes 24608 | tf_op jit(solution)/shard_map/ppermute | solution.py:34
  166.3 5.5 %collective-permute-done.39 = f32[3,16,256]{2,1,0:T(8,128)S(1)} collective-permute-done((f32[3,16,256]{2,1,0:T(8,128)S(1)}, f32[3,16,256]{2,1,0:T(8,128)S(1)}, u32[]{:S(2)}, u32[]{:S(2)}) %collective-permute-start.39) | collective-permute-done | bytes 49184 | tf_op jit(solution)/shard_map/ppermute | solution.py:38
  172.1 7.5 %collective-permute-done.40 = f32[3,16,256]{2,1,0:T(8,128)S(1)} collective-permute-done((f32[3,16,256]{2,1,0:T(8,128)S(1)}, f32[3,16,256]{2,1,0:T(8,128)S(1)}, u32[]{:S(2)}, u32[]{:S(2)}) %collective-permute-start.40) | collective-permute-done | bytes 49184 | tf_op jit(solution)/shard_map/ppermute | solution.py:38
  181.9 6.0 %collective-permute-start.36 = (f32[3,16,1,128]{3,1,0,2:T(8,128)S(1)}, f32[3,16,1,128]{3,1,0,2:T(8,128)S(1)}, u32[]{:S(2)}, u32[]{:S(2)}) collective-permute-start(f32[3,16,1,128]{3,1,0,2:T(8,128)S(1)} %get-tuple-element.135), channel_id=1, source_target_pairs={{1,0},{2,1},{3,2},{4,3},{5,4},{6,5},{7,6},{9,8},{10,9},{11,10},{12... | collective-permute-start | bytes 73736 | tf_op jit(solution)/shard_map/ppermute | solution.py:19
  188.0 5.3 %collective-permute-start.34 = (f32[3,16,16,1]{3,1,0,2:T(8,128)S(1)}, f32[3,16,16,1]{3,1,0,2:T(8,128)S(1)}, u32[]{:S(2)}, u32[]{:S(2)}) collective-permute-start(f32[3,16,16,1]{3,1,0,2:T(8,128)S(1)} %get-tuple-element.132), channel_id=1, source_target_pairs={{8,0},{16,8},{24,16},{32,24},{40,32},{48,40},{56,48},{64,56},{72,6... | collective-permute-start | bytes 9224 | tf_op jit(solution)/shard_map/ppermute | solution.py:19
  193.5 6.9 %collective-permute-done.33 = f32[3,16,16,1]{3,1,0,2:T(8,128)S(1)} collective-permute-done((f32[3,16,16,1]{3,1,0,2:T(8,128)S(1)}, f32[3,16,16,1]{3,1,0,2:T(8,128)S(1)}, u32[]{:S(2)}, u32[]{:S(2)}) %collective-permute-start.33) | collective-permute-done | bytes 3104 | tf_op jit(solution)/shard_map/ppermute | solution.py:16
  200.7 3.6 collective-permute-done.42
  206.2 3.8 collective-permute-done.43
  213.7 5.7 %collective-permute-done.49 = f32[3,16,128]{2,1,0:T(8,128)S(1)} collective-permute-done((f32[3,16,128]{2,1,0:T(8,128)S(1)}, f32[3,16,128]{2,1,0:T(8,128)S(1)}, u32[]{:S(2)}, u32[]{:S(2)}) %collective-permute-start.49) | collective-permute-done | bytes 24608 | tf_op jit(solution)/shard_map/ppermute | solution.py:34
  221.0 5.5 %collective-permute-done.50 = f32[3,16,256]{2,1,0:T(8,128)S(1)} collective-permute-done((f32[3,16,256]{2,1,0:T(8,128)S(1)}, f32[3,16,256]{2,1,0:T(8,128)S(1)}, u32[]{:S(2)}, u32[]{:S(2)}) %collective-permute-start.50) | collective-permute-done | bytes 49184 | tf_op jit(solution)/shard_map/ppermute | solution.py:38
  226.8 7.5 %collective-permute-done.51 = f32[3,16,256]{2,1,0:T(8,128)S(1)} collective-permute-done((f32[3,16,256]{2,1,0:T(8,128)S(1)}, f32[3,16,256]{2,1,0:T(8,128)S(1)}, u32[]{:S(2)}, u32[]{:S(2)}) %collective-permute-start.51) | collective-permute-done | bytes 49184 | tf_op jit(solution)/shard_map/ppermute | solution.py:38
  237.0 6.0 %collective-permute-start.47 = (f32[3,16,1,128]{3,1,0,2:T(8,128)S(1)}, f32[3,16,1,128]{3,1,0,2:T(8,128)S(1)}, u32[]{:S(2)}, u32[]{:S(2)}) collective-permute-start(f32[3,16,1,128]{3,1,0,2:T(8,128)S(1)} %copy-done.16), channel_id=1, source_target_pairs={{1,0},{2,1},{3,2},{4,3},{5,4},{6,5},{7,6},{9,8},{10,9},{11,10},{12... | collective-permute-start | bytes 73736 | tf_op jit(solution)/shard_map/ppermute | solution.py:19
  243.1 5.3 %collective-permute-start.45 = (f32[3,16,16,1]{3,1,0,2:T(8,128)S(1)}, f32[3,16,16,1]{3,1,0,2:T(8,128)S(1)}, u32[]{:S(2)}, u32[]{:S(2)}) collective-permute-start(f32[3,16,16,1]{3,1,0,2:T(8,128)S(1)} %get-tuple-element.127), channel_id=1, source_target_pairs={{8,0},{16,8},{24,16},{32,24},{40,32},{48,40},{56,48},{64,56},{72,6... | collective-permute-start | bytes 9224 | tf_op jit(solution)/shard_map/ppermute | solution.py:19
  248.6 6.9 %collective-permute-done.44 = f32[3,16,16,1]{3,1,0,2:T(8,128)S(1)} collective-permute-done((f32[3,16,16,1]{3,1,0,2:T(8,128)S(1)}, f32[3,16,16,1]{3,1,0,2:T(8,128)S(1)}, u32[]{:S(2)}, u32[]{:S(2)}) %collective-permute-start.44) | collective-permute-done | bytes 3104 | tf_op jit(solution)/shard_map/ppermute | solution.py:16
  255.8 3.1 collective-permute-done.53
  260.6 4.1 collective-permute-done.54
  271.8 6.0 %collective-permute-start.58 = (f32[3,16,1,128]{3,2,1,0:T(1,128)S(1)}, f32[3,16,1,128]{3,2,1,0:T(1,128)S(1)}, u32[]{:S(2)}, u32[]{:S(2)}) collective-permute-start(f32[3,16,1,128]{3,2,1,0:T(1,128)S(1)} %slice.757), channel_id=1, source_target_pairs={{1,0},{2,1},{3,2},{4,3},{5,4},{6,5},{7,6},{9,8},{10,9},{11,10},{12... | collective-permute-start | bytes 73736 | tf_op jit(solution)/shard_map/ppermute | solution.py:19
  279.0 5.2 %collective-permute-start.56 = (f32[3,16,16,1]{3,1,0,2:T(8,128)S(1)}, f32[3,16,16,1]{3,1,0,2:T(8,128)S(1)}, u32[]{:S(2)}, u32[]{:S(2)}) collective-permute-start(f32[3,16,16,1]{3,1,0,2:T(8,128)S(1)} %copy-done.5), channel_id=1, source_target_pairs={{8,0},{16,8},{24,16},{32,24},{40,32},{48,40},{56,48},{64,56},{72,6... | collective-permute-start | bytes 9224 | tf_op jit(solution)/shard_map/ppermute | solution.py:19
  284.3 4.6 collective-permute-done.55
  291.7 7.5 %collective-permute-done.62 = f32[3,16,256]{2,1,0:T(8,128)S(1)} collective-permute-done((f32[3,16,256]{2,1,0:T(8,128)S(1)}, f32[3,16,256]{2,1,0:T(8,128)S(1)}, u32[]{:S(2)}, u32[]{:S(2)}) %collective-permute-start.62) | collective-permute-done | bytes 49184 | tf_op jit(solution)/shard_map/ppermute | solution.py:38
  299.5 8.4 %collective-permute-done.63 = f32[3,16,256]{2,1,0:T(8,128)S(1)} collective-permute-done((f32[3,16,256]{2,1,0:T(8,128)S(1)}, f32[3,16,256]{2,1,0:T(8,128)S(1)}, u32[]{:S(2)}, u32[]{:S(2)}) %collective-permute-start.63) | collective-permute-done | bytes 49184 | tf_op jit(solution)/shard_map/ppermute | solution.py:38
  308.1 10.3 %collective-permute-done.64 = f32[3,16,256]{2,1,0:T(8,128)S(1)} collective-permute-done((f32[3,16,256]{2,1,0:T(8,128)S(1)}, f32[3,16,256]{2,1,0:T(8,128)S(1)}, u32[]{:S(2)}, u32[]{:S(2)}) %collective-permute-start.64) | collective-permute-done | bytes 49184 | tf_op jit(solution)/shard_map/ppermute | solution.py:38
  320.2 3.9 collective-permute-done.65
  327.6 6.0 %collective-permute-done.71 = f32[3,16,128]{2,1,0:T(8,128)S(1)} collective-permute-done((f32[3,16,128]{2,1,0:T(8,128)S(1)}, f32[3,16,128]{2,1,0:T(8,128)S(1)}, u32[]{:S(2)}, u32[]{:S(2)}) %collective-permute-start.71) | collective-permute-done | bytes 24608 | tf_op jit(solution)/shard_map/ppermute | solution.py:34
  333.7 7.1 %collective-permute-done.72 = f32[3,16,256]{2,1,0:T(8,128)S(1)} collective-permute-done((f32[3,16,256]{2,1,0:T(8,128)S(1)}, f32[3,16,256]{2,1,0:T(8,128)S(1)}, u32[]{:S(2)}, u32[]{:S(2)}) %collective-permute-start.72) | collective-permute-done | bytes 49184 | tf_op jit(solution)/shard_map/ppermute | solution.py:38
  342.9 6.0 %collective-permute-start.69 = (f32[3,16,1,128]{3,1,0,2:T(8,128)S(1)}, f32[3,16,1,128]{3,1,0,2:T(8,128)S(1)}, u32[]{:S(2)}, u32[]{:S(2)}) collective-permute-start(f32[3,16,1,128]{3,1,0,2:T(8,128)S(1)} %get-tuple-element.118), channel_id=1, source_target_pairs={{1,0},{2,1},{3,2},{4,3},{5,4},{6,5},{7,6},{9,8},{10,9},{11,10},{12... | collective-permute-start | bytes 73736 | tf_op jit(solution)/shard_map/ppermute | solution.py:19
  349.1 5.3 %collective-permute-start.67 = (f32[3,16,16,1]{3,1,0,2:T(8,128)S(1)}, f32[3,16,16,1]{3,1,0,2:T(8,128)S(1)}, u32[]{:S(2)}, u32[]{:S(2)}) collective-permute-start(f32[3,16,16,1]{3,1,0,2:T(8,128)S(1)} %get-tuple-element.119), channel_id=1, source_target_pairs={{8,0},{16,8},{24,16},{32,24},{40,32},{48,40},{56,48},{64,56},{72,6... | collective-permute-start | bytes 9224 | tf_op jit(solution)/shard_map/ppermute | solution.py:19
  354.7 5.7 %collective-permute-done.66 = f32[3,16,16,1]{3,1,0,2:T(8,128)S(1)} collective-permute-done((f32[3,16,16,1]{3,1,0,2:T(8,128)S(1)}, f32[3,16,16,1]{3,1,0,2:T(8,128)S(1)}, u32[]{:S(2)}, u32[]{:S(2)}) %collective-permute-start.66) | collective-permute-done | bytes 3104 | tf_op jit(solution)/shard_map/ppermute | solution.py:16
  363.6 10.3 %collective-permute-done.75 = f32[3,16,256]{2,1,0:T(8,128)S(1)} collective-permute-done((f32[3,16,256]{2,1,0:T(8,128)S(1)}, f32[3,16,256]{2,1,0:T(8,128)S(1)}, u32[]{:S(2)}, u32[]{:S(2)}) %collective-permute-start.75) | collective-permute-done | bytes 49184 | tf_op jit(solution)/shard_map/ppermute | solution.py:38
  375.7 3.9 collective-permute-done.76
  380.9 3.7 collective-permute-start.82
  384.7 3.2 collective-permute-done.82
  388.0 7.1 %collective-permute-done.83 = f32[3,16,256]{2,1,0:T(8,128)S(1)} collective-permute-done((f32[3,16,256]{2,1,0:T(8,128)S(1)}, f32[3,16,256]{2,1,0:T(8,128)S(1)}, u32[]{:S(2)}, u32[]{:S(2)}) %collective-permute-start.83) | collective-permute-done | bytes 49184 | tf_op jit(solution)/shard_map/ppermute | solution.py:38
  397.2 6.0 %collective-permute-start.80 = (f32[3,16,1,128]{3,1,0,2:T(8,128)S(1)}, f32[3,16,1,128]{3,1,0,2:T(8,128)S(1)}, u32[]{:S(2)}, u32[]{:S(2)}) collective-permute-start(f32[3,16,1,128]{3,1,0,2:T(8,128)S(1)} %get-tuple-element.109), channel_id=1, source_target_pairs={{1,0},{2,1},{3,2},{4,3},{5,4},{6,5},{7,6},{9,8},{10,9},{11,10},{12... | collective-permute-start | bytes 73736 | tf_op jit(solution)/shard_map/ppermute | solution.py:19
  403.4 5.3 %collective-permute-start.78 = (f32[3,16,16,1]{3,1,0,2:T(8,128)S(1)}, f32[3,16,16,1]{3,1,0,2:T(8,128)S(1)}, u32[]{:S(2)}, u32[]{:S(2)}) collective-permute-start(f32[3,16,16,1]{3,1,0,2:T(8,128)S(1)} %get-tuple-element.110), channel_id=1, source_target_pairs={{8,0},{16,8},{24,16},{32,24},{40,32},{48,40},{56,48},{64,56},{72,6... | collective-permute-start | bytes 9224 | tf_op jit(solution)/shard_map/ppermute | solution.py:19
  408.8 5.9 %collective-permute-done.77 = f32[3,16,16,1]{3,1,0,2:T(8,128)S(1)} collective-permute-done((f32[3,16,16,1]{3,1,0,2:T(8,128)S(1)}, f32[3,16,16,1]{3,1,0,2:T(8,128)S(1)}, u32[]{:S(2)}, u32[]{:S(2)}) %collective-permute-start.77) | collective-permute-done | bytes 3104 | tf_op jit(solution)/shard_map/ppermute | solution.py:16
  415.0 2.7 collective-permute-done.85
  417.9 10.3 %collective-permute-done.86 = f32[3,16,256]{2,1,0:T(8,128)S(1)} collective-permute-done((f32[3,16,256]{2,1,0:T(8,128)S(1)}, f32[3,16,256]{2,1,0:T(8,128)S(1)}, u32[]{:S(2)}, u32[]{:S(2)}) %collective-permute-start.86) | collective-permute-done | bytes 49184 | tf_op jit(solution)/shard_map/ppermute | solution.py:38
  430.0 3.9 collective-permute-done.87
  444.2 3.3 collective-permute-done.90
  449.4 6.3 %collective-permute-done.91 = f32[]{:T(128)} collective-permute-done((f32[]{:T(128)}, f32[]{:T(128)}, u32[]{:S(2)}, u32[]{:S(2)}) %collective-permute-start.91) | collective-permute-done | bytes 36 | tf_op jit(solution)/shard_map/ppermute | solution.py:50
  456.3 2.8 collective-permute-start.92
  467.8 3.9 collective-permute-done.94
  (313 shorter events, 113.5 us)
Async XLA Ops:
  3.1 41.5 %collective-permute-start.15 = (f32[3,16,128]{2,1,0:T(8,128)}, f32[3,16,128]{2,1,0:T(8,128)}, u32[]{:S(2)}, u32[]{:S(2)}) collective-permute-start(f32[3,16,128]{2,1,0:T(8,128)} %rev.25), channel_id=1, source_target_pairs={{0,0},{248,8},{240,16},{232,24},{224,32},{216,40},{208,48},{200,56... | collective-permute-start | bytes 73736 | tf_op jit(solution)/shard_map/ppermute | solution.py:33
  5.2 49.4 %collective-permute-start.16 = (f32[3,16,128]{2,1,0:T(8,128)}, f32[3,16,128]{2,1,0:T(8,128)}, u32[]{:S(2)}, u32[]{:S(2)}) collective-permute-start(f32[3,16,128]{2,1,0:T(8,128)} %rev.25), channel_id=1, source_target_pairs={{248,0},{240,8},{232,16},{224,24},{216,32},{208,40},{200,48},{192,... | collective-permute-start | bytes 73736 | tf_op jit(solution)/shard_map/ppermute | solution.py:34
  13.6 36.6 %collective-permute-start.8 = (f32[3,16,128]{2,1,0:T(8,128)}, f32[3,16,128]{2,1,0:T(8,128)}, u32[]{:S(2)}, u32[]{:S(2)}) collective-permute-start(f32[3,16,128]{2,1,0:T(8,128)} %rev.24), channel_id=1, source_target_pairs={{0,0},{248,8},{240,16},{232,24},{224,32},{216,40},{208,48},{200,56... | collective-permute-start | bytes 73736 | tf_op jit(solution)/shard_map/ppermute | solution.py:33
  16.8 12.9 %collective-permute-start.1 = (f32[4,16,16,1]{3,1,2,0:T(8,128)}, f32[4,16,16,1]{3,1,2,0:T(8,128)S(1)}, u32[]{:S(2)}, u32[]{:S(2)}) collective-permute-start(f32[4,16,16,1]{3,1,2,0:T(8,128)} %get-tuple-element.104), channel_id=1, source_target_pairs={{8,0},{16,8},{24,16},{32,24},{40,32},{48,40},{56,48},{64,56},{72,6... | collective-permute-start | bytes 12296 | tf_op jit(solution)/shard_map/ppermute | solution.py:19
  22.4 12.4 %collective-permute-start = (f32[4,16,16,1]{3,1,2,0:T(8,128)}, f32[4,16,16,1]{3,1,2,0:T(8,128)S(1)}, u32[]{:S(2)}, u32[]{:S(2)}) collective-permute-start(f32[4,16,16,1]{3,1,2,0:T(8,128)} %get-tuple-element.103), channel_id=1, source_target_pairs={{0,8},{8,16},{16,24},{24,32},{32,40},{40,48},{48,56},{56,64},{64,7... | collective-permute-start | bytes 12296 | tf_op jit(solution)/shard_map/ppermute | solution.py:16
  29.6 11.1 %collective-permute-start.2 = (f32[3,16,16,1]{3,1,0,2:T(8,128)}, f32[3,16,16,1]{3,1,0,2:T(8,128)S(1)}, u32[]{:S(2)}, u32[]{:S(2)}) collective-permute-start(f32[3,16,16,1]{3,1,0,2:T(8,128)} %get-tuple-element.143), channel_id=1, source_target_pairs={{0,8},{8,16},{16,24},{24,32},{32,40},{40,48},{48,56},{56,64},{64,7... | collective-permute-start | bytes 9224 | tf_op jit(solution)/shard_map/ppermute | solution.py:16
  40.7 16.8 %collective-permute-start.9 = (f32[3,16,128]{2,1,0:T(8,128)}, f32[3,16,128]{2,1,0:T(8,128)S(1)}, u32[]{:S(2)}, u32[]{:S(2)}) collective-permute-start(f32[3,16,128]{2,1,0:T(8,128)} %rev.24), channel_id=1, source_target_pairs={{248,0},{240,8},{232,16},{224,24},{216,32},{208,40},{200,48},{192,... | collective-permute-start | bytes 73736 | tf_op jit(solution)/shard_map/ppermute | solution.py:34
  40.7 21.9 %collective-permute-start.6 = (f32[3,16,1,128]{3,1,0,2:T(8,128)S(1)}, f32[3,16,1,128]{3,1,0,2:T(8,128)S(1)}, u32[]{:S(2)}, u32[]{:S(2)}) collective-permute-start(f32[3,16,1,128]{3,1,0,2:T(8,128)S(1)} %copy-done.15), channel_id=1, source_target_pairs={{0,1},{1,2},{2,3},{3,4},{4,5},{5,6},{6,7},{8,9},{9,10},{10,11},{11... | collective-permute-start | bytes 73736 | tf_op jit(solution)/shard_map/ppermute | solution.py:16
  45.0 17.6 %collective-permute-start.7 = (f32[3,16,1,128]{3,1,0,2:T(8,128)S(1)}, f32[3,16,1,128]{3,1,0,2:T(8,128)S(1)}, u32[]{:S(2)}, u32[]{:S(2)}) collective-permute-start(f32[3,16,1,128]{3,1,0,2:T(8,128)S(1)} %copy-done.14), channel_id=1, source_target_pairs={{1,0},{2,1},{3,2},{4,3},{5,4},{6,5},{7,6},{9,8},{10,9},{11,10},{12... | collective-permute-start | bytes 73736 | tf_op jit(solution)/shard_map/ppermute | solution.py:19
  54.6 7.9 %collective-permute-start.4 = (f32[4,16,1,128]{3,1,2,0:T(8,128)S(1)}, f32[4,16,1,128]{3,1,2,0:T(8,128)S(1)}, u32[]{:S(2)}, u32[]{:S(2)}) collective-permute-start(f32[4,16,1,128]{3,1,2,0:T(8,128)S(1)} %copy-done.12), channel_id=1, source_target_pairs={{0,1},{1,2},{2,3},{3,4},{4,5},{5,6},{6,7},{8,9},{9,10},{10,11},{11... | collective-permute-start | bytes 98312 | tf_op jit(solution)/shard_map/ppermute | solution.py:16
  57.5 7.8 %collective-permute-start.17 = (f32[3,16,256]{2,1,0:T(8,128)S(1)}, f32[3,16,256]{2,1,0:T(8,128)S(1)}, u32[]{:S(2)}, u32[]{:S(2)}) collective-permute-start(f32[3,16,256]{2,1,0:T(8,128)S(1)} %constant_dynamic-update-slice_fusion.2), channel_id=1, source_target_pairs={{0,8},{8,16},{16,24},{24,32},{32,40},{40,48},{48,56},{56,64},{64,7... | collective-permute-start | bytes 147464 | tf_op jit(solution)/shard_map/ppermute | solution.py:38
  57.5 7.6 %collective-permute-start.10 = (f32[3,16,256]{2,1,0:T(8,128)S(1)}, f32[3,16,256]{2,1,0:T(8,128)S(1)}, u32[]{:S(2)}, u32[]{:S(2)}) collective-permute-start(f32[3,16,256]{2,1,0:T(8,128)S(1)} %constant_dynamic-update-slice_fusion), channel_id=1, source_target_pairs={{0,8},{8,16},{16,24},{24,32},{32,40},{40,48},{48,56},{56,64},{64,7... | collective-permute-start | bytes 147464 | tf_op jit(solution)/shard_map/ppermute | solution.py:38
  65.2 7.8 %collective-permute-start.11 = (f32[3,16,256]{2,1,0:T(8,128)S(1)}, f32[3,16,256]{2,1,0:T(8,128)S(1)}, u32[]{:S(2)}, u32[]{:S(2)}) collective-permute-start(f32[3,16,256]{2,1,0:T(8,128)S(1)} %broadcast_select_fusion.7), channel_id=1, source_target_pairs={{0,16},{8,24},{16,32},{24,40},{32,48},{40,56},{48,64},{56,72},{64,... | collective-permute-start | bytes 147464 | tf_op jit(solution)/shard_map/ppermute | solution.py:38
  65.3 8.4 %collective-permute-start.18 = (f32[3,16,256]{2,1,0:T(8,128)S(1)}, f32[3,16,256]{2,1,0:T(8,128)S(1)}, u32[]{:S(2)}, u32[]{:S(2)}) collective-permute-start(f32[3,16,256]{2,1,0:T(8,128)S(1)} %broadcast_select_fusion.6), channel_id=1, source_target_pairs={{0,16},{8,24},{16,32},{24,40},{32,48},{40,56},{48,64},{56,72},{64,... | collective-permute-start | bytes 147464 | tf_op jit(solution)/shard_map/ppermute | solution.py:38
  73.0 8.7 %collective-permute-start.12 = (f32[3,16,256]{2,1,0:T(8,128)S(1)}, f32[3,16,256]{2,1,0:T(8,128)S(1)}, u32[]{:S(2)}, u32[]{:S(2)}) collective-permute-start(f32[3,16,256]{2,1,0:T(8,128)S(1)} %broadcast_select_fusion.15), channel_id=1, source_target_pairs={{0,32},{8,40},{16,48},{24,56},{32,64},{40,72},{48,80},{56,88},{64,... | collective-permute-start | bytes 147464 | tf_op jit(solution)/shard_map/ppermute | solution.py:38
  73.7 8.7 %collective-permute-start.19 = (f32[3,16,256]{2,1,0:T(8,128)S(1)}, f32[3,16,256]{2,1,0:T(8,128)S(1)}, u32[]{:S(2)}, u32[]{:S(2)}) collective-permute-start(f32[3,16,256]{2,1,0:T(8,128)S(1)} %broadcast_select_fusion.14), channel_id=1, source_target_pairs={{0,32},{8,40},{16,48},{24,56},{32,64},{40,72},{48,80},{56,88},{64,... | collective-permute-start | bytes 147464 | tf_op jit(solution)/shard_map/ppermute | solution.py:38
  81.7 10.5 %collective-permute-start.13 = (f32[3,16,256]{2,1,0:T(8,128)S(1)}, f32[3,16,256]{2,1,0:T(8,128)S(1)}, u32[]{:S(2)}, u32[]{:S(2)}) collective-permute-start(f32[3,16,256]{2,1,0:T(8,128)S(1)} %broadcast_select_fusion.23), channel_id=1, source_target_pairs={{0,64},{8,72},{16,80},{24,88},{32,96},{40,104},{48,112},{56,120},{... | collective-permute-start | bytes 147464 | tf_op jit(solution)/shard_map/ppermute | solution.py:38
  82.4 11.6 %collective-permute-start.20 = (f32[3,16,256]{2,1,0:T(8,128)S(1)}, f32[3,16,256]{2,1,0:T(8,128)S(1)}, u32[]{:S(2)}, u32[]{:S(2)}) collective-permute-start(f32[3,16,256]{2,1,0:T(8,128)S(1)} %broadcast_select_fusion.22), channel_id=1, source_target_pairs={{0,64},{8,72},{16,80},{24,88},{32,96},{40,104},{48,112},{56,120},{... | collective-permute-start | bytes 147464 | tf_op jit(solution)/shard_map/ppermute | solution.py:38
  116.7 7.8 %collective-permute-start.29 = (f32[3,16,256]{2,1,0:T(8,128)S(1)}, f32[3,16,256]{2,1,0:T(8,128)S(1)}, u32[]{:S(2)}, u32[]{:S(2)}) collective-permute-start(f32[3,16,256]{2,1,0:T(8,128)S(1)} %broadcast_select_fusion.5), channel_id=1, source_target_pairs={{0,16},{8,24},{16,32},{24,40},{32,48},{40,56},{48,64},{56,72},{64,... | collective-permute-start | bytes 147464 | tf_op jit(solution)/shard_map/ppermute | solution.py:38
  124.5 13.9 %collective-permute-start.30 = (f32[3,16,256]{2,1,0:T(8,128)S(1)}, f32[3,16,256]{2,1,0:T(8,128)S(1)}, u32[]{:S(2)}, u32[]{:S(2)}) collective-permute-start(f32[3,16,256]{2,1,0:T(8,128)S(1)} %broadcast_select_fusion.13), channel_id=1, source_target_pairs={{0,32},{8,40},{16,48},{24,56},{32,64},{40,72},{48,80},{56,88},{64,... | collective-permute-start | bytes 147464 | tf_op jit(solution)/shard_map/ppermute | solution.py:38
  124.6 26.3 %collective-permute-start.24 = (f32[3,16,1,128]{3,1,0,2:T(8,128)S(1)}, f32[3,16,1,128]{3,1,0,2:T(8,128)S(1)}, u32[]{:S(2)}, u32[]{:S(2)}) collective-permute-start(f32[3,16,1,128]{3,1,0,2:T(8,128)S(1)} %get-tuple-element.141), channel_id=1, source_target_pairs={{0,1},{1,2},{2,3},{3,4},{4,5},{5,6},{6,7},{8,9},{9,10},{10,11},{11... | collective-permute-start | bytes 73736 | tf_op jit(solution)/shard_map/ppermute | solution.py:16
  126.6 24.4 %collective-permute-start.25 = (f32[3,16,1,128]{3,1,0,2:T(8,128)S(1)}, f32[3,16,1,128]{3,1,0,2:T(8,128)S(1)}, u32[]{:S(2)}, u32[]{:S(2)}) collective-permute-start(f32[3,16,1,128]{3,1,0,2:T(8,128)S(1)} %get-tuple-element.140), channel_id=1, source_target_pairs={{1,0},{2,1},{3,2},{4,3},{5,4},{6,5},{7,6},{9,8},{10,9},{11,10},{12... | collective-permute-start | bytes 73736 | tf_op jit(solution)/shard_map/ppermute | solution.py:19
  133.0 12.5 %collective-permute-start.22 = (f32[3,16,16,1]{3,1,0,2:T(8,128)S(1)}, f32[3,16,16,1]{3,1,0,2:T(8,128)S(1)}, u32[]{:S(2)}, u32[]{:S(2)}) collective-permute-start(f32[3,16,16,1]{3,1,0,2:T(8,128)S(1)} %get-tuple-element.138), channel_id=1, source_target_pairs={{0,8},{8,16},{16,24},{24,32},{32,40},{40,48},{48,56},{56,64},{64,7... | collective-permute-start | bytes 9224 | tf_op jit(solution)/shard_map/ppermute | solution.py:16
  133.1 12.4 %collective-permute-start.23 = (f32[3,16,16,1]{3,1,0,2:T(8,128)S(1)}, f32[3,16,16,1]{3,1,0,2:T(8,128)S(1)}, u32[]{:S(2)}, u32[]{:S(2)}) collective-permute-start(f32[3,16,16,1]{3,1,0,2:T(8,128)S(1)} %get-tuple-element.137), channel_id=1, source_target_pairs={{8,0},{16,8},{24,16},{32,24},{40,32},{48,40},{56,48},{64,56},{72,6... | collective-permute-start | bytes 9224 | tf_op jit(solution)/shard_map/ppermute | solution.py:19
  138.4 10.6 %collective-permute-start.31 = (f32[3,16,256]{2,1,0:T(8,128)S(1)}, f32[3,16,256]{2,1,0:T(8,128)S(1)}, u32[]{:S(2)}, u32[]{:S(2)}) collective-permute-start(f32[3,16,256]{2,1,0:T(8,128)S(1)} %broadcast_select_fusion.21), channel_id=1, source_target_pairs={{0,64},{8,72},{16,80},{24,88},{32,96},{40,104},{48,112},{56,120},{... | collective-permute-start | bytes 147464 | tf_op jit(solution)/shard_map/ppermute | solution.py:38
  156.9 7.7 %collective-permute-start.38 = (f32[3,16,128]{2,1,0:T(8,128)S(1)}, f32[3,16,128]{2,1,0:T(8,128)S(1)}, u32[]{:S(2)}, u32[]{:S(2)}) collective-permute-start(f32[3,16,128]{2,1,0:T(8,128)S(1)} %rev.27), channel_id=1, source_target_pairs={{248,0},{240,8},{232,16},{224,24},{216,32},{208,40},{200,48},{192,... | collective-permute-start | bytes 73736 | tf_op jit(solution)/shard_map/ppermute | solution.py:34
  171.8 7.8 %collective-permute-start.40 = (f32[3,16,256]{2,1,0:T(8,128)S(1)}, f32[3,16,256]{2,1,0:T(8,128)S(1)}, u32[]{:S(2)}, u32[]{:S(2)}) collective-permute-start(f32[3,16,256]{2,1,0:T(8,128)S(1)} %broadcast_select_fusion.4), channel_id=1, source_target_pairs={{0,16},{8,24},{16,32},{24,40},{32,48},{40,56},{48,64},{56,72},{64,... | collective-permute-start | bytes 147464 | tf_op jit(solution)/shard_map/ppermute | solution.py:38
  179.6 13.8 %collective-permute-start.41 = (f32[3,16,256]{2,1,0:T(8,128)S(1)}, f32[3,16,256]{2,1,0:T(8,128)S(1)}, u32[]{:S(2)}, u32[]{:S(2)}) collective-permute-start(f32[3,16,256]{2,1,0:T(8,128)S(1)} %broadcast_select_fusion.12), channel_id=1, source_target_pairs={{0,32},{8,40},{16,48},{24,56},{32,64},{40,72},{48,80},{56,88},{64,... | collective-permute-start | bytes 147464 | tf_op jit(solution)/shard_map/ppermute | solution.py:38
  180.0 26.2 %collective-permute-start.35 = (f32[3,16,1,128]{3,1,0,2:T(8,128)S(1)}, f32[3,16,1,128]{3,1,0,2:T(8,128)S(1)}, u32[]{:S(2)}, u32[]{:S(2)}) collective-permute-start(f32[3,16,1,128]{3,1,0,2:T(8,128)S(1)} %get-tuple-element.136), channel_id=1, source_target_pairs={{0,1},{1,2},{2,3},{3,4},{4,5},{5,6},{6,7},{8,9},{9,10},{10,11},{11... | collective-permute-start | bytes 73736 | tf_op jit(solution)/shard_map/ppermute | solution.py:16
  181.9 24.2 %collective-permute-start.36 = (f32[3,16,1,128]{3,1,0,2:T(8,128)S(1)}, f32[3,16,1,128]{3,1,0,2:T(8,128)S(1)}, u32[]{:S(2)}, u32[]{:S(2)}) collective-permute-start(f32[3,16,1,128]{3,1,0,2:T(8,128)S(1)} %get-tuple-element.135), channel_id=1, source_target_pairs={{1,0},{2,1},{3,2},{4,3},{5,4},{6,5},{7,6},{9,8},{10,9},{11,10},{12... | collective-permute-start | bytes 73736 | tf_op jit(solution)/shard_map/ppermute | solution.py:19
  187.9 12.5 %collective-permute-start.33 = (f32[3,16,16,1]{3,1,0,2:T(8,128)S(1)}, f32[3,16,16,1]{3,1,0,2:T(8,128)S(1)}, u32[]{:S(2)}, u32[]{:S(2)}) collective-permute-start(f32[3,16,16,1]{3,1,0,2:T(8,128)S(1)} %get-tuple-element.133), channel_id=1, source_target_pairs={{0,8},{8,16},{16,24},{24,32},{32,40},{40,48},{48,56},{56,64},{64,7... | collective-permute-start | bytes 9224 | tf_op jit(solution)/shard_map/ppermute | solution.py:16
  188.0 12.4 %collective-permute-start.34 = (f32[3,16,16,1]{3,1,0,2:T(8,128)S(1)}, f32[3,16,16,1]{3,1,0,2:T(8,128)S(1)}, u32[]{:S(2)}, u32[]{:S(2)}) collective-permute-start(f32[3,16,16,1]{3,1,0,2:T(8,128)S(1)} %get-tuple-element.132), channel_id=1, source_target_pairs={{8,0},{16,8},{24,16},{32,24},{40,32},{48,40},{56,48},{64,56},{72,6... | collective-permute-start | bytes 9224 | tf_op jit(solution)/shard_map/ppermute | solution.py:19
  193.4 10.9 %collective-permute-start.42 = (f32[3,16,256]{2,1,0:T(8,128)S(1)}, f32[3,16,256]{2,1,0:T(8,128)S(1)}, u32[]{:S(2)}, u32[]{:S(2)}) collective-permute-start(f32[3,16,256]{2,1,0:T(8,128)S(1)} %broadcast_select_fusion.20), channel_id=1, source_target_pairs={{0,64},{8,72},{16,80},{24,88},{32,96},{40,104},{48,112},{56,120},{... | collective-permute-start | bytes 147464 | tf_op jit(solution)/shard_map/ppermute | solution.py:38
  226.5 7.8 %collective-permute-start.51 = (f32[3,16,256]{2,1,0:T(8,128)S(1)}, f32[3,16,256]{2,1,0:T(8,128)S(1)}, u32[]{:S(2)}, u32[]{:S(2)}) collective-permute-start(f32[3,16,256]{2,1,0:T(8,128)S(1)} %broadcast_select_fusion.3), channel_id=1, source_target_pairs={{0,16},{8,24},{16,32},{24,40},{32,48},{40,56},{48,64},{56,72},{64,... | collective-permute-start | bytes 147464 | tf_op jit(solution)/shard_map/ppermute | solution.py:38
  234.3 14.1 %collective-permute-start.52 = (f32[3,16,256]{2,1,0:T(8,128)S(1)}, f32[3,16,256]{2,1,0:T(8,128)S(1)}, u32[]{:S(2)}, u32[]{:S(2)}) collective-permute-start(f32[3,16,256]{2,1,0:T(8,128)S(1)} %broadcast_select_fusion.11), channel_id=1, source_target_pairs={{0,32},{8,40},{16,48},{24,56},{32,64},{40,72},{48,80},{56,88},{64,... | collective-permute-start | bytes 147464 | tf_op jit(solution)/shard_map/ppermute | solution.py:38
  235.1 25.4 %collective-permute-start.46 = (f32[3,16,1,128]{3,1,0,2:T(8,128)S(1)}, f32[3,16,1,128]{3,1,0,2:T(8,128)S(1)}, u32[]{:S(2)}, u32[]{:S(2)}) collective-permute-start(f32[3,16,1,128]{3,1,0,2:T(8,128)S(1)} %copy-done.17), channel_id=1, source_target_pairs={{0,1},{1,2},{2,3},{3,4},{4,5},{5,6},{6,7},{8,9},{9,10},{10,11},{11... | collective-permute-start | bytes 73736 | tf_op jit(solution)/shard_map/ppermute | solution.py:16
  237.0 23.5 %collective-permute-start.47 = (f32[3,16,1,128]{3,1,0,2:T(8,128)S(1)}, f32[3,16,1,128]{3,1,0,2:T(8,128)S(1)}, u32[]{:S(2)}, u32[]{:S(2)}) collective-permute-start(f32[3,16,1,128]{3,1,0,2:T(8,128)S(1)} %copy-done.16), channel_id=1, source_target_pairs={{1,0},{2,1},{3,2},{4,3},{5,4},{6,5},{7,6},{9,8},{10,9},{11,10},{12... | collective-permute-start | bytes 73736 | tf_op jit(solution)/shard_map/ppermute | solution.py:19
  243.0 12.5 %collective-permute-start.44 = (f32[3,16,16,1]{3,1,0,2:T(8,128)S(1)}, f32[3,16,16,1]{3,1,0,2:T(8,128)S(1)}, u32[]{:S(2)}, u32[]{:S(2)}) collective-permute-start(f32[3,16,16,1]{3,1,0,2:T(8,128)S(1)} %get-tuple-element.128), channel_id=1, source_target_pairs={{0,8},{8,16},{16,24},{24,32},{32,40},{40,48},{48,56},{56,64},{64,7... | collective-permute-start | bytes 9224 | tf_op jit(solution)/shard_map/ppermute | solution.py:16
  243.1 12.4 %collective-permute-start.45 = (f32[3,16,16,1]{3,1,0,2:T(8,128)S(1)}, f32[3,16,16,1]{3,1,0,2:T(8,128)S(1)}, u32[]{:S(2)}, u32[]{:S(2)}) collective-permute-start(f32[3,16,16,1]{3,1,0,2:T(8,128)S(1)} %get-tuple-element.127), channel_id=1, source_target_pairs={{8,0},{16,8},{24,16},{32,24},{40,32},{48,40},{56,48},{64,56},{72,6... | collective-permute-start | bytes 9224 | tf_op jit(solution)/shard_map/ppermute | solution.py:19
  248.5 10.5 %collective-permute-start.53 = (f32[3,16,256]{2,1,0:T(8,128)S(1)}, f32[3,16,256]{2,1,0:T(8,128)S(1)}, u32[]{:S(2)}, u32[]{:S(2)}) collective-permute-start(f32[3,16,256]{2,1,0:T(8,128)S(1)} %broadcast_select_fusion.19), channel_id=1, source_target_pairs={{0,64},{8,72},{16,80},{24,88},{32,96},{40,104},{48,112},{56,120},{... | collective-permute-start | bytes 147464 | tf_op jit(solution)/shard_map/ppermute | solution.py:38
  266.8 12.2 %collective-permute-start.59 = (f32[3,16,128]{2,1,0:T(8,128)S(1)}, f32[3,16,128]{2,1,0:T(8,128)S(1)}, u32[]{:S(2)}, u32[]{:S(2)}) collective-permute-start(f32[3,16,128]{2,1,0:T(8,128)S(1)} %rev.29), channel_id=1, source_target_pairs={{0,0},{248,8},{240,16},{232,24},{224,32},{216,40},{208,48},{200,56... | collective-permute-start | bytes 73736 | tf_op jit(solution)/shard_map/ppermute | solution.py:33
  267.4 16.8 %collective-permute-start.60 = (f32[3,16,128]{2,1,0:T(8,128)S(1)}, f32[3,16,128]{2,1,0:T(8,128)S(1)}, u32[]{:S(2)}, u32[]{:S(2)}) collective-permute-start(f32[3,16,128]{2,1,0:T(8,128)S(1)} %rev.29), channel_id=1, source_target_pairs={{248,0},{240,8},{232,16},{224,24},{216,32},{208,40},{200,48},{192,... | collective-permute-start | bytes 73736 | tf_op jit(solution)/shard_map/ppermute | solution.py:34
  269.8 29.5 %collective-permute-start.57 = (f32[3,16,1,128]{3,1,0,2:T(8,128)S(1)}, f32[3,16,1,128]{3,1,0,2:T(8,128)S(1)}, u32[]{:S(2)}, u32[]{:S(2)}) collective-permute-start(f32[3,16,1,128]{3,1,0,2:T(8,128)S(1)} %get-tuple-element.124), channel_id=1, source_target_pairs={{0,1},{1,2},{2,3},{3,4},{4,5},{5,6},{6,7},{8,9},{9,10},{10,11},{11... | collective-permute-start | bytes 73736 | tf_op jit(solution)/shard_map/ppermute | solution.py:16
  271.8 27.6 %collective-permute-start.58 = (f32[3,16,1,128]{3,2,1,0:T(1,128)S(1)}, f32[3,16,1,128]{3,2,1,0:T(1,128)S(1)}, u32[]{:S(2)}, u32[]{:S(2)}) collective-permute-start(f32[3,16,1,128]{3,2,1,0:T(1,128)S(1)} %slice.757), channel_id=1, source_target_pairs={{1,0},{2,1},{3,2},{4,3},{5,4},{6,5},{7,6},{9,8},{10,9},{11,10},{12... | collective-permute-start | bytes 73736 | tf_op jit(solution)/shard_map/ppermute | solution.py:19
  277.8 11.1 %collective-permute-start.55 = (f32[3,16,16,1]{3,1,0,2:T(8,128)}, f32[3,16,16,1]{3,1,0,2:T(8,128)S(1)}, u32[]{:S(2)}, u32[]{:S(2)}) collective-permute-start(f32[3,16,16,1]{3,1,0,2:T(8,128)} %get-tuple-element.126), channel_id=1, source_target_pairs={{0,8},{8,16},{16,24},{24,32},{32,40},{40,48},{48,56},{56,64},{64,7... | collective-permute-start | bytes 9224 | tf_op jit(solution)/shard_map/ppermute | solution.py:16
  279.0 10.5 %collective-permute-start.56 = (f32[3,16,16,1]{3,1,0,2:T(8,128)S(1)}, f32[3,16,16,1]{3,1,0,2:T(8,128)S(1)}, u32[]{:S(2)}, u32[]{:S(2)}) collective-permute-start(f32[3,16,16,1]{3,1,0,2:T(8,128)S(1)} %copy-done.5), channel_id=1, source_target_pairs={{8,0},{16,8},{24,16},{32,24},{40,32},{48,40},{56,48},{64,56},{72,6... | collective-permute-start | bytes 9224 | tf_op jit(solution)/shard_map/ppermute | solution.py:19
  291.4 7.8 %collective-permute-start.62 = (f32[3,16,256]{2,1,0:T(8,128)S(1)}, f32[3,16,256]{2,1,0:T(8,128)S(1)}, u32[]{:S(2)}, u32[]{:S(2)}) collective-permute-start(f32[3,16,256]{2,1,0:T(8,128)S(1)} %broadcast_select_fusion.2), channel_id=1, source_target_pairs={{0,16},{8,24},{16,32},{24,40},{32,48},{40,56},{48,64},{56,72},{64,... | collective-permute-start | bytes 147464 | tf_op jit(solution)/shard_map/ppermute | solution.py:38
  299.2 8.7 %collective-permute-start.63 = (f32[3,16,256]{2,1,0:T(8,128)S(1)}, f32[3,16,256]{2,1,0:T(8,128)S(1)}, u32[]{:S(2)}, u32[]{:S(2)}) collective-permute-start(f32[3,16,256]{2,1,0:T(8,128)S(1)} %broadcast_select_fusion.10), channel_id=1, source_target_pairs={{0,32},{8,40},{16,48},{24,56},{32,64},{40,72},{48,80},{56,88},{64,... | collective-permute-start | bytes 147464 | tf_op jit(solution)/shard_map/ppermute | solution.py:38
  307.9 10.5 %collective-permute-start.64 = (f32[3,16,256]{2,1,0:T(8,128)S(1)}, f32[3,16,256]{2,1,0:T(8,128)S(1)}, u32[]{:S(2)}, u32[]{:S(2)}) collective-permute-start(f32[3,16,256]{2,1,0:T(8,128)S(1)} %broadcast_select_fusion.18), channel_id=1, source_target_pairs={{0,64},{8,72},{16,80},{24,88},{32,96},{40,104},{48,112},{56,120},{... | collective-permute-start | bytes 147464 | tf_op jit(solution)/shard_map/ppermute | solution.py:38
  340.8 13.7 %collective-permute-start.73 = (f32[3,16,256]{2,1,0:T(8,128)S(1)}, f32[3,16,256]{2,1,0:T(8,128)S(1)}, u32[]{:S(2)}, u32[]{:S(2)}) collective-permute-start(f32[3,16,256]{2,1,0:T(8,128)S(1)} %broadcast_select_fusion.1), channel_id=1, source_target_pairs={{0,16},{8,24},{16,32},{24,40},{32,48},{40,56},{48,64},{56,72},{64,... | collective-permute-start | bytes 147464 | tf_op jit(solution)/shard_map/ppermute | solution.py:38
  341.0 22.5 %collective-permute-start.68 = (f32[3,16,1,128]{3,1,0,2:T(8,128)S(1)}, f32[3,16,1,128]{3,1,0,2:T(8,128)S(1)}, u32[]{:S(2)}, u32[]{:S(2)}) collective-permute-start(f32[3,16,1,128]{3,1,0,2:T(8,128)S(1)} %get-tuple-element.117), channel_id=1, source_target_pairs={{0,1},{1,2},{2,3},{3,4},{4,5},{5,6},{6,7},{8,9},{9,10},{10,11},{11... | collective-permute-start | bytes 73736 | tf_op jit(solution)/shard_map/ppermute | solution.py:16
  342.9 20.6 %collective-permute-start.69 = (f32[3,16,1,128]{3,1,0,2:T(8,128)S(1)}, f32[3,16,1,128]{3,1,0,2:T(8,128)S(1)}, u32[]{:S(2)}, u32[]{:S(2)}) collective-permute-start(f32[3,16,1,128]{3,1,0,2:T(8,128)S(1)} %get-tuple-element.118), channel_id=1, source_target_pairs={{1,0},{2,1},{3,2},{4,3},{5,4},{6,5},{7,6},{9,8},{10,9},{11,10},{12... | collective-permute-start | bytes 73736 | tf_op jit(solution)/shard_map/ppermute | solution.py:19
  349.0 11.4 %collective-permute-start.66 = (f32[3,16,16,1]{3,1,0,2:T(8,128)S(1)}, f32[3,16,16,1]{3,1,0,2:T(8,128)S(1)}, u32[]{:S(2)}, u32[]{:S(2)}) collective-permute-start(f32[3,16,16,1]{3,1,0,2:T(8,128)S(1)} %get-tuple-element.120), channel_id=1, source_target_pairs={{0,8},{8,16},{16,24},{24,32},{32,40},{40,48},{48,56},{56,64},{64,7... | collective-permute-start | bytes 9224 | tf_op jit(solution)/shard_map/ppermute | solution.py:16
  349.1 11.3 %collective-permute-start.67 = (f32[3,16,16,1]{3,1,0,2:T(8,128)S(1)}, f32[3,16,16,1]{3,1,0,2:T(8,128)S(1)}, u32[]{:S(2)}, u32[]{:S(2)}) collective-permute-start(f32[3,16,16,1]{3,1,0,2:T(8,128)S(1)} %get-tuple-element.119), channel_id=1, source_target_pairs={{8,0},{16,8},{24,16},{32,24},{40,32},{48,40},{56,48},{64,56},{72,6... | collective-permute-start | bytes 9224 | tf_op jit(solution)/shard_map/ppermute | solution.py:19
  354.4 9.0 %collective-permute-start.74 = (f32[3,16,256]{2,1,0:T(8,128)S(1)}, f32[3,16,256]{2,1,0:T(8,128)S(1)}, u32[]{:S(2)}, u32[]{:S(2)}) collective-permute-start(f32[3,16,256]{2,1,0:T(8,128)S(1)} %broadcast_select_fusion.9), channel_id=1, source_target_pairs={{0,32},{8,40},{16,48},{24,56},{32,64},{40,72},{48,80},{56,88},{64,... | collective-permute-start | bytes 147464 | tf_op jit(solution)/shard_map/ppermute | solution.py:38
  363.4 10.5 %collective-permute-start.75 = (f32[3,16,256]{2,1,0:T(8,128)S(1)}, f32[3,16,256]{2,1,0:T(8,128)S(1)}, u32[]{:S(2)}, u32[]{:S(2)}) collective-permute-start(f32[3,16,256]{2,1,0:T(8,128)S(1)} %broadcast_select_fusion.17), channel_id=1, source_target_pairs={{0,64},{8,72},{16,80},{24,88},{32,96},{40,104},{48,112},{56,120},{... | collective-permute-start | bytes 147464 | tf_op jit(solution)/shard_map/ppermute | solution.py:38
  395.0 13.7 %collective-permute-start.84 = (f32[3,16,256]{2,1,0:T(8,128)S(1)}, f32[3,16,256]{2,1,0:T(8,128)S(1)}, u32[]{:S(2)}, u32[]{:S(2)}) collective-permute-start(f32[3,16,256]{2,1,0:T(8,128)S(1)} %broadcast_select_fusion), channel_id=1, source_target_pairs={{0,16},{8,24},{16,32},{24,40},{32,48},{40,56},{48,64},{56,72},{64,... | collective-permute-start | bytes 147464 | tf_op jit(solution)/shard_map/ppermute | solution.py:38
  395.3 22.5 %collective-permute-start.79 = (f32[3,16,1,128]{3,1,0,2:T(8,128)S(1)}, f32[3,16,1,128]{3,1,0,2:T(8,128)S(1)}, u32[]{:S(2)}, u32[]{:S(2)}) collective-permute-start(f32[3,16,1,128]{3,1,0,2:T(8,128)S(1)} %get-tuple-element.108), channel_id=1, source_target_pairs={{0,1},{1,2},{2,3},{3,4},{4,5},{5,6},{6,7},{8,9},{9,10},{10,11},{11... | collective-permute-start | bytes 73736 | tf_op jit(solution)/shard_map/ppermute | solution.py:16
  397.2 20.6 %collective-permute-start.80 = (f32[3,16,1,128]{3,1,0,2:T(8,128)S(1)}, f32[3,16,1,128]{3,1,0,2:T(8,128)S(1)}, u32[]{:S(2)}, u32[]{:S(2)}) collective-permute-start(f32[3,16,1,128]{3,1,0,2:T(8,128)S(1)} %get-tuple-element.109), channel_id=1, source_target_pairs={{1,0},{2,1},{3,2},{4,3},{5,4},{6,5},{7,6},{9,8},{10,9},{11,10},{12... | collective-permute-start | bytes 73736 | tf_op jit(solution)/shard_map/ppermute | solution.py:19
  403.3 11.4 %collective-permute-start.77 = (f32[3,16,16,1]{3,1,0,2:T(8,128)S(1)}, f32[3,16,16,1]{3,1,0,2:T(8,128)S(1)}, u32[]{:S(2)}, u32[]{:S(2)}) collective-permute-start(f32[3,16,16,1]{3,1,0,2:T(8,128)S(1)} %get-tuple-element.111), channel_id=1, source_target_pairs={{0,8},{8,16},{16,24},{24,32},{32,40},{40,48},{48,56},{56,64},{64,7... | collective-permute-start | bytes 9224 | tf_op jit(solution)/shard_map/ppermute | solution.py:16
  403.4 11.3 %collective-permute-start.78 = (f32[3,16,16,1]{3,1,0,2:T(8,128)S(1)}, f32[3,16,16,1]{3,1,0,2:T(8,128)S(1)}, u32[]{:S(2)}, u32[]{:S(2)}) collective-permute-start(f32[3,16,16,1]{3,1,0,2:T(8,128)S(1)} %get-tuple-element.110), channel_id=1, source_target_pairs={{8,0},{16,8},{24,16},{32,24},{40,32},{48,40},{56,48},{64,56},{72,6... | collective-permute-start | bytes 9224 | tf_op jit(solution)/shard_map/ppermute | solution.py:19
  408.7 9.0 %collective-permute-start.85 = (f32[3,16,256]{2,1,0:T(8,128)S(1)}, f32[3,16,256]{2,1,0:T(8,128)S(1)}, u32[]{:S(2)}, u32[]{:S(2)}) collective-permute-start(f32[3,16,256]{2,1,0:T(8,128)S(1)} %broadcast_select_fusion.8), channel_id=1, source_target_pairs={{0,32},{8,40},{16,48},{24,56},{32,64},{40,72},{48,80},{56,88},{64,... | collective-permute-start | bytes 147464 | tf_op jit(solution)/shard_map/ppermute | solution.py:38
  417.7 10.5 %collective-permute-start.86 = (f32[3,16,256]{2,1,0:T(8,128)S(1)}, f32[3,16,256]{2,1,0:T(8,128)S(1)}, u32[]{:S(2)}, u32[]{:S(2)}) collective-permute-start(f32[3,16,256]{2,1,0:T(8,128)S(1)} %broadcast_select_fusion.16), channel_id=1, source_target_pairs={{0,64},{8,72},{16,80},{24,88},{32,96},{40,104},{48,112},{56,120},{... | collective-permute-start | bytes 147464 | tf_op jit(solution)/shard_map/ppermute | solution.py:38
  448.0 7.7 %collective-permute-start.91 = (f32[]{:T(128)}, f32[]{:T(128)}, u32[]{:S(2)}, u32[]{:S(2)}) collective-permute-start(f32[]{:T(128)} %add.469), channel_id=1, source_target_pairs={{0,64},{8,72},{16,80},{24,88},{32,96},{40,104},{48,112},{56,120},{... | collective-permute-start | bytes 20 | tf_op jit(solution)/shard_map/ppermute | solution.py:50
  (52 other events, 275.7 us)

commit v2 on v0

--- a/solution.py
+++ b/solution.py
@@ -19,6 +19,35 @@
         high = lax.ppermute(lax.slice_in_dim(block, 0, width, axis=dim), axis, backward)
         block = jnp.concatenate([low, block, high], axis=dim)
     return block
+
+
+def fold_row(row, fold_partner):
+    count = lax.axis_size("lon")
+    width = row.shape[-1]
+    here = lax.axis_index("lon")
+    offset = (fold_partner[0] + width * here) % (width * count)
+    turns = offset // width
+    shift = offset % width
+    flipped = row[..., ::-1]
+    slots = jnp.arange(count).reshape((count,) + (1,) * row.ndim)
+    wanted = (slots == (turns - here) % count) | (slots == (turns - here - 1) % count)
+    sent = jnp.where(wanted, flipped[None], 0.0)
+    got = lax.all_to_all(sent, "lon", 0, 0)
+    first = lax.dynamic_index_in_dim(got, (turns - here) % count, 0, keepdims=False)
+    second = lax.dynamic_index_in_dim(got, (turns - here - 1) % count, 0, keepdims=False)
+    pair = jnp.concatenate([first, second], axis=-1)
+    return lax.dynamic_slice_in_dim(pair, width - 1 - shift, width, axis=pair.ndim - 1)
+
+
+def tree_sum(value, axes):
+    count = 1
+    for axis in axes:
+        count *= lax.axis_size(axis)
+    got = lax.all_to_all(jnp.broadcast_to(value, (count,)), axes, 0, 0)
+    total = got[0]
+    for j in range(1, count):
+        total = total + got[j]
+    return total
 
 
 def upwind_pair(velocity, mixing, face_sea):
@@ -57,8 +86,7 @@
         vertical_vel[:-1], 0.5 * (diffusivity[:-1] + diffusivity[1:]), ocean[:-1] * ocean[1:]
     )
     top_static = jnp.stack([north_vel[:, -1, :], diffusivity[:, -1, :], ocean[:, -1, :]])
-    fold_all = lax.all_gather(top_static, "lon", axis=2, tiled=True)
-    across = jnp.take(fold_all, fold_partner, axis=2)
+    across = fold_row(top_static, fold_partner)
     north_top = (lax.axis_index("lat") == lax.axis_size("lat") - 1).astype(jnp.float32)
     fold_own, fold_next = upwind_pair(
         0.5 * (top_static[0] - across[0]),
@@ -71,8 +99,7 @@
         east_west = with_halo(quantity, (("lon", 3),), 1, True)
         south_north = with_halo(quantity, (("lat", 2),), 1, False)
         top_row = quantity[:, :, -1, :]
-        whole_top = lax.all_gather(top_row, "lon", axis=2, tiled=True)
-        partner_row = jnp.take(whole_top, fold_partner, axis=2)
+        partner_row = fold_row(top_row, fold_partner)
         return (east_west, south_north, partner_row)
 
     kept_states = [tracer_start]
@@ -137,7 +164,7 @@
         spread = 1.0 + current * current
         adjoint = weight - result - decay_rate / (spread * jnp.sqrt(spread)) * weight
         source_grad = source_grad + ocean * adjoint
-    squares = lax.psum(jnp.sum(source_grad * source_grad), ("lon", "lat"))
+    squares = tree_sum(jnp.sum(source_grad * source_grad), ("lon", "lat"))
     return (source_grad, jnp.sqrt(squares))
 
 

time: 701 us -> 526 us (0.75)
  blocking collectives: 422 us -> 21.5 us
  between operations: 3.37 us -> 162 us
  waiting for transfers between devices: 9.06 us -> 108 us
  local copies, waits for them, and re-layouts: 115 us -> 37.1 us
  starting transfers between devices: 106 us -> 152 us
    all_gather x8 -> x0, blocking collectives: 349 us -> none  [the longest x7 310 us: neighbours(): whole_top = lax.all_gather(top_row, 'lon', axis=2, tiled=True)]
    psum x1 -> x0, blocking collectives: 72.8 us -> none  [on_device(): squares = lax.psum(jnp.sum(source_grad * source_grad), ('lon', 'lat'))]
    ppermute x16, waiting for transfers between devices: 9.02 us -> 76.8 us  [with_halo(): lax.ppermute(lax.slice_in_dim(block, block.shape[dim] - width, None, axis...]
    all_gather x8 -> x0, local copies, waits for them, and re-layouts: 52.8 us -> none  [the longest x7 46.9 us: neighbours(): whole_top = lax.all_gather(top_row, 'lon', axis=2, tiled=True)]
    all_to_all x0 -> x8, starting transfers between devices: none -> 47.5 us  [fold_row(): got = lax.all_to_all(sent, 'lon', 0, 0)]
    gather x16 -> x0, local copies, waits for them, and re-layouts: 41.7 us -> none  [the longest x14 37.4 us: neighbours(): partner_row = jnp.take(whole_top, fold_partner, axis=2)]
    all_to_all x0 -> x1, blocking collectives: none -> 21.5 us  [tree_sum(): got = lax.all_to_all(jnp.broadcast_to(value, (count,)), axes, 0, 0)]
    all_to_all x0 -> x8, waiting for transfers between devices: none -> 19.1 us  [fold_row(): got = lax.all_to_all(sent, 'lon', 0, 0)]
  transfers between devices with their start and end apart: 32 -> 40, of which waited for: 2 -> 10; matrix products, arithmetic and copies ran while one was open for 18% -> 5% of each run, Pallas kernels for 0% -> 0%
where the time goes in v2:
time: 526 us; the launch traced here: 519 us
  between operations  162 us (31%)
  starting transfers between devices  152 us (29%)
  waiting for transfers between devices  108 us (21%)
  other arithmetic  38.9 us (7%)
  local copies, waits for them, and re-layouts  37.1 us (7%)
  blocking collectives  21.5 us (4%)
    ppermute x16, starting transfers between devices, with_halo(): lax.ppermute(lax.slice_in_dim(block, 0, width, axis=dim), axis, backward)  77.2 us
    ppermute x16, waiting for transfers between devices, with_halo(): lax.ppermute(lax.slice_in_dim(block, block.shape[dim] - width, None, axis...  76.8 us
    all_to_all x8, starting transfers between devices, fold_row(): got = lax.all_to_all(sent, 'lon', 0, 0)  47.5 us
    ppermute x16, starting transfers between devices, with_halo(): lax.ppermute(lax.slice_in_dim(block, block.shape[dim] - width, None, axis...  26.9 us
    all_to_all x1, blocking collectives, tree_sum(): got = lax.all_to_all(jnp.broadcast_to(value, (count,)), axes, 0, 0)  21.5 us
    all_to_all x8, waiting for transfers between devices, fold_row(): got = lax.all_to_all(sent, 'lon', 0, 0)  19.1 us
    ppermute x16, waiting for transfers between devices, with_halo(): lax.ppermute(lax.slice_in_dim(block, 0, width, axis=dim), axis, backward)  11.7 us
    unnamed x67, local copies, waits for them, and re-layouts  10.8 us
  transfers between devices with their start and end apart: 40, of which 10 were waited for; matrix products, arithmetic and copies ran while one was open for 5% of the time, Pallas kernels for 0%

profile of v2, /device:TPU:2, one launch (start us, length us, event | category | flops | bytes accessed | tf_op | source)
XLA Modules:
  0.0 519.2 jit_solution(12303746643406596813)
XLA Ops:
  0.6 1.1 copy.31
  2.4 3.5 collective-permute-start.6
  5.9 4.5 collective-permute-start.7
  12.3 1.3 broadcast_select_fusion.7
  13.6 10.7 %all-to-all-start = ((f32[32,3,16,128]{3,2,1,0:T(8,128)}), f32[32,3,16,128]{3,2,1,0:T(8,128)}, u32[]{:S(2)}, u32[]{:S(2)}) async-start(f32[32,3,16,128]{3,2,1,0:T(8,128)} %get-tuple-element.423), calls=%async_computation | async-start | bytes 1572864 | tf_op jit(solution)/shard_map/all_to_all | solution.py:35
  25.0 3.7 collective-permute-start.5
  28.7 0.9 fusion.118
  29.7 4.3 collective-permute-start.1
  34.1 1.0 fusion.125
  36.0 11.6 %collective-permute-done.1 = f32[4,16,16,1]{3,2,1,0:T(8,128)S(1)} collective-permute-done((f32[4,16,16,1]{3,2,1,0:T(8,128)}, f32[4,16,16,1]{3,2,1,0:T(8,128)S(1)}, u32[]{:S(2)}, u32[]{:S(2)}) %collective-permute-start.1) | collective-permute-done | bytes 4128 | tf_op jit(solution)/shard_map/ppermute | solution.py:19
  47.7 2.0 collective-permute-start.2
  49.6 3.6 collective-permute-done
  54.0 1.3 add_bitcast_fusion
  56.3 2.6 collective-permute-done.2
  58.9 1.9 collective-permute-start.4
  60.8 7.2 %all-to-all-start.1 = ((f32[32,3,16,128]{3,2,1,0:T(8,128)}), f32[32,3,16,128]{3,2,1,0:T(8,128)}, u32[]{:S(2)}, u32[]{:S(2)}) async-start(f32[32,3,16,128]{3,2,1,0:T(8,128)} %get-tuple-element.424), calls=%async_computation.1 | async-start | bytes 1572864 | tf_op jit(solution)/shard_map/all_to_all | solution.py:35
  68.1 2.3 fusion
  73.7 19.1 %all-to-all-done.1 = f32[32,3,16,128]{3,2,1,0:T(8,128)} async-done(((f32[32,3,16,128]{3,2,1,0:T(8,128)}), f32[32,3,16,128]{3,2,1,0:T(8,128)}, u32[]{:S(2)}, u32[]{:S(2)}) %all-to-all-start.1) | async-done | bytes 786464 | tf_op jit(solution)/shard_map/all_to_all | solution.py:35
  94.3 2.9 fusion.11
  97.9 1.0 broadcast_select_fusion.5
  98.9 4.6 all-to-all-start.2
  103.9 5.3 %collective-permute-start.9 = (f32[3,16,16,1]{3,1,0,2:T(8,128)S(1)}, f32[3,16,16,1]{3,1,0,2:T(8,128)S(1)}, u32[]{:S(2)}, u32[]{:S(2)}) collective-permute-start(f32[3,16,16,1]{3,1,0,2:T(8,128)S(1)} %get-tuple-element.153), channel_id=1, source_target_pairs={{8,0},{16,8},{24,16},{32,24},{40,32},{48,40},{56,48},{64,56},{72,6... | collective-permute-start | bytes 9224 | tf_op jit(solution)/shard_map/ppermute | solution.py:19
  110.0 2.9 collective-permute-start.10
  112.9 5.6 %collective-permute-start.11 = (f32[3,16,1,128]{3,1,0,2:T(8,128)S(1)}, f32[3,16,1,128]{3,1,0,2:T(8,128)S(1)}, u32[]{:S(2)}, u32[]{:S(2)}) collective-permute-start(f32[3,16,1,128]{3,1,0,2:T(8,128)S(1)} %get-tuple-element.156), channel_id=1, source_target_pairs={{1,0},{2,1},{3,2},{4,3},{5,4},{6,5},{7,6},{9,8},{10,9},{11,10},{12... | collective-permute-start | bytes 73736 | tf_op jit(solution)/shard_map/ppermute | solution.py:19
  118.5 12.5 %collective-permute-done.8 = f32[3,16,16,1]{3,1,0,2:T(8,128)S(1)} collective-permute-done((f32[3,16,16,1]{3,1,0,2:T(8,128)S(1)}, f32[3,16,16,1]{3,1,0,2:T(8,128)S(1)}, u32[]{:S(2)}, u32[]{:S(2)}) %collective-permute-start.8) | collective-permute-done | bytes 3104 | tf_op jit(solution)/shard_map/ppermute | solution.py:16
  131.0 1.2 fusion.1
  133.2 2.8 fusion.15
  136.1 1.0 broadcast_select_fusion.4
  137.1 5.0 all-to-all-start.3
  142.8 5.2 collective-permute-start.13
  148.7 2.9 collective-permute-start.14
  151.7 5.6 %collective-permute-start.15 = (f32[3,16,1,128]{3,1,0,2:T(8,128)S(1)}, f32[3,16,1,128]{3,1,0,2:T(8,128)S(1)}, u32[]{:S(2)}, u32[]{:S(2)}) collective-permute-start(f32[3,16,1,128]{3,1,0,2:T(8,128)S(1)} %get-tuple-element.151), channel_id=1, source_target_pairs={{1,0},{2,1},{3,2},{4,3},{5,4},{6,5},{7,6},{9,8},{10,9},{11,10},{12... | collective-permute-start | bytes 73736 | tf_op jit(solution)/shard_map/ppermute | solution.py:19
  157.3 12.3 %collective-permute-done.12 = f32[3,16,16,1]{3,1,0,2:T(8,128)S(1)} collective-permute-done((f32[3,16,16,1]{3,1,0,2:T(8,128)S(1)}, f32[3,16,16,1]{3,1,0,2:T(8,128)S(1)}, u32[]{:S(2)}, u32[]{:S(2)}) %collective-permute-start.12) | collective-permute-done | bytes 3104 | tf_op jit(solution)/shard_map/ppermute | solution.py:16
  169.6 1.2 fusion.2
  171.8 2.9 fusion.21
  175.3 1.0 broadcast_select_fusion.3
  176.3 5.0 all-to-all-start.4
  183.9 0.9 copy-done.14
  186.6 5.2 collective-permute-start.17
  192.6 2.9 collective-permute-start.18
  195.6 5.6 %collective-permute-start.19 = (f32[3,16,1,128]{3,1,0,2:T(8,128)S(1)}, f32[3,16,1,128]{3,1,0,2:T(8,128)S(1)}, u32[]{:S(2)}, u32[]{:S(2)}) collective-permute-start(f32[3,16,1,128]{3,1,0,2:T(8,128)S(1)} %copy-done.28), channel_id=1, source_target_pairs={{1,0},{2,1},{3,2},{4,3},{5,4},{6,5},{7,6},{9,8},{10,9},{11,10},{12... | collective-permute-start | bytes 73736 | tf_op jit(solution)/shard_map/ppermute | solution.py:19
  201.2 7.7 %collective-permute-done.16 = f32[3,16,16,1]{3,1,0,2:T(8,128)S(1)} collective-permute-done((f32[3,16,16,1]{3,1,0,2:T(8,128)S(1)}, f32[3,16,16,1]{3,1,0,2:T(8,128)S(1)}, u32[]{:S(2)}, u32[]{:S(2)}) %collective-permute-start.16) | collective-permute-done | bytes 3104 | tf_op jit(solution)/shard_map/ppermute | solution.py:16
  210.8 1.8 fusion.20
  213.5 1.0 broadcast_select_fusion.2
  214.5 4.9 all-to-all-start.5
  219.9 5.2 collective-permute-start.21
  225.8 3.1 collective-permute-start.22
  228.9 5.6 %collective-permute-start.23 = (f32[3,16,1,128]{3,2,1,0:T(1,128)S(1)}, f32[3,16,1,128]{3,2,1,0:T(1,128)S(1)}, u32[]{:S(2)}, u32[]{:S(2)}) collective-permute-start(f32[3,16,1,128]{3,2,1,0:T(1,128)S(1)} %slice.2033), channel_id=1, source_target_pairs={{1,0},{2,1},{3,2},{4,3},{5,4},{6,5},{7,6},{9,8},{10,9},{11,10},{12... | collective-permute-start | bytes 73736 | tf_op jit(solution)/shard_map/ppermute | solution.py:19
  234.6 12.3 %collective-permute-done.20 = f32[3,16,16,1]{3,1,0,2:T(8,128)S(1)} collective-permute-done((f32[3,16,16,1]{3,1,0,2:T(8,128)S(1)}, f32[3,16,16,1]{3,1,0,2:T(8,128)S(1)}, u32[]{:S(2)}, u32[]{:S(2)}) %collective-permute-start.20) | collective-permute-done | bytes 3104 | tf_op jit(solution)/shard_map/ppermute | solution.py:16
  250.6 1.3 fusion.58
  252.1 1.0 broadcast_select_fusion.1
  253.1 5.1 all-to-all-start.6
  258.8 5.3 %collective-permute-start.25 = (f32[3,16,16,1]{3,1,0,2:T(8,128)S(1)}, f32[3,16,16,1]{3,1,0,2:T(8,128)S(1)}, u32[]{:S(2)}, u32[]{:S(2)}) collective-permute-start(f32[3,16,16,1]{3,1,0,2:T(8,128)S(1)} %get-tuple-element.135), channel_id=1, source_target_pairs={{8,0},{16,8},{24,16},{32,24},{40,32},{48,40},{56,48},{64,56},{72,6... | collective-permute-start | bytes 9224 | tf_op jit(solution)/shard_map/ppermute | solution.py:19
  264.1 2.9 collective-permute-start.26
  267.1 5.6 %collective-permute-start.27 = (f32[3,16,1,128]{3,1,0,2:T(8,128)S(1)}, f32[3,16,1,128]{3,1,0,2:T(8,128)S(1)}, u32[]{:S(2)}, u32[]{:S(2)}) collective-permute-start(f32[3,16,1,128]{3,1,0,2:T(8,128)S(1)} %get-tuple-element.134), channel_id=1, source_target_pairs={{1,0},{2,1},{3,2},{4,3},{5,4},{6,5},{7,6},{9,8},{10,9},{11,10},{12... | collective-permute-start | bytes 73736 | tf_op jit(solution)/shard_map/ppermute | solution.py:19
  272.7 13.1 %collective-permute-done.24 = f32[3,16,16,1]{3,1,0,2:T(8,128)S(1)} collective-permute-done((f32[3,16,16,1]{3,1,0,2:T(8,128)S(1)}, f32[3,16,16,1]{3,1,0,2:T(8,128)S(1)}, u32[]{:S(2)}, u32[]{:S(2)}) %collective-permute-start.24) | collective-permute-done | bytes 3104 | tf_op jit(solution)/shard_map/ppermute | solution.py:16
  288.4 1.0 broadcast_select_fusion
  289.4 5.0 all-to-all-start.7
  294.9 5.2 collective-permute-start.29
  300.8 2.9 collective-permute-start.30
  303.8 5.6 %collective-permute-start.31 = (f32[3,16,1,128]{3,1,0,2:T(8,128)S(1)}, f32[3,16,1,128]{3,1,0,2:T(8,128)S(1)}, u32[]{:S(2)}, u32[]{:S(2)}) collective-permute-start(f32[3,16,1,128]{3,1,0,2:T(8,128)S(1)} %get-tuple-element.125), channel_id=1, source_target_pairs={{1,0},{2,1},{3,2},{4,3},{5,4},{6,5},{7,6},{9,8},{10,9},{11,10},{12... | collective-permute-start | bytes 73736 | tf_op jit(solution)/shard_map/ppermute | solution.py:19
  309.4 12.5 %collective-permute-done.28 = f32[3,16,16,1]{3,1,0,2:T(8,128)S(1)} collective-permute-done((f32[3,16,16,1]{3,1,0,2:T(8,128)S(1)}, f32[3,16,16,1]{3,1,0,2:T(8,128)S(1)}, u32[]{:S(2)}, u32[]{:S(2)}) %collective-permute-start.28) | collective-permute-done | bytes 3104 | tf_op jit(solution)/shard_map/ppermute | solution.py:16
  324.2 2.8 multiply_reduce_fusion
  327.7 21.5 %all_to_all.46 = f32[256,1,1]{2,1,0:T(1,128)S(1)} all-to-all(f32[256,1,1]{2,1,0:T(1,128)S(1)} %broadcast_in_dim.173), channel_id=1, replica_groups=mesh['lon'=32,'lat'=8] {'lon','lat'}, dimensions={0} | all-to-all | bytes 2048 | tf_op jit(solution)/shard_map/all_to_all | solution.py:46
  (215 shorter events, 46.1 us)
Async XLA Ops:
  1.8 9.4 %copy-start.20 = (s32[16,16,128]{2,1,0:T(8,128)S(1)}, s32[16,16,128]{2,1,0:T(8,128)}, u32[]{:S(2)}) copy-start(s32[16,16,128]{2,1,0:T(8,128)} %param.31) | copy-start | bytes 393220
  2.4 69.5 %collective-permute-start.6 = (f32[3,16,1,128]{3,1,0,2:T(8,128)}, f32[3,16,1,128]{3,1,0,2:T(8,128)}, u32[]{:S(2)}, u32[]{:S(2)}) collective-permute-start(f32[3,16,1,128]{3,1,0,2:T(8,128)} %get-tuple-element.162), channel_id=1, source_target_pairs={{0,1},{1,2},{2,3},{3,4},{4,5},{5,6},{6,7},{8,9},{9,10},{10,11},{11... | collective-permute-start | bytes 73736 | tf_op jit(solution)/shard_map/ppermute | solution.py:16
  5.9 66.1 %collective-permute-start.7 = (f32[3,16,1,128]{3,1,0,2:T(8,128)}, f32[3,16,1,128]{3,1,0,2:T(8,128)}, u32[]{:S(2)}, u32[]{:S(2)}) collective-permute-start(f32[3,16,1,128]{3,1,0,2:T(8,128)} %get-tuple-element.161), channel_id=1, source_target_pairs={{1,0},{2,1},{3,2},{4,3},{5,4},{6,5},{7,6},{9,8},{10,9},{11,10},{12... | collective-permute-start | bytes 73736 | tf_op jit(solution)/shard_map/ppermute | solution.py:19
  11.1 0.9 copy-start.1
  11.1 1.0 copy-start.2
  12.3 1.3 copy-start.25
  13.6 10.7 %copy-start.6 = (f32[16,16,128]{2,1,0:T(8,128)S(1)}, f32[16,16,128]{2,1,0:T(8,128)}, u32[]{:S(2)}) copy-start(f32[16,16,128]{2,1,0:T(8,128)} %param.27) | copy-start | bytes 393220
  13.6 47.2 %all-to-all-start = ((f32[32,3,16,128]{3,2,1,0:T(8,128)}), f32[32,3,16,128]{3,2,1,0:T(8,128)}, u32[]{:S(2)}, u32[]{:S(2)}) async-start(f32[32,3,16,128]{3,2,1,0:T(8,128)} %get-tuple-element.423), calls=%async_computation | async-start | bytes 1572864 | tf_op jit(solution)/shard_map/all_to_all | solution.py:35
  25.0 45.4 %collective-permute-start.5 = (f32[4,16,1,128]{3,2,1,0:T(1,128)}, f32[4,16,1,128]{3,2,1,0:T(1,128)}, u32[]{:S(2)}, u32[]{:S(2)}) collective-permute-start(f32[4,16,1,128]{3,2,1,0:T(1,128)} %get-tuple-element.122), channel_id=1, source_target_pairs={{1,0},{2,1},{3,2},{4,3},{5,4},{6,5},{7,6},{9,8},{10,9},{11,10},{12... | collective-permute-start | bytes 98312 | tf_op jit(solution)/shard_map/ppermute | solution.py:19
  28.7 5.2 %copy-start.21 = (f32[16,16,128]{2,1,0:T(8,128)S(1)}, f32[16,16,128]{2,1,0:T(8,128)}, u32[]{:S(2)}) copy-start(f32[16,16,128]{2,1,0:T(8,128)} %param.29) | copy-start | bytes 393220
  29.7 18.0 %collective-permute-start.1 = (f32[4,16,16,1]{3,2,1,0:T(8,128)}, f32[4,16,16,1]{3,2,1,0:T(8,128)S(1)}, u32[]{:S(2)}, u32[]{:S(2)}) collective-permute-start(f32[4,16,16,1]{3,2,1,0:T(8,128)} %get-tuple-element.120), channel_id=1, source_target_pairs={{8,0},{16,8},{24,16},{32,24},{40,32},{48,40},{56,48},{64,56},{72,6... | collective-permute-start | bytes 12296 | tf_op jit(solution)/shard_map/ppermute | solution.py:19
  33.9 19.3 %collective-permute-start = (f32[4,16,16,1]{3,2,1,0:T(8,128)S(1)}, f32[4,16,16,1]{3,2,1,0:T(8,128)S(1)}, u32[]{:S(2)}, u32[]{:S(2)}) collective-permute-start(f32[4,16,16,1]{3,2,1,0:T(8,128)S(1)} %get-tuple-element.119), channel_id=1, source_target_pairs={{0,8},{8,16},{16,24},{24,32},{32,40},{40,48},{48,56},{56,64},{64,7... | collective-permute-start | bytes 12296 | tf_op jit(solution)/shard_map/ppermute | solution.py:16
  47.7 11.2 %collective-permute-start.2 = (f32[3,16,16,1]{3,1,0,2:T(8,128)}, f32[3,16,16,1]{3,1,0,2:T(8,128)}, u32[]{:S(2)}, u32[]{:S(2)}) collective-permute-start(f32[3,16,16,1]{3,1,0,2:T(8,128)} %get-tuple-element.159), channel_id=1, source_target_pairs={{0,8},{8,16},{16,24},{24,32},{32,40},{40,48},{48,56},{56,64},{64,7... | collective-permute-start | bytes 9224 | tf_op jit(solution)/shard_map/ppermute | solution.py:16
  54.0 14.0 %collective-permute-start.3 = (f32[3,16,16,1]{3,1,0,2:T(8,128)}, f32[3,16,16,1]{3,1,0,2:T(8,128)}, u32[]{:S(2)}, u32[]{:S(2)}) collective-permute-start(f32[3,16,16,1]{3,1,0,2:T(8,128)} %get-tuple-element.158), channel_id=1, source_target_pairs={{8,0},{16,8},{24,16},{32,24},{40,32},{48,40},{56,48},{64,56},{72,6... | collective-permute-start | bytes 9224 | tf_op jit(solution)/shard_map/ppermute | solution.py:19
  56.1 2.8 copy-start.24
  58.9 11.4 %collective-permute-start.4 = (f32[4,16,1,128]{3,2,1,0:T(1,128)S(1)}, f32[4,16,1,128]{3,2,1,0:T(1,128)S(1)}, u32[]{:S(2)}, u32[]{:S(2)}) collective-permute-start(f32[4,16,1,128]{3,2,1,0:T(1,128)S(1)} %copy-done.24), channel_id=1, source_target_pairs={{0,1},{1,2},{2,3},{3,4},{4,5},{5,6},{6,7},{8,9},{9,10},{10,11},{11... | collective-permute-start | bytes 98312 | tf_op jit(solution)/shard_map/ppermute | solution.py:16
  60.8 32.0 %all-to-all-start.1 = ((f32[32,3,16,128]{3,2,1,0:T(8,128)}), f32[32,3,16,128]{3,2,1,0:T(8,128)}, u32[]{:S(2)}, u32[]{:S(2)}) async-start(f32[32,3,16,128]{3,2,1,0:T(8,128)} %get-tuple-element.424), calls=%async_computation.1 | async-start | bytes 1572864 | tf_op jit(solution)/shard_map/all_to_all | solution.py:35
  72.8 20.9 %copy-start = (f32[3,16,16,128]{3,2,1,0:T(8,128)S(1)}, f32[3,16,16,128]{3,2,1,0:T(8,128)}, u32[]{:S(2)}) copy-start(f32[3,16,16,128]{3,2,1,0:T(8,128)} %param.25) | copy-start | bytes 1179652
  98.9 33.4 %all-to-all-start.2 = ((f32[32,3,16,128]{3,2,1,0:T(8,128)}), f32[32,3,16,128]{3,2,1,0:T(8,128)}, u32[]{:S(2)}, u32[]{:S(2)}) async-start(f32[32,3,16,128]{3,2,1,0:T(8,128)} %broadcast_select_fusion.5), calls=%async_computation.2 | async-start | bytes 1572864 | tf_op jit(solution)/shard_map/all_to_all | solution.py:35
  103.7 27.3 %collective-permute-start.8 = (f32[3,16,16,1]{3,1,0,2:T(8,128)S(1)}, f32[3,16,16,1]{3,1,0,2:T(8,128)S(1)}, u32[]{:S(2)}, u32[]{:S(2)}) collective-permute-start(f32[3,16,16,1]{3,1,0,2:T(8,128)S(1)} %get-tuple-element.154), channel_id=1, source_target_pairs={{0,8},{8,16},{16,24},{24,32},{32,40},{40,48},{48,56},{56,64},{64,7... | collective-permute-start | bytes 9224 | tf_op jit(solution)/shard_map/ppermute | solution.py:16
  103.9 27.2 %collective-permute-start.9 = (f32[3,16,16,1]{3,1,0,2:T(8,128)S(1)}, f32[3,16,16,1]{3,1,0,2:T(8,128)S(1)}, u32[]{:S(2)}, u32[]{:S(2)}) collective-permute-start(f32[3,16,16,1]{3,1,0,2:T(8,128)S(1)} %get-tuple-element.153), channel_id=1, source_target_pairs={{8,0},{16,8},{24,16},{32,24},{40,32},{48,40},{56,48},{64,56},{72,6... | collective-permute-start | bytes 9224 | tf_op jit(solution)/shard_map/ppermute | solution.py:19
  110.0 22.3 %collective-permute-start.10 = (f32[3,16,1,128]{3,1,0,2:T(8,128)S(1)}, f32[3,16,1,128]{3,1,0,2:T(8,128)S(1)}, u32[]{:S(2)}, u32[]{:S(2)}) collective-permute-start(f32[3,16,1,128]{3,1,0,2:T(8,128)S(1)} %get-tuple-element.157), channel_id=1, source_target_pairs={{0,1},{1,2},{2,3},{3,4},{4,5},{5,6},{6,7},{8,9},{9,10},{10,11},{11... | collective-permute-start | bytes 73736 | tf_op jit(solution)/shard_map/ppermute | solution.py:16
  112.9 19.3 %collective-permute-start.11 = (f32[3,16,1,128]{3,1,0,2:T(8,128)S(1)}, f32[3,16,1,128]{3,1,0,2:T(8,128)S(1)}, u32[]{:S(2)}, u32[]{:S(2)}) collective-permute-start(f32[3,16,1,128]{3,1,0,2:T(8,128)S(1)} %get-tuple-element.156), channel_id=1, source_target_pairs={{1,0},{2,1},{3,2},{4,3},{5,4},{6,5},{7,6},{9,8},{10,9},{11,10},{12... | collective-permute-start | bytes 73736 | tf_op jit(solution)/shard_map/ppermute | solution.py:19
  137.1 33.8 %all-to-all-start.3 = ((f32[32,3,16,128]{3,2,1,0:T(8,128)}), f32[32,3,16,128]{3,2,1,0:T(8,128)}, u32[]{:S(2)}, u32[]{:S(2)}) async-start(f32[32,3,16,128]{3,2,1,0:T(8,128)} %broadcast_select_fusion.4), calls=%async_computation.3 | async-start | bytes 1572864 | tf_op jit(solution)/shard_map/all_to_all | solution.py:35
  142.3 27.3 %collective-permute-start.12 = (f32[3,16,16,1]{3,1,0,2:T(8,128)S(1)}, f32[3,16,16,1]{3,1,0,2:T(8,128)S(1)}, u32[]{:S(2)}, u32[]{:S(2)}) collective-permute-start(f32[3,16,16,1]{3,1,0,2:T(8,128)S(1)} %get-tuple-element.149), channel_id=1, source_target_pairs={{0,8},{8,16},{16,24},{24,32},{32,40},{40,48},{48,56},{56,64},{64,7... | collective-permute-start | bytes 9224 | tf_op jit(solution)/shard_map/ppermute | solution.py:16
  142.8 26.9 %collective-permute-start.13 = (f32[3,16,16,1]{3,1,0,2:T(8,128)S(1)}, f32[3,16,16,1]{3,1,0,2:T(8,128)S(1)}, u32[]{:S(2)}, u32[]{:S(2)}) collective-permute-start(f32[3,16,16,1]{3,1,0,2:T(8,128)S(1)} %get-tuple-element.148), channel_id=1, source_target_pairs={{8,0},{16,8},{24,16},{32,24},{40,32},{48,40},{56,48},{64,56},{72,6... | collective-permute-start | bytes 9224 | tf_op jit(solution)/shard_map/ppermute | solution.py:19
  148.7 22.1 %collective-permute-start.14 = (f32[3,16,1,128]{3,1,0,2:T(8,128)S(1)}, f32[3,16,1,128]{3,1,0,2:T(8,128)S(1)}, u32[]{:S(2)}, u32[]{:S(2)}) collective-permute-start(f32[3,16,1,128]{3,1,0,2:T(8,128)S(1)} %get-tuple-element.152), channel_id=1, source_target_pairs={{0,1},{1,2},{2,3},{3,4},{4,5},{5,6},{6,7},{8,9},{9,10},{10,11},{11... | collective-permute-start | bytes 73736 | tf_op jit(solution)/shard_map/ppermute | solution.py:16
  151.7 19.2 %collective-permute-start.15 = (f32[3,16,1,128]{3,1,0,2:T(8,128)S(1)}, f32[3,16,1,128]{3,1,0,2:T(8,128)S(1)}, u32[]{:S(2)}, u32[]{:S(2)}) collective-permute-start(f32[3,16,1,128]{3,1,0,2:T(8,128)S(1)} %get-tuple-element.151), channel_id=1, source_target_pairs={{1,0},{2,1},{3,2},{4,3},{5,4},{6,5},{7,6},{9,8},{10,9},{11,10},{12... | collective-permute-start | bytes 73736 | tf_op jit(solution)/shard_map/ppermute | solution.py:19
  176.3 33.0 %all-to-all-start.4 = ((f32[32,3,16,128]{3,2,1,0:T(8,128)}), f32[32,3,16,128]{3,2,1,0:T(8,128)}, u32[]{:S(2)}, u32[]{:S(2)}) async-start(f32[32,3,16,128]{3,2,1,0:T(8,128)} %broadcast_select_fusion.3), calls=%async_computation.4 | async-start | bytes 1572864 | tf_op jit(solution)/shard_map/all_to_all | solution.py:35
  181.3 0.9 slice-start
  182.9 1.0 copy-start.12
  183.9 0.9 copy-start.14
  186.4 22.6 %collective-permute-start.16 = (f32[3,16,16,1]{3,1,0,2:T(8,128)S(1)}, f32[3,16,16,1]{3,1,0,2:T(8,128)S(1)}, u32[]{:S(2)}, u32[]{:S(2)}) collective-permute-start(f32[3,16,16,1]{3,1,0,2:T(8,128)S(1)} %get-tuple-element.144), channel_id=1, source_target_pairs={{0,8},{8,16},{16,24},{24,32},{32,40},{40,48},{48,56},{56,64},{64,7... | collective-permute-start | bytes 9224 | tf_op jit(solution)/shard_map/ppermute | solution.py:16
  186.6 6.0 %copy-start.29 = (f32[3,16,1,128]{3,1,0,2:T(8,128)S(1)}, f32[3,16,1,128]{3,1,0,2:T(8,128)}, u32[]{:S(2)}) copy-start(f32[3,16,1,128]{3,1,0,2:T(8,128)} %get-tuple-element.147) | copy-start | bytes 73732
  186.6 8.9 %copy-start.28 = (f32[3,16,1,128]{3,1,0,2:T(8,128)S(1)}, f32[3,16,1,128]{3,1,0,2:T(8,128)}, u32[]{:S(2)}) copy-start(f32[3,16,1,128]{3,1,0,2:T(8,128)} %get-tuple-element.146) | copy-start | bytes 73732
  186.6 22.3 %collective-permute-start.17 = (f32[3,16,16,1]{3,1,0,2:T(8,128)S(1)}, f32[3,16,16,1]{3,1,0,2:T(8,128)S(1)}, u32[]{:S(2)}, u32[]{:S(2)}) collective-permute-start(f32[3,16,16,1]{3,1,0,2:T(8,128)S(1)} %get-tuple-element.143), channel_id=1, source_target_pairs={{8,0},{16,8},{24,16},{32,24},{40,32},{48,40},{56,48},{64,56},{72,6... | collective-permute-start | bytes 9224 | tf_op jit(solution)/shard_map/ppermute | solution.py:19
  192.6 16.6 %collective-permute-start.18 = (f32[3,16,1,128]{3,1,0,2:T(8,128)S(1)}, f32[3,16,1,128]{3,1,0,2:T(8,128)S(1)}, u32[]{:S(2)}, u32[]{:S(2)}) collective-permute-start(f32[3,16,1,128]{3,1,0,2:T(8,128)S(1)} %copy-done.29), channel_id=1, source_target_pairs={{0,1},{1,2},{2,3},{3,4},{4,5},{5,6},{6,7},{8,9},{9,10},{10,11},{11... | collective-permute-start | bytes 73736 | tf_op jit(solution)/shard_map/ppermute | solution.py:16
  195.6 13.7 %collective-permute-start.19 = (f32[3,16,1,128]{3,1,0,2:T(8,128)S(1)}, f32[3,16,1,128]{3,1,0,2:T(8,128)S(1)}, u32[]{:S(2)}, u32[]{:S(2)}) collective-permute-start(f32[3,16,1,128]{3,1,0,2:T(8,128)S(1)} %copy-done.28), channel_id=1, source_target_pairs={{1,0},{2,1},{3,2},{4,3},{5,4},{6,5},{7,6},{9,8},{10,9},{11,10},{12... | collective-permute-start | bytes 73736 | tf_op jit(solution)/shard_map/ppermute | solution.py:19
  214.5 35.1 %all-to-all-start.5 = ((f32[32,3,16,128]{3,2,1,0:T(8,128)}), f32[32,3,16,128]{3,2,1,0:T(8,128)}, u32[]{:S(2)}, u32[]{:S(2)}) async-start(f32[32,3,16,128]{3,2,1,0:T(8,128)} %broadcast_select_fusion.2), calls=%async_computation.5 | async-start | bytes 1572864 | tf_op jit(solution)/shard_map/all_to_all | solution.py:35
  219.6 27.3 %collective-permute-start.20 = (f32[3,16,16,1]{3,1,0,2:T(8,128)S(1)}, f32[3,16,16,1]{3,1,0,2:T(8,128)S(1)}, u32[]{:S(2)}, u32[]{:S(2)}) collective-permute-start(f32[3,16,16,1]{3,1,0,2:T(8,128)S(1)} %get-tuple-element.142), channel_id=1, source_target_pairs={{0,8},{8,16},{16,24},{24,32},{32,40},{40,48},{48,56},{56,64},{64,7... | collective-permute-start | bytes 9224 | tf_op jit(solution)/shard_map/ppermute | solution.py:16
  219.9 27.0 %collective-permute-start.21 = (f32[3,16,16,1]{3,1,0,2:T(8,128)S(1)}, f32[3,16,16,1]{3,1,0,2:T(8,128)S(1)}, u32[]{:S(2)}, u32[]{:S(2)}) collective-permute-start(f32[3,16,16,1]{3,1,0,2:T(8,128)S(1)} %get-tuple-element.141), channel_id=1, source_target_pairs={{8,0},{16,8},{24,16},{32,24},{40,32},{48,40},{56,48},{64,56},{72,6... | collective-permute-start | bytes 9224 | tf_op jit(solution)/shard_map/ppermute | solution.py:19
  225.8 21.4 %copy-start.4 = (f32[16,16,128]{2,0,1:T(8,128)S(1)}, f32[16,16,128]{2,0,1:T(8,128)}, u32[]{:S(2)}) copy-start(f32[16,16,128]{2,0,1:T(8,128)} %copy.53) | copy-start | bytes 393220
  225.8 21.4 %copy-start.5 = (f32[16,16,128]{2,0,1:T(8,128)S(1)}, f32[16,16,128]{2,0,1:T(8,128)}, u32[]{:S(2)}) copy-start(f32[16,16,128]{2,0,1:T(8,128)} %copy.48) | copy-start | bytes 393220
  225.8 21.5 %collective-permute-start.22 = (f32[3,16,1,128]{3,1,0,2:T(8,128)S(1)}, f32[3,16,1,128]{3,1,0,2:T(8,128)S(1)}, u32[]{:S(2)}, u32[]{:S(2)}) collective-permute-start(f32[3,16,1,128]{3,1,0,2:T(8,128)S(1)} %get-tuple-element.140), channel_id=1, source_target_pairs={{0,1},{1,2},{2,3},{3,4},{4,5},{5,6},{6,7},{8,9},{9,10},{10,11},{11... | collective-permute-start | bytes 73736 | tf_op jit(solution)/shard_map/ppermute | solution.py:16
  228.9 18.5 %collective-permute-start.23 = (f32[3,16,1,128]{3,2,1,0:T(1,128)S(1)}, f32[3,16,1,128]{3,2,1,0:T(1,128)S(1)}, u32[]{:S(2)}, u32[]{:S(2)}) collective-permute-start(f32[3,16,1,128]{3,2,1,0:T(1,128)S(1)} %slice.2033), channel_id=1, source_target_pairs={{1,0},{2,1},{3,2},{4,3},{5,4},{6,5},{7,6},{9,8},{10,9},{11,10},{12... | collective-permute-start | bytes 73736 | tf_op jit(solution)/shard_map/ppermute | solution.py:19
  247.5 0.9 copy-start.3
  248.4 0.9 copy-start.17
  249.3 1.3 copy-start.9
  253.1 5.1 copy-start.18
  253.1 33.3 %all-to-all-start.6 = ((f32[32,3,16,128]{3,2,1,0:T(8,128)}), f32[32,3,16,128]{3,2,1,0:T(8,128)}, u32[]{:S(2)}, u32[]{:S(2)}) async-start(f32[32,3,16,128]{3,2,1,0:T(8,128)} %broadcast_select_fusion.1), calls=%async_computation.6 | async-start | bytes 1572864 | tf_op jit(solution)/shard_map/all_to_all | solution.py:35
  258.3 27.8 %copy-start.15 = (f32[16,16,128]{2,0,1:T(8,128)}, f32[16,16,128]{2,0,1:T(8,128)S(1)}, u32[]{:S(2)}) copy-start(f32[16,16,128]{2,0,1:T(8,128)S(1)} %copy.58) | copy-start | bytes 393220
  258.5 27.3 %collective-permute-start.24 = (f32[3,16,16,1]{3,1,0,2:T(8,128)S(1)}, f32[3,16,16,1]{3,1,0,2:T(8,128)S(1)}, u32[]{:S(2)}, u32[]{:S(2)}) collective-permute-start(f32[3,16,16,1]{3,1,0,2:T(8,128)S(1)} %get-tuple-element.136), channel_id=1, source_target_pairs={{0,8},{8,16},{16,24},{24,32},{32,40},{40,48},{48,56},{56,64},{64,7... | collective-permute-start | bytes 9224 | tf_op jit(solution)/shard_map/ppermute | solution.py:16
  258.8 27.0 %collective-permute-start.25 = (f32[3,16,16,1]{3,1,0,2:T(8,128)S(1)}, f32[3,16,16,1]{3,1,0,2:T(8,128)S(1)}, u32[]{:S(2)}, u32[]{:S(2)}) collective-permute-start(f32[3,16,16,1]{3,1,0,2:T(8,128)S(1)} %get-tuple-element.135), channel_id=1, source_target_pairs={{8,0},{16,8},{24,16},{32,24},{40,32},{48,40},{56,48},{64,56},{72,6... | collective-permute-start | bytes 9224 | tf_op jit(solution)/shard_map/ppermute | solution.py:19
  264.1 21.9 %collective-permute-start.26 = (f32[3,16,1,128]{3,1,0,2:T(8,128)S(1)}, f32[3,16,1,128]{3,1,0,2:T(8,128)S(1)}, u32[]{:S(2)}, u32[]{:S(2)}) collective-permute-start(f32[3,16,1,128]{3,1,0,2:T(8,128)S(1)} %get-tuple-element.133), channel_id=1, source_target_pairs={{0,1},{1,2},{2,3},{3,4},{4,5},{5,6},{6,7},{8,9},{9,10},{10,11},{11... | collective-permute-start | bytes 73736 | tf_op jit(solution)/shard_map/ppermute | solution.py:16
  267.1 19.0 %collective-permute-start.27 = (f32[3,16,1,128]{3,1,0,2:T(8,128)S(1)}, f32[3,16,1,128]{3,1,0,2:T(8,128)S(1)}, u32[]{:S(2)}, u32[]{:S(2)}) collective-permute-start(f32[3,16,1,128]{3,1,0,2:T(8,128)S(1)} %get-tuple-element.134), channel_id=1, source_target_pairs={{1,0},{2,1},{3,2},{4,3},{5,4},{6,5},{7,6},{9,8},{10,9},{11,10},{12... | collective-permute-start | bytes 73736 | tf_op jit(solution)/shard_map/ppermute | solution.py:19
  286.1 1.1 copy-start.8
  289.4 34.0 %all-to-all-start.7 = ((f32[32,3,16,128]{3,2,1,0:T(8,128)}), f32[32,3,16,128]{3,2,1,0:T(8,128)}, u32[]{:S(2)}, u32[]{:S(2)}) async-start(f32[32,3,16,128]{3,2,1,0:T(8,128)} %broadcast_select_fusion), calls=%async_computation.7 | async-start | bytes 1572864 | tf_op jit(solution)/shard_map/all_to_all | solution.py:35
  294.6 27.3 %collective-permute-start.28 = (f32[3,16,16,1]{3,1,0,2:T(8,128)S(1)}, f32[3,16,16,1]{3,1,0,2:T(8,128)S(1)}, u32[]{:S(2)}, u32[]{:S(2)}) collective-permute-start(f32[3,16,16,1]{3,1,0,2:T(8,128)S(1)} %get-tuple-element.127), channel_id=1, source_target_pairs={{0,8},{8,16},{16,24},{24,32},{32,40},{40,48},{48,56},{56,64},{64,7... | collective-permute-start | bytes 9224 | tf_op jit(solution)/shard_map/ppermute | solution.py:16
  294.9 6.0 %copy-start.30 = (f32[3,16,1,128]{3,1,0,2:T(8,128)S(1)}, f32[3,16,1,128]{3,1,0,2:T(8,128)}, u32[]{:S(2)}) copy-start(f32[3,16,1,128]{3,1,0,2:T(8,128)} %get-tuple-element.124) | copy-start | bytes 73732
  294.9 27.0 %collective-permute-start.29 = (f32[3,16,16,1]{3,1,0,2:T(8,128)S(1)}, f32[3,16,16,1]{3,1,0,2:T(8,128)S(1)}, u32[]{:S(2)}, u32[]{:S(2)}) collective-permute-start(f32[3,16,16,1]{3,1,0,2:T(8,128)S(1)} %get-tuple-element.126), channel_id=1, source_target_pairs={{8,0},{16,8},{24,16},{32,24},{40,32},{48,40},{56,48},{64,56},{72,6... | collective-permute-start | bytes 9224 | tf_op jit(solution)/shard_map/ppermute | solution.py:19
  300.8 21.4 %collective-permute-start.30 = (f32[3,16,1,128]{3,1,0,2:T(8,128)S(1)}, f32[3,16,1,128]{3,1,0,2:T(8,128)S(1)}, u32[]{:S(2)}, u32[]{:S(2)}) collective-permute-start(f32[3,16,1,128]{3,1,0,2:T(8,128)S(1)} %copy-done.30), channel_id=1, source_target_pairs={{0,1},{1,2},{2,3},{3,4},{4,5},{5,6},{6,7},{8,9},{9,10},{10,11},{11... | collective-permute-start | bytes 73736 | tf_op jit(solution)/shard_map/ppermute | solution.py:16
  303.8 18.4 %collective-permute-start.31 = (f32[3,16,1,128]{3,1,0,2:T(8,128)S(1)}, f32[3,16,1,128]{3,1,0,2:T(8,128)S(1)}, u32[]{:S(2)}, u32[]{:S(2)}) collective-permute-start(f32[3,16,1,128]{3,1,0,2:T(8,128)S(1)} %get-tuple-element.125), channel_id=1, source_target_pairs={{1,0},{2,1},{3,2},{4,3},{5,4},{6,5},{7,6},{9,8},{10,9},{11,10},{12... | collective-permute-start | bytes 73736 | tf_op jit(solution)/shard_map/ppermute | solution.py:19
  322.2 0.9 copy-start.16
  323.1 1.1 copy-start.10
  (9 other events, 6.3 us)

commit v3 on v2

--- a/solution.py
+++ b/solution.py
@@ -44,10 +44,7 @@
     for axis in axes:
         count *= lax.axis_size(axis)
     got = lax.all_to_all(jnp.broadcast_to(value, (count,)), axes, 0, 0)
-    total = got[0]
-    for j in range(1, count):
-        total = total + got[j]
-    return total
+    return jnp.sum(got)
 
 
 def upwind_pair(velocity, mixing, face_sea):

time: 526 us -> 356 us (0.68)
  between operations: 162 us -> 3.54 us
  local copies, waits for them, and re-layouts: 37.1 us -> 27.2 us
    slice x14 -> x0, local copies, waits for them, and re-layouts: 9.27 us -> none  [tree_sum(): total = total + got[j]]
    unnamed x67 -> x63, local copies, waits for them, and re-layouts: 10.8 us -> 10.8 us
  transfers between devices with their start and end apart: 40 -> 40, of which waited for: 10 -> 10; matrix products, arithmetic and copies ran while one was open for 5% -> 7% of each run, Pallas kernels for 0% -> 0%
where the time goes in v3:
time: 356 us; the launch traced here: 351 us
  starting transfers between devices  152 us (43%)
  waiting for transfers between devices  108 us (30%)
  other arithmetic  39.8 us (11%)
  local copies, waits for them, and re-layouts  27.2 us (8%)
  blocking collectives  21.5 us (6%)
    ppermute x16, starting transfers between devices, with_halo(): lax.ppermute(lax.slice_in_dim(block, 0, width, axis=dim), axis, backward)  77.2 us
    ppermute x16, waiting for transfers between devices, with_halo(): lax.ppermute(lax.slice_in_dim(block, block.shape[dim] - width, None, axis...  76.8 us
    all_to_all x8, starting transfers between devices, fold_row(): got = lax.all_to_all(sent, 'lon', 0, 0)  47.5 us
    ppermute x16, starting transfers between devices, with_halo(): lax.ppermute(lax.slice_in_dim(block, block.shape[dim] - width, None, axis...  26.9 us
    all_to_all x1, blocking collectives, tree_sum(): got = lax.all_to_all(jnp.broadcast_to(value, (count,)), axes, 0, 0)  21.5 us
    all_to_all x8, waiting for transfers between devices, fold_row(): got = lax.all_to_all(sent, 'lon', 0, 0)  19.2 us
    ppermute x16, waiting for transfers between devices, with_halo(): lax.ppermute(lax.slice_in_dim(block, 0, width, axis=dim), axis, backward)  11.7 us
    unnamed x63, local copies, waits for them, and re-layouts  10.8 us
  transfers between devices with their start and end apart: 40, of which 10 were waited for; matrix products, arithmetic and copies ran while one was open for 7% of the time, Pallas kernels for 0%

profile of v3, /device:TPU:2, one launch (start us, length us, event | category | flops | bytes accessed | tf_op | source)
XLA Modules:
  0.0 351.3 jit_solution(10246319971255678313)
XLA Ops:
  0.6 1.1 copy.179
  2.4 3.5 collective-permute-start.6
  5.9 4.5 %collective-permute-start.7 = (f32[3,16,1,128]{3,1,0,2:T(8,128)}, f32[3,16,1,128]{3,1,0,2:T(8,128)}, u32[]{:S(2)}, u32[]{:S(2)}) collective-permute-start(f32[3,16,1,128]{3,1,0,2:T(8,128)} %get-tuple-element.161), channel_id=1, source_target_pairs={{1,0},{2,1},{3,2},{4,3},{5,4},{6,5},{7,6},{9,8},{10,9},{11,10},{12... | collective-permute-start | bytes 73736 | tf_op jit(solution)/shard_map/ppermute | solution.py:19
  12.3 1.3 broadcast_select_fusion.7
  13.6 10.7 %all-to-all-start = ((f32[32,3,16,128]{3,2,1,0:T(8,128)}), f32[32,3,16,128]{3,2,1,0:T(8,128)}, u32[]{:S(2)}, u32[]{:S(2)}) async-start(f32[32,3,16,128]{3,2,1,0:T(8,128)} %get-tuple-element.167), calls=%async_computation | async-start | bytes 1572864 | tf_op jit(solution)/shard_map/all_to_all | solution.py:35
  25.0 3.7 %collective-permute-start.5 = (f32[4,16,1,128]{3,2,1,0:T(1,128)}, f32[4,16,1,128]{3,2,1,0:T(1,128)}, u32[]{:S(2)}, u32[]{:S(2)}) collective-permute-start(f32[4,16,1,128]{3,2,1,0:T(1,128)} %get-tuple-element.122), channel_id=1, source_target_pairs={{1,0},{2,1},{3,2},{4,3},{5,4},{6,5},{7,6},{9,8},{10,9},{11,10},{12... | collective-permute-start | bytes 98312 | tf_op jit(solution)/shard_map/ppermute | solution.py:19
  28.7 0.9 fusion.118
  29.7 4.3 %collective-permute-start.1 = (f32[4,16,16,1]{3,2,1,0:T(8,128)}, f32[4,16,16,1]{3,2,1,0:T(8,128)S(1)}, u32[]{:S(2)}, u32[]{:S(2)}) collective-permute-start(f32[4,16,16,1]{3,2,1,0:T(8,128)} %get-tuple-element.120), channel_id=1, source_target_pairs={{8,0},{16,8},{24,16},{32,24},{40,32},{48,40},{56,48},{64,56},{72,6... | collective-permute-start | bytes 12296 | tf_op jit(solution)/shard_map/ppermute | solution.py:19
  34.1 1.0 fusion.125
  36.0 11.7 %collective-permute-done.1 = f32[4,16,16,1]{3,2,1,0:T(8,128)S(1)} collective-permute-done((f32[4,16,16,1]{3,2,1,0:T(8,128)}, f32[4,16,16,1]{3,2,1,0:T(8,128)S(1)}, u32[]{:S(2)}, u32[]{:S(2)}) %collective-permute-start.1) | collective-permute-done | bytes 4128 | tf_op jit(solution)/shard_map/ppermute | solution.py:19
  47.6 2.0 collective-permute-start.2
  49.6 3.6 %collective-permute-done = f32[4,16,16,1]{3,2,1,0:T(8,128)S(1)} collective-permute-done((f32[4,16,16,1]{3,2,1,0:T(8,128)S(1)}, f32[4,16,16,1]{3,2,1,0:T(8,128)S(1)}, u32[]{:S(2)}, u32[]{:S(2)}) %collective-permute-start) | collective-permute-done | bytes 4128 | tf_op jit(solution)/shard_map/ppermute | solution.py:16
  54.0 1.3 add_bitcast_fusion
  56.2 2.7 collective-permute-done.2
  58.9 1.9 collective-permute-start.4
  60.8 7.2 %all-to-all-start.1 = ((f32[32,3,16,128]{3,2,1,0:T(8,128)}), f32[32,3,16,128]{3,2,1,0:T(8,128)}, u32[]{:S(2)}, u32[]{:S(2)}) async-start(f32[32,3,16,128]{3,2,1,0:T(8,128)} %get-tuple-element.168), calls=%async_computation.1 | async-start | bytes 1572864 | tf_op jit(solution)/shard_map/all_to_all | solution.py:35
  68.0 2.3 fusion
  73.7 19.1 %all-to-all-done.1 = f32[32,3,16,128]{3,2,1,0:T(8,128)} async-done(((f32[32,3,16,128]{3,2,1,0:T(8,128)}), f32[32,3,16,128]{3,2,1,0:T(8,128)}, u32[]{:S(2)}, u32[]{:S(2)}) %all-to-all-start.1) | async-done | bytes 786464 | tf_op jit(solution)/shard_map/all_to_all | solution.py:35
  94.3 2.9 fusion.11
  97.9 1.0 broadcast_select_fusion.5
  98.9 4.6 %all-to-all-start.2 = ((f32[32,3,16,128]{3,2,1,0:T(8,128)}), f32[32,3,16,128]{3,2,1,0:T(8,128)}, u32[]{:S(2)}, u32[]{:S(2)}) async-start(f32[32,3,16,128]{3,2,1,0:T(8,128)} %broadcast_select_fusion.5), calls=%async_computation.2 | async-start | bytes 1572864 | tf_op jit(solution)/shard_map/all_to_all | solution.py:35
  103.9 5.3 %collective-permute-start.9 = (f32[3,16,16,1]{3,1,0,2:T(8,128)S(1)}, f32[3,16,16,1]{3,1,0,2:T(8,128)S(1)}, u32[]{:S(2)}, u32[]{:S(2)}) collective-permute-start(f32[3,16,16,1]{3,1,0,2:T(8,128)S(1)} %get-tuple-element.153), channel_id=1, source_target_pairs={{8,0},{16,8},{24,16},{32,24},{40,32},{48,40},{56,48},{64,56},{72,6... | collective-permute-start | bytes 9224 | tf_op jit(solution)/shard_map/ppermute | solution.py:19
  109.9 2.9 collective-permute-start.10
  112.9 5.6 %collective-permute-start.11 = (f32[3,16,1,128]{3,1,0,2:T(8,128)S(1)}, f32[3,16,1,128]{3,1,0,2:T(8,128)S(1)}, u32[]{:S(2)}, u32[]{:S(2)}) collective-permute-start(f32[3,16,1,128]{3,1,0,2:T(8,128)S(1)} %get-tuple-element.156), channel_id=1, source_target_pairs={{1,0},{2,1},{3,2},{4,3},{5,4},{6,5},{7,6},{9,8},{10,9},{11,10},{12... | collective-permute-start | bytes 73736 | tf_op jit(solution)/shard_map/ppermute | solution.py:19
  118.5 12.5 %collective-permute-done.8 = f32[3,16,16,1]{3,1,0,2:T(8,128)S(1)} collective-permute-done((f32[3,16,16,1]{3,1,0,2:T(8,128)S(1)}, f32[3,16,16,1]{3,1,0,2:T(8,128)S(1)}, u32[]{:S(2)}, u32[]{:S(2)}) %collective-permute-start.8) | collective-permute-done | bytes 3104 | tf_op jit(solution)/shard_map/ppermute | solution.py:16
  131.0 1.2 fusion.1
  133.1 2.9 fusion.15
  136.1 1.0 broadcast_select_fusion.4
  137.1 5.0 %all-to-all-start.3 = ((f32[32,3,16,128]{3,2,1,0:T(8,128)}), f32[32,3,16,128]{3,2,1,0:T(8,128)}, u32[]{:S(2)}, u32[]{:S(2)}) async-start(f32[32,3,16,128]{3,2,1,0:T(8,128)} %broadcast_select_fusion.4), calls=%async_computation.3 | async-start | bytes 1572864 | tf_op jit(solution)/shard_map/all_to_all | solution.py:35
  142.8 5.2 %collective-permute-start.13 = (f32[3,16,16,1]{3,1,0,2:T(8,128)S(1)}, f32[3,16,16,1]{3,1,0,2:T(8,128)S(1)}, u32[]{:S(2)}, u32[]{:S(2)}) collective-permute-start(f32[3,16,16,1]{3,1,0,2:T(8,128)S(1)} %get-tuple-element.148), channel_id=1, source_target_pairs={{8,0},{16,8},{24,16},{32,24},{40,32},{48,40},{56,48},{64,56},{72,6... | collective-permute-start | bytes 9224 | tf_op jit(solution)/shard_map/ppermute | solution.py:19
  148.7 2.9 collective-permute-start.14
  151.7 5.6 %collective-permute-start.15 = (f32[3,16,1,128]{3,1,0,2:T(8,128)S(1)}, f32[3,16,1,128]{3,1,0,2:T(8,128)S(1)}, u32[]{:S(2)}, u32[]{:S(2)}) collective-permute-start(f32[3,16,1,128]{3,1,0,2:T(8,128)S(1)} %get-tuple-element.151), channel_id=1, source_target_pairs={{1,0},{2,1},{3,2},{4,3},{5,4},{6,5},{7,6},{9,8},{10,9},{11,10},{12... | collective-permute-start | bytes 73736 | tf_op jit(solution)/shard_map/ppermute | solution.py:19
  157.3 12.3 %collective-permute-done.12 = f32[3,16,16,1]{3,1,0,2:T(8,128)S(1)} collective-permute-done((f32[3,16,16,1]{3,1,0,2:T(8,128)S(1)}, f32[3,16,16,1]{3,1,0,2:T(8,128)S(1)}, u32[]{:S(2)}, u32[]{:S(2)}) %collective-permute-start.12) | collective-permute-done | bytes 3104 | tf_op jit(solution)/shard_map/ppermute | solution.py:16
  169.6 1.2 fusion.2
  171.7 2.9 fusion.21
  174.7 1.0 broadcast_select_fusion.3
  175.7 5.0 %all-to-all-start.4 = ((f32[32,3,16,128]{3,2,1,0:T(8,128)}), f32[32,3,16,128]{3,2,1,0:T(8,128)}, u32[]{:S(2)}, u32[]{:S(2)}) async-start(f32[32,3,16,128]{3,2,1,0:T(8,128)} %broadcast_select_fusion.3), calls=%async_computation.4 | async-start | bytes 1572864 | tf_op jit(solution)/shard_map/all_to_all | solution.py:35
  183.3 0.9 copy-done.14
  186.0 5.2 %collective-permute-start.17 = (f32[3,16,16,1]{3,1,0,2:T(8,128)S(1)}, f32[3,16,16,1]{3,1,0,2:T(8,128)S(1)}, u32[]{:S(2)}, u32[]{:S(2)}) collective-permute-start(f32[3,16,16,1]{3,1,0,2:T(8,128)S(1)} %get-tuple-element.143), channel_id=1, source_target_pairs={{8,0},{16,8},{24,16},{32,24},{40,32},{48,40},{56,48},{64,56},{72,6... | collective-permute-start | bytes 9224 | tf_op jit(solution)/shard_map/ppermute | solution.py:19
  192.0 2.9 collective-permute-start.18
  194.9 5.6 %collective-permute-start.19 = (f32[3,16,1,128]{3,1,0,2:T(8,128)S(1)}, f32[3,16,1,128]{3,1,0,2:T(8,128)S(1)}, u32[]{:S(2)}, u32[]{:S(2)}) collective-permute-start(f32[3,16,1,128]{3,1,0,2:T(8,128)S(1)} %get-tuple-element.146), channel_id=1, source_target_pairs={{1,0},{2,1},{3,2},{4,3},{5,4},{6,5},{7,6},{9,8},{10,9},{11,10},{12... | collective-permute-start | bytes 73736 | tf_op jit(solution)/shard_map/ppermute | solution.py:19
  200.5 7.8 %collective-permute-done.16 = f32[3,16,16,1]{3,1,0,2:T(8,128)S(1)} collective-permute-done((f32[3,16,16,1]{3,1,0,2:T(8,128)S(1)}, f32[3,16,16,1]{3,1,0,2:T(8,128)S(1)}, u32[]{:S(2)}, u32[]{:S(2)}) %collective-permute-start.16) | collective-permute-done | bytes 3104 | tf_op jit(solution)/shard_map/ppermute | solution.py:16
  210.2 1.8 fusion.20
  212.9 1.0 broadcast_select_fusion.2
  213.9 4.9 %all-to-all-start.5 = ((f32[32,3,16,128]{3,2,1,0:T(8,128)}), f32[32,3,16,128]{3,2,1,0:T(8,128)}, u32[]{:S(2)}, u32[]{:S(2)}) async-start(f32[32,3,16,128]{3,2,1,0:T(8,128)} %broadcast_select_fusion.2), calls=%async_computation.5 | async-start | bytes 1572864 | tf_op jit(solution)/shard_map/all_to_all | solution.py:35
  219.3 5.2 %collective-permute-start.21 = (f32[3,16,16,1]{3,1,0,2:T(8,128)S(1)}, f32[3,16,16,1]{3,1,0,2:T(8,128)S(1)}, u32[]{:S(2)}, u32[]{:S(2)}) collective-permute-start(f32[3,16,16,1]{3,1,0,2:T(8,128)S(1)} %get-tuple-element.141), channel_id=1, source_target_pairs={{8,0},{16,8},{24,16},{32,24},{40,32},{48,40},{56,48},{64,56},{72,6... | collective-permute-start | bytes 9224 | tf_op jit(solution)/shard_map/ppermute | solution.py:19
  225.3 3.1 collective-permute-start.22
  228.3 5.6 %collective-permute-start.23 = (f32[3,16,1,128]{3,2,1,0:T(1,128)S(1)}, f32[3,16,1,128]{3,2,1,0:T(1,128)S(1)}, u32[]{:S(2)}, u32[]{:S(2)}) collective-permute-start(f32[3,16,1,128]{3,2,1,0:T(1,128)S(1)} %slice.753), channel_id=1, source_target_pairs={{1,0},{2,1},{3,2},{4,3},{5,4},{6,5},{7,6},{9,8},{10,9},{11,10},{12... | collective-permute-start | bytes 73736 | tf_op jit(solution)/shard_map/ppermute | solution.py:19
  234.0 12.3 %collective-permute-done.20 = f32[3,16,16,1]{3,1,0,2:T(8,128)S(1)} collective-permute-done((f32[3,16,16,1]{3,1,0,2:T(8,128)S(1)}, f32[3,16,16,1]{3,1,0,2:T(8,128)S(1)}, u32[]{:S(2)}, u32[]{:S(2)}) %collective-permute-start.20) | collective-permute-done | bytes 3104 | tf_op jit(solution)/shard_map/ppermute | solution.py:16
  250.0 1.3 fusion.58
  251.5 1.0 broadcast_select_fusion.1
  252.5 5.1 %all-to-all-start.6 = ((f32[32,3,16,128]{3,2,1,0:T(8,128)}), f32[32,3,16,128]{3,2,1,0:T(8,128)}, u32[]{:S(2)}, u32[]{:S(2)}) async-start(f32[32,3,16,128]{3,2,1,0:T(8,128)} %broadcast_select_fusion.1), calls=%async_computation.6 | async-start | bytes 1572864 | tf_op jit(solution)/shard_map/all_to_all | solution.py:35
  258.2 5.3 %collective-permute-start.25 = (f32[3,16,16,1]{3,1,0,2:T(8,128)S(1)}, f32[3,16,16,1]{3,1,0,2:T(8,128)S(1)}, u32[]{:S(2)}, u32[]{:S(2)}) collective-permute-start(f32[3,16,16,1]{3,1,0,2:T(8,128)S(1)} %get-tuple-element.135), channel_id=1, source_target_pairs={{8,0},{16,8},{24,16},{32,24},{40,32},{48,40},{56,48},{64,56},{72,6... | collective-permute-start | bytes 9224 | tf_op jit(solution)/shard_map/ppermute | solution.py:19
  263.5 2.9 collective-permute-start.26
  266.5 5.6 %collective-permute-start.27 = (f32[3,16,1,128]{3,1,0,2:T(8,128)S(1)}, f32[3,16,1,128]{3,1,0,2:T(8,128)S(1)}, u32[]{:S(2)}, u32[]{:S(2)}) collective-permute-start(f32[3,16,1,128]{3,1,0,2:T(8,128)S(1)} %get-tuple-element.134), channel_id=1, source_target_pairs={{1,0},{2,1},{3,2},{4,3},{5,4},{6,5},{7,6},{9,8},{10,9},{11,10},{12... | collective-permute-start | bytes 73736 | tf_op jit(solution)/shard_map/ppermute | solution.py:19
  272.1 13.1 %collective-permute-done.24 = f32[3,16,16,1]{3,1,0,2:T(8,128)S(1)} collective-permute-done((f32[3,16,16,1]{3,1,0,2:T(8,128)S(1)}, f32[3,16,16,1]{3,1,0,2:T(8,128)S(1)}, u32[]{:S(2)}, u32[]{:S(2)}) %collective-permute-start.24) | collective-permute-done | bytes 3104 | tf_op jit(solution)/shard_map/ppermute | solution.py:16
  287.8 1.0 broadcast_select_fusion
  288.8 5.0 %all-to-all-start.7 = ((f32[32,3,16,128]{3,2,1,0:T(8,128)}), f32[32,3,16,128]{3,2,1,0:T(8,128)}, u32[]{:S(2)}, u32[]{:S(2)}) async-start(f32[32,3,16,128]{3,2,1,0:T(8,128)} %broadcast_select_fusion), calls=%async_computation.7 | async-start | bytes 1572864 | tf_op jit(solution)/shard_map/all_to_all | solution.py:35
  294.3 5.2 %collective-permute-start.29 = (f32[3,16,16,1]{3,1,0,2:T(8,128)S(1)}, f32[3,16,16,1]{3,1,0,2:T(8,128)S(1)}, u32[]{:S(2)}, u32[]{:S(2)}) collective-permute-start(f32[3,16,16,1]{3,1,0,2:T(8,128)S(1)} %get-tuple-element.126), channel_id=1, source_target_pairs={{8,0},{16,8},{24,16},{32,24},{40,32},{48,40},{56,48},{64,56},{72,6... | collective-permute-start | bytes 9224 | tf_op jit(solution)/shard_map/ppermute | solution.py:19
  300.3 2.9 collective-permute-start.30
  303.2 5.6 %collective-permute-start.31 = (f32[3,16,1,128]{3,1,0,2:T(8,128)S(1)}, f32[3,16,1,128]{3,1,0,2:T(8,128)S(1)}, u32[]{:S(2)}, u32[]{:S(2)}) collective-permute-start(f32[3,16,1,128]{3,1,0,2:T(8,128)S(1)} %get-tuple-element.125), channel_id=1, source_target_pairs={{1,0},{2,1},{3,2},{4,3},{5,4},{6,5},{7,6},{9,8},{10,9},{11,10},{12... | collective-permute-start | bytes 73736 | tf_op jit(solution)/shard_map/ppermute | solution.py:19
  308.8 12.5 %collective-permute-done.28 = f32[3,16,16,1]{3,1,0,2:T(8,128)S(1)} collective-permute-done((f32[3,16,16,1]{3,1,0,2:T(8,128)S(1)}, f32[3,16,16,1]{3,1,0,2:T(8,128)S(1)}, u32[]{:S(2)}, u32[]{:S(2)}) %collective-permute-start.28) | collective-permute-done | bytes 3104 | tf_op jit(solution)/shard_map/ppermute | solution.py:16
  323.7 2.8 multiply_reduce_fusion
  327.2 21.5 %all_to_all.46 = f32[256,1,1]{2,1,0:T(1,128)S(1)} all-to-all(f32[256,1,1]{2,1,0:T(1,128)S(1)} %broadcast_in_dim.173), channel_id=1, replica_groups=mesh['lon'=32,'lat'=8] {'lon','lat'}, dimensions={0} | all-to-all | bytes 2048 | tf_op jit(solution)/shard_map/all_to_all | solution.py:46
  (198 shorter events, 37.1 us)
Async XLA Ops:
  1.8 9.4 %copy-start.20 = (s32[16,16,128]{2,1,0:T(8,128)S(1)}, s32[16,16,128]{2,1,0:T(8,128)}, u32[]{:S(2)}) copy-start(s32[16,16,128]{2,1,0:T(8,128)} %param.31) | copy-start | bytes 393220
  2.4 69.5 %collective-permute-start.6 = (f32[3,16,1,128]{3,1,0,2:T(8,128)}, f32[3,16,1,128]{3,1,0,2:T(8,128)}, u32[]{:S(2)}, u32[]{:S(2)}) collective-permute-start(f32[3,16,1,128]{3,1,0,2:T(8,128)} %get-tuple-element.162), channel_id=1, source_target_pairs={{0,1},{1,2},{2,3},{3,4},{4,5},{5,6},{6,7},{8,9},{9,10},{10,11},{11... | collective-permute-start | bytes 73736 | tf_op jit(solution)/shard_map/ppermute | solution.py:16
  5.9 66.0 %collective-permute-start.7 = (f32[3,16,1,128]{3,1,0,2:T(8,128)}, f32[3,16,1,128]{3,1,0,2:T(8,128)}, u32[]{:S(2)}, u32[]{:S(2)}) collective-permute-start(f32[3,16,1,128]{3,1,0,2:T(8,128)} %get-tuple-element.161), channel_id=1, source_target_pairs={{1,0},{2,1},{3,2},{4,3},{5,4},{6,5},{7,6},{9,8},{10,9},{11,10},{12... | collective-permute-start | bytes 73736 | tf_op jit(solution)/shard_map/ppermute | solution.py:19
  11.1 0.9 copy-start.1
  11.1 1.0 copy-start.2
  12.3 1.3 copy-start.25
  13.6 10.7 %copy-start.6 = (f32[16,16,128]{2,1,0:T(8,128)S(1)}, f32[16,16,128]{2,1,0:T(8,128)}, u32[]{:S(2)}) copy-start(f32[16,16,128]{2,1,0:T(8,128)} %param.27) | copy-start | bytes 393220
  13.6 47.2 %all-to-all-start = ((f32[32,3,16,128]{3,2,1,0:T(8,128)}), f32[32,3,16,128]{3,2,1,0:T(8,128)}, u32[]{:S(2)}, u32[]{:S(2)}) async-start(f32[32,3,16,128]{3,2,1,0:T(8,128)} %get-tuple-element.167), calls=%async_computation | async-start | bytes 1572864 | tf_op jit(solution)/shard_map/all_to_all | solution.py:35
  25.0 45.3 %collective-permute-start.5 = (f32[4,16,1,128]{3,2,1,0:T(1,128)}, f32[4,16,1,128]{3,2,1,0:T(1,128)}, u32[]{:S(2)}, u32[]{:S(2)}) collective-permute-start(f32[4,16,1,128]{3,2,1,0:T(1,128)} %get-tuple-element.122), channel_id=1, source_target_pairs={{1,0},{2,1},{3,2},{4,3},{5,4},{6,5},{7,6},{9,8},{10,9},{11,10},{12... | collective-permute-start | bytes 98312 | tf_op jit(solution)/shard_map/ppermute | solution.py:19
  28.7 5.2 %copy-start.21 = (f32[16,16,128]{2,1,0:T(8,128)S(1)}, f32[16,16,128]{2,1,0:T(8,128)}, u32[]{:S(2)}) copy-start(f32[16,16,128]{2,1,0:T(8,128)} %param.29) | copy-start | bytes 393220
  29.7 18.0 %collective-permute-start.1 = (f32[4,16,16,1]{3,2,1,0:T(8,128)}, f32[4,16,16,1]{3,2,1,0:T(8,128)S(1)}, u32[]{:S(2)}, u32[]{:S(2)}) collective-permute-start(f32[4,16,16,1]{3,2,1,0:T(8,128)} %get-tuple-element.120), channel_id=1, source_target_pairs={{8,0},{16,8},{24,16},{32,24},{40,32},{48,40},{56,48},{64,56},{72,6... | collective-permute-start | bytes 12296 | tf_op jit(solution)/shard_map/ppermute | solution.py:19
  33.9 19.3 %collective-permute-start = (f32[4,16,16,1]{3,2,1,0:T(8,128)S(1)}, f32[4,16,16,1]{3,2,1,0:T(8,128)S(1)}, u32[]{:S(2)}, u32[]{:S(2)}) collective-permute-start(f32[4,16,16,1]{3,2,1,0:T(8,128)S(1)} %get-tuple-element.119), channel_id=1, source_target_pairs={{0,8},{8,16},{16,24},{24,32},{32,40},{40,48},{48,56},{56,64},{64,7... | collective-permute-start | bytes 12296 | tf_op jit(solution)/shard_map/ppermute | solution.py:16
  47.6 11.2 %collective-permute-start.2 = (f32[3,16,16,1]{3,1,0,2:T(8,128)}, f32[3,16,16,1]{3,1,0,2:T(8,128)}, u32[]{:S(2)}, u32[]{:S(2)}) collective-permute-start(f32[3,16,16,1]{3,1,0,2:T(8,128)} %get-tuple-element.159), channel_id=1, source_target_pairs={{0,8},{8,16},{16,24},{24,32},{32,40},{40,48},{48,56},{56,64},{64,7... | collective-permute-start | bytes 9224 | tf_op jit(solution)/shard_map/ppermute | solution.py:16
  53.2 0.8 copy-start.19
  54.0 14.0 %collective-permute-start.3 = (f32[3,16,16,1]{3,1,0,2:T(8,128)}, f32[3,16,16,1]{3,1,0,2:T(8,128)}, u32[]{:S(2)}, u32[]{:S(2)}) collective-permute-start(f32[3,16,16,1]{3,1,0,2:T(8,128)} %get-tuple-element.158), channel_id=1, source_target_pairs={{8,0},{16,8},{24,16},{32,24},{40,32},{48,40},{56,48},{64,56},{72,6... | collective-permute-start | bytes 9224 | tf_op jit(solution)/shard_map/ppermute | solution.py:19
  56.1 2.8 copy-start.24
  58.9 11.4 %collective-permute-start.4 = (f32[4,16,1,128]{3,2,1,0:T(1,128)S(1)}, f32[4,16,1,128]{3,2,1,0:T(1,128)S(1)}, u32[]{:S(2)}, u32[]{:S(2)}) collective-permute-start(f32[4,16,1,128]{3,2,1,0:T(1,128)S(1)} %copy-done.24), channel_id=1, source_target_pairs={{0,1},{1,2},{2,3},{3,4},{4,5},{5,6},{6,7},{8,9},{9,10},{10,11},{11... | collective-permute-start | bytes 98312 | tf_op jit(solution)/shard_map/ppermute | solution.py:16
  60.8 32.0 %all-to-all-start.1 = ((f32[32,3,16,128]{3,2,1,0:T(8,128)}), f32[32,3,16,128]{3,2,1,0:T(8,128)}, u32[]{:S(2)}, u32[]{:S(2)}) async-start(f32[32,3,16,128]{3,2,1,0:T(8,128)} %get-tuple-element.168), calls=%async_computation.1 | async-start | bytes 1572864 | tf_op jit(solution)/shard_map/all_to_all | solution.py:35
  71.2 0.7 copy-start.13
  72.8 20.9 %copy-start = (f32[3,16,16,128]{3,2,1,0:T(8,128)S(1)}, f32[3,16,16,128]{3,2,1,0:T(8,128)}, u32[]{:S(2)}) copy-start(f32[3,16,16,128]{3,2,1,0:T(8,128)} %param.25) | copy-start | bytes 1179652
  98.9 33.4 %all-to-all-start.2 = ((f32[32,3,16,128]{3,2,1,0:T(8,128)}), f32[32,3,16,128]{3,2,1,0:T(8,128)}, u32[]{:S(2)}, u32[]{:S(2)}) async-start(f32[32,3,16,128]{3,2,1,0:T(8,128)} %broadcast_select_fusion.5), calls=%async_computation.2 | async-start | bytes 1572864 | tf_op jit(solution)/shard_map/all_to_all | solution.py:35
  103.7 27.3 %collective-permute-start.8 = (f32[3,16,16,1]{3,1,0,2:T(8,128)S(1)}, f32[3,16,16,1]{3,1,0,2:T(8,128)S(1)}, u32[]{:S(2)}, u32[]{:S(2)}) collective-permute-start(f32[3,16,16,1]{3,1,0,2:T(8,128)S(1)} %get-tuple-element.154), channel_id=1, source_target_pairs={{0,8},{8,16},{16,24},{24,32},{32,40},{40,48},{48,56},{56,64},{64,7... | collective-permute-start | bytes 9224 | tf_op jit(solution)/shard_map/ppermute | solution.py:16
  103.9 27.2 %collective-permute-start.9 = (f32[3,16,16,1]{3,1,0,2:T(8,128)S(1)}, f32[3,16,16,1]{3,1,0,2:T(8,128)S(1)}, u32[]{:S(2)}, u32[]{:S(2)}) collective-permute-start(f32[3,16,16,1]{3,1,0,2:T(8,128)S(1)} %get-tuple-element.153), channel_id=1, source_target_pairs={{8,0},{16,8},{24,16},{32,24},{40,32},{48,40},{56,48},{64,56},{72,6... | collective-permute-start | bytes 9224 | tf_op jit(solution)/shard_map/ppermute | solution.py:19
  109.9 22.2 %collective-permute-start.10 = (f32[3,16,1,128]{3,1,0,2:T(8,128)S(1)}, f32[3,16,1,128]{3,1,0,2:T(8,128)S(1)}, u32[]{:S(2)}, u32[]{:S(2)}) collective-permute-start(f32[3,16,1,128]{3,1,0,2:T(8,128)S(1)} %get-tuple-element.157), channel_id=1, source_target_pairs={{0,1},{1,2},{2,3},{3,4},{4,5},{5,6},{6,7},{8,9},{9,10},{10,11},{11... | collective-permute-start | bytes 73736 | tf_op jit(solution)/shard_map/ppermute | solution.py:16
  112.9 19.3 %collective-permute-start.11 = (f32[3,16,1,128]{3,1,0,2:T(8,128)S(1)}, f32[3,16,1,128]{3,1,0,2:T(8,128)S(1)}, u32[]{:S(2)}, u32[]{:S(2)}) collective-permute-start(f32[3,16,1,128]{3,1,0,2:T(8,128)S(1)} %get-tuple-element.156), channel_id=1, source_target_pairs={{1,0},{2,1},{3,2},{4,3},{5,4},{6,5},{7,6},{9,8},{10,9},{11,10},{12... | collective-permute-start | bytes 73736 | tf_op jit(solution)/shard_map/ppermute | solution.py:19
  137.1 33.8 %all-to-all-start.3 = ((f32[32,3,16,128]{3,2,1,0:T(8,128)}), f32[32,3,16,128]{3,2,1,0:T(8,128)}, u32[]{:S(2)}, u32[]{:S(2)}) async-start(f32[32,3,16,128]{3,2,1,0:T(8,128)} %broadcast_select_fusion.4), calls=%async_computation.3 | async-start | bytes 1572864 | tf_op jit(solution)/shard_map/all_to_all | solution.py:35
  142.3 27.3 %collective-permute-start.12 = (f32[3,16,16,1]{3,1,0,2:T(8,128)S(1)}, f32[3,16,16,1]{3,1,0,2:T(8,128)S(1)}, u32[]{:S(2)}, u32[]{:S(2)}) collective-permute-start(f32[3,16,16,1]{3,1,0,2:T(8,128)S(1)} %get-tuple-element.149), channel_id=1, source_target_pairs={{0,8},{8,16},{16,24},{24,32},{32,40},{40,48},{48,56},{56,64},{64,7... | collective-permute-start | bytes 9224 | tf_op jit(solution)/shard_map/ppermute | solution.py:16
  142.8 26.9 %collective-permute-start.13 = (f32[3,16,16,1]{3,1,0,2:T(8,128)S(1)}, f32[3,16,16,1]{3,1,0,2:T(8,128)S(1)}, u32[]{:S(2)}, u32[]{:S(2)}) collective-permute-start(f32[3,16,16,1]{3,1,0,2:T(8,128)S(1)} %get-tuple-element.148), channel_id=1, source_target_pairs={{8,0},{16,8},{24,16},{32,24},{40,32},{48,40},{56,48},{64,56},{72,6... | collective-permute-start | bytes 9224 | tf_op jit(solution)/shard_map/ppermute | solution.py:19
  148.7 22.1 %collective-permute-start.14 = (f32[3,16,1,128]{3,1,0,2:T(8,128)S(1)}, f32[3,16,1,128]{3,1,0,2:T(8,128)S(1)}, u32[]{:S(2)}, u32[]{:S(2)}) collective-permute-start(f32[3,16,1,128]{3,1,0,2:T(8,128)S(1)} %get-tuple-element.152), channel_id=1, source_target_pairs={{0,1},{1,2},{2,3},{3,4},{4,5},{5,6},{6,7},{8,9},{9,10},{10,11},{11... | collective-permute-start | bytes 73736 | tf_op jit(solution)/shard_map/ppermute | solution.py:16
  151.7 19.1 %collective-permute-start.15 = (f32[3,16,1,128]{3,1,0,2:T(8,128)S(1)}, f32[3,16,1,128]{3,1,0,2:T(8,128)S(1)}, u32[]{:S(2)}, u32[]{:S(2)}) collective-permute-start(f32[3,16,1,128]{3,1,0,2:T(8,128)S(1)} %get-tuple-element.151), channel_id=1, source_target_pairs={{1,0},{2,1},{3,2},{4,3},{5,4},{6,5},{7,6},{9,8},{10,9},{11,10},{12... | collective-permute-start | bytes 73736 | tf_op jit(solution)/shard_map/ppermute | solution.py:19
  175.7 33.0 %all-to-all-start.4 = ((f32[32,3,16,128]{3,2,1,0:T(8,128)}), f32[32,3,16,128]{3,2,1,0:T(8,128)}, u32[]{:S(2)}, u32[]{:S(2)}) async-start(f32[32,3,16,128]{3,2,1,0:T(8,128)} %broadcast_select_fusion.3), calls=%async_computation.4 | async-start | bytes 1572864 | tf_op jit(solution)/shard_map/all_to_all | solution.py:35
  180.7 0.9 slice-start
  182.3 1.0 copy-start.12
  183.3 0.9 copy-start.14
  185.7 22.6 %collective-permute-start.16 = (f32[3,16,16,1]{3,1,0,2:T(8,128)S(1)}, f32[3,16,16,1]{3,1,0,2:T(8,128)S(1)}, u32[]{:S(2)}, u32[]{:S(2)}) collective-permute-start(f32[3,16,16,1]{3,1,0,2:T(8,128)S(1)} %get-tuple-element.144), channel_id=1, source_target_pairs={{0,8},{8,16},{16,24},{24,32},{32,40},{40,48},{48,56},{56,64},{64,7... | collective-permute-start | bytes 9224 | tf_op jit(solution)/shard_map/ppermute | solution.py:16
  186.0 22.3 %collective-permute-start.17 = (f32[3,16,16,1]{3,1,0,2:T(8,128)S(1)}, f32[3,16,16,1]{3,1,0,2:T(8,128)S(1)}, u32[]{:S(2)}, u32[]{:S(2)}) collective-permute-start(f32[3,16,16,1]{3,1,0,2:T(8,128)S(1)} %get-tuple-element.143), channel_id=1, source_target_pairs={{8,0},{16,8},{24,16},{32,24},{40,32},{48,40},{56,48},{64,56},{72,6... | collective-permute-start | bytes 9224 | tf_op jit(solution)/shard_map/ppermute | solution.py:19
  192.0 16.6 %collective-permute-start.18 = (f32[3,16,1,128]{3,1,0,2:T(8,128)S(1)}, f32[3,16,1,128]{3,1,0,2:T(8,128)S(1)}, u32[]{:S(2)}, u32[]{:S(2)}) collective-permute-start(f32[3,16,1,128]{3,1,0,2:T(8,128)S(1)} %get-tuple-element.147), channel_id=1, source_target_pairs={{0,1},{1,2},{2,3},{3,4},{4,5},{5,6},{6,7},{8,9},{9,10},{10,11},{11... | collective-permute-start | bytes 73736 | tf_op jit(solution)/shard_map/ppermute | solution.py:16
  194.9 13.7 %collective-permute-start.19 = (f32[3,16,1,128]{3,1,0,2:T(8,128)S(1)}, f32[3,16,1,128]{3,1,0,2:T(8,128)S(1)}, u32[]{:S(2)}, u32[]{:S(2)}) collective-permute-start(f32[3,16,1,128]{3,1,0,2:T(8,128)S(1)} %get-tuple-element.146), channel_id=1, source_target_pairs={{1,0},{2,1},{3,2},{4,3},{5,4},{6,5},{7,6},{9,8},{10,9},{11,10},{12... | collective-permute-start | bytes 73736 | tf_op jit(solution)/shard_map/ppermute | solution.py:19
  213.9 35.1 %all-to-all-start.5 = ((f32[32,3,16,128]{3,2,1,0:T(8,128)}), f32[32,3,16,128]{3,2,1,0:T(8,128)}, u32[]{:S(2)}, u32[]{:S(2)}) async-start(f32[32,3,16,128]{3,2,1,0:T(8,128)} %broadcast_select_fusion.2), calls=%async_computation.5 | async-start | bytes 1572864 | tf_op jit(solution)/shard_map/all_to_all | solution.py:35
  219.0 27.3 %collective-permute-start.20 = (f32[3,16,16,1]{3,1,0,2:T(8,128)S(1)}, f32[3,16,16,1]{3,1,0,2:T(8,128)S(1)}, u32[]{:S(2)}, u32[]{:S(2)}) collective-permute-start(f32[3,16,16,1]{3,1,0,2:T(8,128)S(1)} %get-tuple-element.142), channel_id=1, source_target_pairs={{0,8},{8,16},{16,24},{24,32},{32,40},{40,48},{48,56},{56,64},{64,7... | collective-permute-start | bytes 9224 | tf_op jit(solution)/shard_map/ppermute | solution.py:16
  219.3 27.0 %collective-permute-start.21 = (f32[3,16,16,1]{3,1,0,2:T(8,128)S(1)}, f32[3,16,16,1]{3,1,0,2:T(8,128)S(1)}, u32[]{:S(2)}, u32[]{:S(2)}) collective-permute-start(f32[3,16,16,1]{3,1,0,2:T(8,128)S(1)} %get-tuple-element.141), channel_id=1, source_target_pairs={{8,0},{16,8},{24,16},{32,24},{40,32},{48,40},{56,48},{64,56},{72,6... | collective-permute-start | bytes 9224 | tf_op jit(solution)/shard_map/ppermute | solution.py:19
  225.2 21.4 %copy-start.4 = (f32[16,16,128]{2,0,1:T(8,128)S(1)}, f32[16,16,128]{2,0,1:T(8,128)}, u32[]{:S(2)}) copy-start(f32[16,16,128]{2,0,1:T(8,128)} %copy.201) | copy-start | bytes 393220
  225.2 21.4 %copy-start.5 = (f32[16,16,128]{2,0,1:T(8,128)S(1)}, f32[16,16,128]{2,0,1:T(8,128)}, u32[]{:S(2)}) copy-start(f32[16,16,128]{2,0,1:T(8,128)} %copy.196) | copy-start | bytes 393220
  225.3 21.5 %collective-permute-start.22 = (f32[3,16,1,128]{3,1,0,2:T(8,128)S(1)}, f32[3,16,1,128]{3,1,0,2:T(8,128)S(1)}, u32[]{:S(2)}, u32[]{:S(2)}) collective-permute-start(f32[3,16,1,128]{3,1,0,2:T(8,128)S(1)} %get-tuple-element.140), channel_id=1, source_target_pairs={{0,1},{1,2},{2,3},{3,4},{4,5},{5,6},{6,7},{8,9},{9,10},{10,11},{11... | collective-permute-start | bytes 73736 | tf_op jit(solution)/shard_map/ppermute | solution.py:16
  228.3 18.5 %collective-permute-start.23 = (f32[3,16,1,128]{3,2,1,0:T(1,128)S(1)}, f32[3,16,1,128]{3,2,1,0:T(1,128)S(1)}, u32[]{:S(2)}, u32[]{:S(2)}) collective-permute-start(f32[3,16,1,128]{3,2,1,0:T(1,128)S(1)} %slice.753), channel_id=1, source_target_pairs={{1,0},{2,1},{3,2},{4,3},{5,4},{6,5},{7,6},{9,8},{10,9},{11,10},{12... | collective-permute-start | bytes 73736 | tf_op jit(solution)/shard_map/ppermute | solution.py:19
  246.9 0.9 copy-start.3
  247.8 0.9 copy-start.17
  248.7 1.3 copy-start.9
  252.5 5.1 %copy-start.18 = (f32[16,16,128]{2,1,0:T(8,128)S(1)}, f32[16,16,128]{2,1,0:T(8,128)}, u32[]{:S(2)}) copy-start(f32[16,16,128]{2,1,0:T(8,128)} %slice.755) | copy-start | bytes 393220
  252.5 33.3 %all-to-all-start.6 = ((f32[32,3,16,128]{3,2,1,0:T(8,128)}), f32[32,3,16,128]{3,2,1,0:T(8,128)}, u32[]{:S(2)}, u32[]{:S(2)}) async-start(f32[32,3,16,128]{3,2,1,0:T(8,128)} %broadcast_select_fusion.1), calls=%async_computation.6 | async-start | bytes 1572864 | tf_op jit(solution)/shard_map/all_to_all | solution.py:35
  257.7 27.8 %copy-start.15 = (f32[16,16,128]{2,0,1:T(8,128)}, f32[16,16,128]{2,0,1:T(8,128)S(1)}, u32[]{:S(2)}) copy-start(f32[16,16,128]{2,0,1:T(8,128)S(1)} %copy.206) | copy-start | bytes 393220
  257.9 27.3 %collective-permute-start.24 = (f32[3,16,16,1]{3,1,0,2:T(8,128)S(1)}, f32[3,16,16,1]{3,1,0,2:T(8,128)S(1)}, u32[]{:S(2)}, u32[]{:S(2)}) collective-permute-start(f32[3,16,16,1]{3,1,0,2:T(8,128)S(1)} %get-tuple-element.136), channel_id=1, source_target_pairs={{0,8},{8,16},{16,24},{24,32},{32,40},{40,48},{48,56},{56,64},{64,7... | collective-permute-start | bytes 9224 | tf_op jit(solution)/shard_map/ppermute | solution.py:16
  258.2 27.0 %collective-permute-start.25 = (f32[3,16,16,1]{3,1,0,2:T(8,128)S(1)}, f32[3,16,16,1]{3,1,0,2:T(8,128)S(1)}, u32[]{:S(2)}, u32[]{:S(2)}) collective-permute-start(f32[3,16,16,1]{3,1,0,2:T(8,128)S(1)} %get-tuple-element.135), channel_id=1, source_target_pairs={{8,0},{16,8},{24,16},{32,24},{40,32},{48,40},{56,48},{64,56},{72,6... | collective-permute-start | bytes 9224 | tf_op jit(solution)/shard_map/ppermute | solution.py:19
  263.5 21.9 %collective-permute-start.26 = (f32[3,16,1,128]{3,1,0,2:T(8,128)S(1)}, f32[3,16,1,128]{3,1,0,2:T(8,128)S(1)}, u32[]{:S(2)}, u32[]{:S(2)}) collective-permute-start(f32[3,16,1,128]{3,1,0,2:T(8,128)S(1)} %get-tuple-element.133), channel_id=1, source_target_pairs={{0,1},{1,2},{2,3},{3,4},{4,5},{5,6},{6,7},{8,9},{9,10},{10,11},{11... | collective-permute-start | bytes 73736 | tf_op jit(solution)/shard_map/ppermute | solution.py:16
  266.5 19.0 %collective-permute-start.27 = (f32[3,16,1,128]{3,1,0,2:T(8,128)S(1)}, f32[3,16,1,128]{3,1,0,2:T(8,128)S(1)}, u32[]{:S(2)}, u32[]{:S(2)}) collective-permute-start(f32[3,16,1,128]{3,1,0,2:T(8,128)S(1)} %get-tuple-element.134), channel_id=1, source_target_pairs={{1,0},{2,1},{3,2},{4,3},{5,4},{6,5},{7,6},{9,8},{10,9},{11,10},{12... | collective-permute-start | bytes 73736 | tf_op jit(solution)/shard_map/ppermute | solution.py:19
  285.5 1.1 copy-start.8
  288.8 34.0 %all-to-all-start.7 = ((f32[32,3,16,128]{3,2,1,0:T(8,128)}), f32[32,3,16,128]{3,2,1,0:T(8,128)}, u32[]{:S(2)}, u32[]{:S(2)}) async-start(f32[32,3,16,128]{3,2,1,0:T(8,128)} %broadcast_select_fusion), calls=%async_computation.7 | async-start | bytes 1572864 | tf_op jit(solution)/shard_map/all_to_all | solution.py:35
  294.0 27.3 %collective-permute-start.28 = (f32[3,16,16,1]{3,1,0,2:T(8,128)S(1)}, f32[3,16,16,1]{3,1,0,2:T(8,128)S(1)}, u32[]{:S(2)}, u32[]{:S(2)}) collective-permute-start(f32[3,16,16,1]{3,1,0,2:T(8,128)S(1)} %get-tuple-element.127), channel_id=1, source_target_pairs={{0,8},{8,16},{16,24},{24,32},{32,40},{40,48},{48,56},{56,64},{64,7... | collective-permute-start | bytes 9224 | tf_op jit(solution)/shard_map/ppermute | solution.py:16
  294.3 6.0 %copy-start.28 = (f32[3,16,1,128]{3,1,0,2:T(8,128)S(1)}, f32[3,16,1,128]{3,1,0,2:T(8,128)}, u32[]{:S(2)}) copy-start(f32[3,16,1,128]{3,1,0,2:T(8,128)} %get-tuple-element.124) | copy-start | bytes 73732
  294.3 27.0 %collective-permute-start.29 = (f32[3,16,16,1]{3,1,0,2:T(8,128)S(1)}, f32[3,16,16,1]{3,1,0,2:T(8,128)S(1)}, u32[]{:S(2)}, u32[]{:S(2)}) collective-permute-start(f32[3,16,16,1]{3,1,0,2:T(8,128)S(1)} %get-tuple-element.126), channel_id=1, source_target_pairs={{8,0},{16,8},{24,16},{32,24},{40,32},{48,40},{56,48},{64,56},{72,6... | collective-permute-start | bytes 9224 | tf_op jit(solution)/shard_map/ppermute | solution.py:19
  300.3 21.4 %collective-permute-start.30 = (f32[3,16,1,128]{3,1,0,2:T(8,128)S(1)}, f32[3,16,1,128]{3,1,0,2:T(8,128)S(1)}, u32[]{:S(2)}, u32[]{:S(2)}) collective-permute-start(f32[3,16,1,128]{3,1,0,2:T(8,128)S(1)} %copy-done.28), channel_id=1, source_target_pairs={{0,1},{1,2},{2,3},{3,4},{4,5},{5,6},{6,7},{8,9},{9,10},{10,11},{11... | collective-permute-start | bytes 73736 | tf_op jit(solution)/shard_map/ppermute | solution.py:16
  303.2 18.4 %collective-permute-start.31 = (f32[3,16,1,128]{3,1,0,2:T(8,128)S(1)}, f32[3,16,1,128]{3,1,0,2:T(8,128)S(1)}, u32[]{:S(2)}, u32[]{:S(2)}) collective-permute-start(f32[3,16,1,128]{3,1,0,2:T(8,128)S(1)} %get-tuple-element.125), channel_id=1, source_target_pairs={{1,0},{2,1},{3,2},{4,3},{5,4},{6,5},{7,6},{9,8},{10,9},{11,10},{12... | collective-permute-start | bytes 73736 | tf_op jit(solution)/shard_map/ppermute | solution.py:19
  321.6 0.9 copy-start.16
  322.5 1.1 copy-start.10
  (7 other events, 4.7 us)

commit v4 on v3

--- a/solution.py
+++ b/solution.py
@@ -99,68 +99,84 @@
         partner_row = fold_row(top_row, fold_partner)
         return (east_west, south_north, partner_row)
 
+    def combine(quantity, east_flux, north_flux, vertical_part, uptake, forcing, sea):
+        return sea * (
+            quantity
+            - (
+                east_flux[..., 1:]
+                - east_flux[..., :-1]
+                + (north_flux[:, :, 1:, :] - north_flux[:, :, :-1, :])
+                + vertical_part
+            )
+            - uptake
+            + forcing
+        )
+
     kept_states = [tracer_start]
-    for repeat in range(STEPS):
-        advance_quantity = kept_states[-1]
-        uptake = decay_rate * advance_quantity / jnp.sqrt(1.0 + advance_quantity * advance_quantity)
-        divergence_east_west, divergence_south_north, divergence_partner_row = neighbours(
-            advance_quantity
-        )
-        east_flux = (
-            east_own * divergence_east_west[..., :-1] + east_next * divergence_east_west[..., 1:]
-        )
-        north_flux = (
-            north_own * divergence_south_north[:, :, :-1, :]
-            + north_next * divergence_south_north[:, :, 1:, :]
-        )
-        divergence_top_row = advance_quantity[:, :, -1, :]
-        fold_flux = fold_own * divergence_top_row + fold_next * divergence_partner_row
-        north_flux = north_flux.at[:, :, -1, :].add(fold_flux)
-        up_flux = up_own * advance_quantity[:, :-1] + up_next * advance_quantity[:, 1:]
-        zero_level = jnp.zeros_like(advance_quantity[:, :1])
-        vertical_part = jnp.concatenate([up_flux, zero_level], 1) - jnp.concatenate(
-            [zero_level, up_flux], 1
-        )
-        kept_states.append(
-            ocean
-            * (
-                advance_quantity
-                - (
-                    east_flux[..., 1:]
-                    - east_flux[..., :-1]
-                    + (north_flux[:, :, 1:, :] - north_flux[:, :, :-1, :])
-                    + vertical_part
-                )
-                - uptake
-                + source
-            )
-        )
+    for _ in range(STEPS):
+      advance_quantity = kept_states[-1]
+      uptake = decay_rate * advance_quantity / jnp.sqrt(1.0 + advance_quantity * advance_quantity)
+      divergence_east_west, divergence_south_north, divergence_partner_row = neighbours(
+          advance_quantity
+      )
+      east_flux = (
+          east_own * divergence_east_west[..., :-1] + east_next * divergence_east_west[..., 1:]
+      )
+      north_flux = (
+          north_own * divergence_south_north[:, :, :-1, :]
+          + north_next * divergence_south_north[:, :, 1:, :]
+      )
+      up_flux = up_own * advance_quantity[:, :-1] + up_next * advance_quantity[:, 1:]
+      zero_level = jnp.zeros_like(advance_quantity[:, :1])
+      vertical_part = jnp.concatenate([up_flux, zero_level], 1) - jnp.concatenate(
+          [zero_level, up_flux], 1
+      )
+      main = combine(advance_quantity, east_flux, north_flux, vertical_part, uptake, source, ocean)
+      divergence_top_row = advance_quantity[:, :, -1, :]
+      fold_flux = fold_own * divergence_top_row + fold_next * divergence_partner_row
+      top_north = north_flux[:, :, -2:, :].at[:, :, -1, :].add(fold_flux)
+      top = combine(
+          advance_quantity[:, :, -1:],
+          east_flux[:, :, -1:],
+          top_north,
+          vertical_part[:, :, -1:],
+          uptake[:, :, -1:],
+          source[:, :, -1:],
+          ocean[:, -1:],
+      )
+      kept_states.append(jnp.concatenate([main[:, :, :-1], top], axis=2))
     last_state = kept_states[-1]
     adjoint = ocean * (last_state - target)
     source_grad = ocean * adjoint
     for backward in range(STEPS - 1, 0, -1):
-        current = kept_states[backward]
-        weight = ocean * adjoint
-        transposed_east_west, transposed_south_north, transposed_partner_row = neighbours(weight)
-        east_diff = transposed_east_west[..., :-1] - transposed_east_west[..., 1:]
-        north_diff = transposed_south_north[:, :, :-1, :] - transposed_south_north[:, :, 1:, :]
-        up_diff = weight[:, :-1] - weight[:, 1:]
-        result = east_own[..., 1:] * east_diff[..., 1:] + east_next[..., :-1] * east_diff[..., :-1]
-        result = result + (
-            north_own[:, 1:, :] * north_diff[:, :, 1:, :]
-            + north_next[:, :-1, :] * north_diff[:, :, :-1, :]
-        )
-        result = result.at[:, :, -1, :].add(
-            fold_own * (weight[:, :, -1, :] - transposed_partner_row)
-        )
-        transposed_zero_level = jnp.zeros_like(weight[:, :1])
-        result = result + (
-            jnp.concatenate([up_own * up_diff, transposed_zero_level], 1)
-            + jnp.concatenate([transposed_zero_level, up_next * up_diff], 1)
-        )
-        spread = 1.0 + current * current
-        adjoint = weight - result - decay_rate / (spread * jnp.sqrt(spread)) * weight
-        source_grad = source_grad + ocean * adjoint
+      current = kept_states[backward]
+      weight = ocean * adjoint
+      transposed_east_west, transposed_south_north, transposed_partner_row = neighbours(weight)
+      east_diff = transposed_east_west[..., :-1] - transposed_east_west[..., 1:]
+      north_diff = transposed_south_north[:, :, :-1, :] - transposed_south_north[:, :, 1:, :]
+      up_diff = weight[:, :-1] - weight[:, 1:]
+      result = east_own[..., 1:] * east_diff[..., 1:] + east_next[..., :-1] * east_diff[..., :-1]
+      result = result + (
+          north_own[:, 1:, :] * north_diff[:, :, 1:, :]
+          + north_next[:, :-1, :] * north_diff[:, :, :-1, :]
+      )
+      transposed_zero_level = jnp.zeros_like(weight[:, :1])
+      up_part = jnp.concatenate([up_own * up_diff, transposed_zero_level], 1) + jnp.concatenate(
+          [transposed_zero_level, up_next * up_diff], 1
+      )
+      spread = 1.0 + current * current
+      damping = decay_rate / (spread * jnp.sqrt(spread))
+      main = weight - (result + up_part) - damping * weight
+      top_result = result[:, :, -1:, :] + (
+          fold_own * (weight[:, :, -1, :] - transposed_partner_row)
+      )[:, :, None, :]
+      top = (
+          weight[:, :, -1:]
+          - (top_result + up_part[:, :, -1:])
+          - damping[:, :, -1:] * weight[:, :, -1:]
+      )
+      adjoint = jnp.concatenate([main[:, :, :-1], top], axis=2)
+      source_grad = source_grad + ocean * adjoint
     squares = tree_sum(jnp.sum(source_grad * source_grad), ("lon", "lat"))
     return (source_grad, jnp.sqrt(squares))
 

time: 356 us -> 358 us (level)
  waiting for transfers between devices: 108 us -> 137 us
  blocking collectives: 21.5 us -> 0 us
  other arithmetic: 39.8 us -> 30.9 us
    ppermute x16, waiting for transfers between devices: 76.8 us -> 106 us  [with_halo(): lax.ppermute(lax.slice_in_dim(block, block.shape[dim] - width, None, axis...]
    all_to_all x1 -> x0, blocking collectives: 21.5 us -> none  [tree_sum(): got = lax.all_to_all(jnp.broadcast_to(value, (count,)), axes, 0, 0)]
    ppermute x16, waiting for transfers between devices: 11.7 us -> 0.04 us  [with_halo(): lax.ppermute(lax.slice_in_dim(block, 0, width, axis=dim), axis, backward)]
    all_to_all x0 -> x1, waiting for transfers between devices: none -> 11 us  [tree_sum(): got = lax.all_to_all(jnp.broadcast_to(value, (count,)), axes, 0, 0)]
    all_to_all x0 -> x1, starting transfers between devices: none -> 7.95 us  [tree_sum(): got = lax.all_to_all(jnp.broadcast_to(value, (count,)), axes, 0, 0)]
    div x3, other arithmetic: 8.63 us -> 3.82 us  [on_device(): damping = decay_rate / (spread * jnp.sqrt(spread))]
    ppermute x16, starting transfers between devices: 26.9 us -> 22.2 us  [with_halo(): lax.ppermute(lax.slice_in_dim(block, block.shape[dim] - width, None, axis...]
    mul x3 -> x6, other arithmetic: 1.97 us -> 5.83 us  [combine(): sea * (quantity - (east_flux[..., 1:] - east_flux[..., :-1] + (north_flux...]
  transfers between devices with their start and end apart: 40 -> 41, of which waited for: 10 -> 10; matrix products, arithmetic and copies ran while one was open for 7% -> 6% of each run, Pallas kernels for 0% -> 0%
where the time goes in v4:
time: 358 us; the launch traced here: 353 us
  starting transfers between devices  154 us (43%)
  waiting for transfers between devices  137 us (38%)
  other arithmetic  30.9 us (9%)
  local copies, waits for them, and re-layouts  27.6 us (8%)
  between operations  3.71 us (1%)
    ppermute x16, waiting for transfers between devices, with_halo(): lax.ppermute(lax.slice_in_dim(block, block.shape[dim] - width, None, axis...  106 us
    ppermute x16, starting transfers between devices, with_halo(): lax.ppermute(lax.slice_in_dim(block, 0, width, axis=dim), axis, backward)  78.5 us
    all_to_all x8, starting transfers between devices, fold_row(): got = lax.all_to_all(sent, 'lon', 0, 0)  44.9 us
    ppermute x16, starting transfers between devices, with_halo(): lax.ppermute(lax.slice_in_dim(block, block.shape[dim] - width, None, axis...  22.2 us
    all_to_all x8, waiting for transfers between devices, fold_row(): got = lax.all_to_all(sent, 'lon', 0, 0)  19.8 us
    unnamed x74, local copies, waits for them, and re-layouts  12.8 us
    all_to_all x1, waiting for transfers between devices, tree_sum(): got = lax.all_to_all(jnp.broadcast_to(value, (count,)), axes, 0, 0)  11 us
    all_to_all x1, starting transfers between devices, tree_sum(): got = lax.all_to_all(jnp.broadcast_to(value, (count,)), axes, 0, 0)  7.95 us
  transfers between devices with their start and end apart: 41, of which 10 were waited for; matrix products, arithmetic and copies ran while one was open for 6% of the time, Pallas kernels for 0%

profile of v4, /device:TPU:2, one launch (start us, length us, event | category | flops | bytes accessed | tf_op | source)
XLA Modules:
  0.0 353.1 jit_solution(12690333832951809450)
XLA Ops:
  1.4 1.1 copy.222
  5.1 1.3 broadcast_select_fusion.7
  6.4 10.5 %all-to-all-start = ((f32[32,3,16,128]{3,2,1,0:T(8,128)}), f32[32,3,16,128]{3,2,1,0:T(8,128)S(1)}, u32[]{:S(2)}, u32[]{:S(2)}) async-start(f32[32,3,16,128]{3,2,1,0:T(8,128)} %get-tuple-element.130), calls=%async_computation | async-start | bytes 1572864 | tf_op jit(solution)/shard_map/all_to_all | solution.py:35
  17.1 3.5 collective-permute-start.4
  20.5 4.5 %collective-permute-start.5 = (f32[4,16,1,128]{3,2,1,0:T(1,128)S(1)}, f32[4,16,1,128]{3,2,1,0:T(1,128)S(1)}, u32[]{:S(2)}, u32[]{:S(2)}) collective-permute-start(f32[4,16,1,128]{3,2,1,0:T(1,128)S(1)} %get-tuple-element.82), channel_id=1, source_target_pairs={{1,0},{2,1},{3,2},{4,3},{5,4},{6,5},{7,6},{9,8},{10,9},{11,10},{12... | collective-permute-start | bytes 98312 | tf_op jit(solution)/shard_map/ppermute | solution.py:19
  25.0 1.9 collective-permute-start.6
  27.0 1.1 fusion.172
  28.1 5.4 %collective-permute-start.1 = (f32[4,16,16,1]{3,2,1,0:T(8,128)}, f32[4,16,16,1]{3,2,1,0:T(8,128)}, u32[]{:S(2)}, u32[]{:S(2)}) collective-permute-start(f32[4,16,16,1]{3,2,1,0:T(8,128)} %get-tuple-element.80), channel_id=1, source_target_pairs={{8,0},{16,8},{24,16},{32,24},{40,32},{48,40},{56,48},{64,56},{72,6... | collective-permute-start | bytes 12296 | tf_op jit(solution)/shard_map/ppermute | solution.py:19
  33.7 1.0 fusion.179
  34.8 11.3 %collective-permute-done = f32[4,16,16,1]{3,2,1,0:T(8,128)} collective-permute-done((f32[4,16,16,1]{3,2,1,0:T(8,128)}, f32[4,16,16,1]{3,2,1,0:T(8,128)}, u32[]{:S(2)}, u32[]{:S(2)}) %collective-permute-start) | collective-permute-done | bytes 4128 | tf_op jit(solution)/shard_map/ppermute | solution.py:16
  46.1 5.4 %collective-permute-start.3 = (f32[3,16,16,1]{3,1,0,2:T(8,128)}, f32[3,16,16,1]{3,1,0,2:T(8,128)S(1)}, u32[]{:S(2)}, u32[]{:S(2)}) collective-permute-start(f32[3,16,16,1]{3,1,0,2:T(8,128)} %get-tuple-element.121), channel_id=1, source_target_pairs={{8,0},{16,8},{24,16},{32,24},{40,32},{48,40},{56,48},{64,56},{72,6... | collective-permute-start | bytes 9224 | tf_op jit(solution)/shard_map/ppermute | solution.py:19
  51.5 1.4 add_bitcast_fusion
  53.9 3.3 collective-permute-done.2
  57.2 5.8 %collective-permute-start.7 = (f32[3,16,1,128]{3,1,0,2:T(8,128)}, f32[3,16,1,128]{3,1,0,2:T(8,128)}, u32[]{:S(2)}, u32[]{:S(2)}) collective-permute-start(f32[3,16,1,128]{3,1,0,2:T(8,128)} %get-tuple-element.124), channel_id=1, source_target_pairs={{1,0},{2,1},{3,2},{4,3},{5,4},{6,5},{7,6},{9,8},{10,9},{11,10},{12... | collective-permute-start | bytes 73736 | tf_op jit(solution)/shard_map/ppermute | solution.py:19
  62.9 1.2 fusion
  65.0 4.6 %all-to-all-start.1 = ((f32[32,3,16,128]{3,2,1,0:T(8,128)}), f32[32,3,16,128]{3,2,1,0:T(8,128)}, u32[]{:S(2)}, u32[]{:S(2)}) async-start(f32[32,3,16,128]{3,2,1,0:T(8,128)} %get-tuple-element.131), calls=%async_computation.1 | async-start | bytes 1572864 | tf_op jit(solution)/shard_map/all_to_all | solution.py:35
  71.8 1.3 fusion.59
  74.7 19.8 %all-to-all-done.1 = f32[32,3,16,128]{3,2,1,0:T(8,128)} async-done(((f32[32,3,16,128]{3,2,1,0:T(8,128)}), f32[32,3,16,128]{3,2,1,0:T(8,128)}, u32[]{:S(2)}, u32[]{:S(2)}) %all-to-all-start.1) | async-done | bytes 786464 | tf_op jit(solution)/shard_map/all_to_all | solution.py:35
  95.2 0.9 fusion.161
  96.8 1.0 broadcast_select_fusion.5
  97.8 4.8 %all-to-all-start.2 = ((f32[32,3,16,128]{3,2,1,0:T(8,128)}), f32[32,3,16,128]{3,2,1,0:T(8,128)}, u32[]{:S(2)}, u32[]{:S(2)}) async-start(f32[32,3,16,128]{3,2,1,0:T(8,128)} %broadcast_select_fusion.5), calls=%async_computation.2 | async-start | bytes 1572864 | tf_op jit(solution)/shard_map/all_to_all | solution.py:35
  102.6 2.7 collective-permute-start.11
  105.3 3.2 collective-permute-start.10
  108.8 5.3 %collective-permute-start.9 = (f32[3,16,16,1]{3,1,0,2:T(8,128)S(1)}, f32[3,16,16,1]{3,1,0,2:T(8,128)S(1)}, u32[]{:S(2)}, u32[]{:S(2)}) collective-permute-start(f32[3,16,16,1]{3,1,0,2:T(8,128)S(1)} %get-tuple-element.118), channel_id=1, source_target_pairs={{8,0},{16,8},{24,16},{32,24},{40,32},{48,40},{56,48},{64,56},{72,6... | collective-permute-start | bytes 9224 | tf_op jit(solution)/shard_map/ppermute | solution.py:19
  114.2 15.9 %collective-permute-done.8 = f32[3,16,16,1]{3,1,0,2:T(8,128)S(1)} collective-permute-done((f32[3,16,16,1]{3,1,0,2:T(8,128)S(1)}, f32[3,16,16,1]{3,1,0,2:T(8,128)S(1)}, u32[]{:S(2)}, u32[]{:S(2)}) %collective-permute-start.8) | collective-permute-done | bytes 3104 | tf_op jit(solution)/shard_map/ppermute | solution.py:16
  131.3 1.3 fusion.8
  134.4 1.0 broadcast_select_fusion.4
  135.4 5.0 %all-to-all-start.3 = ((f32[32,3,16,128]{3,2,1,0:T(8,128)}), f32[32,3,16,128]{3,2,1,0:T(8,128)}, u32[]{:S(2)}, u32[]{:S(2)}) async-start(f32[32,3,16,128]{3,2,1,0:T(8,128)} %broadcast_select_fusion.4), calls=%async_computation.3 | async-start | bytes 1572864 | tf_op jit(solution)/shard_map/all_to_all | solution.py:35
  140.5 2.7 collective-permute-start.15
  143.1 3.2 collective-permute-start.14
  146.8 5.3 %collective-permute-start.13 = (f32[3,16,16,1]{3,1,0,2:T(8,128)S(1)}, f32[3,16,16,1]{3,1,0,2:T(8,128)S(1)}, u32[]{:S(2)}, u32[]{:S(2)}) collective-permute-start(f32[3,16,16,1]{3,1,0,2:T(8,128)S(1)} %get-tuple-element.116), channel_id=1, source_target_pairs={{8,0},{16,8},{24,16},{32,24},{40,32},{48,40},{56,48},{64,56},{72,6... | collective-permute-start | bytes 9224 | tf_op jit(solution)/shard_map/ppermute | solution.py:19
  152.2 15.7 %collective-permute-done.12 = f32[3,16,16,1]{3,1,0,2:T(8,128)S(1)} collective-permute-done((f32[3,16,16,1]{3,1,0,2:T(8,128)S(1)}, f32[3,16,16,1]{3,1,0,2:T(8,128)S(1)}, u32[]{:S(2)}, u32[]{:S(2)}) %collective-permute-start.12) | collective-permute-done | bytes 3104 | tf_op jit(solution)/shard_map/ppermute | solution.py:16
  168.4 1.4 fusion.9
  169.8 2.7 collective-permute-start.19
  173.2 0.9 fusion.157
  174.2 3.2 collective-permute-start.18
  177.4 1.1 fusion.10
  178.5 1.0 broadcast_select_fusion.3
  179.6 5.0 %all-to-all-start.4 = ((f32[32,3,16,128]{3,2,1,0:T(8,128)}), f32[32,3,16,128]{3,2,1,0:T(8,128)}, u32[]{:S(2)}, u32[]{:S(2)}) async-start(f32[32,3,16,128]{3,2,1,0:T(8,128)} %broadcast_select_fusion.3), calls=%async_computation.4 | async-start | bytes 1572864 | tf_op jit(solution)/shard_map/all_to_all | solution.py:35
  185.1 5.2 %collective-permute-start.17 = (f32[3,16,16,1]{3,1,0,2:T(8,128)S(1)}, f32[3,16,16,1]{3,1,0,2:T(8,128)S(1)}, u32[]{:S(2)}, u32[]{:S(2)}) collective-permute-start(f32[3,16,16,1]{3,1,0,2:T(8,128)S(1)} %get-tuple-element.114), channel_id=1, source_target_pairs={{8,0},{16,8},{24,16},{32,24},{40,32},{48,40},{56,48},{64,56},{72,6... | collective-permute-start | bytes 9224 | tf_op jit(solution)/shard_map/ppermute | solution.py:19
  190.3 21.8 %collective-permute-done.16 = f32[3,16,16,1]{3,1,0,2:T(8,128)S(1)} collective-permute-done((f32[3,16,16,1]{3,1,0,2:T(8,128)S(1)}, f32[3,16,16,1]{3,1,0,2:T(8,128)S(1)}, u32[]{:S(2)}, u32[]{:S(2)}) %collective-permute-start.16) | collective-permute-done | bytes 3104 | tf_op jit(solution)/shard_map/ppermute | solution.py:16
  216.4 1.2 fusion.61
  218.2 1.0 broadcast_select_fusion.2
  219.2 5.0 %all-to-all-start.5 = ((f32[32,3,16,128]{3,2,1,0:T(8,128)}), f32[32,3,16,128]{3,2,1,0:T(8,128)}, u32[]{:S(2)}, u32[]{:S(2)}) async-start(f32[32,3,16,128]{3,2,1,0:T(8,128)} %broadcast_select_fusion.2), calls=%async_computation.5 | async-start | bytes 1572864 | tf_op jit(solution)/shard_map/all_to_all | solution.py:35
  224.2 0.9 copy-done.10
  227.7 5.2 %collective-permute-start.21 = (f32[3,16,16,1]{3,1,0,2:T(8,128)S(1)}, f32[3,16,16,1]{3,1,0,2:T(8,128)S(1)}, u32[]{:S(2)}, u32[]{:S(2)}) collective-permute-start(f32[3,16,16,1]{3,1,0,2:T(8,128)S(1)} %get-tuple-element.107), channel_id=1, source_target_pairs={{8,0},{16,8},{24,16},{32,24},{40,32},{48,40},{56,48},{64,56},{72,6... | collective-permute-start | bytes 9224 | tf_op jit(solution)/shard_map/ppermute | solution.py:19
  232.9 1.9 collective-permute-start.22
  234.8 6.0 %collective-permute-start.23 = (f32[3,16,1,128]{3,1,0,2:T(8,128)S(1)}, f32[3,16,1,128]{3,1,0,2:T(8,128)S(1)}, u32[]{:S(2)}, u32[]{:S(2)}) collective-permute-start(f32[3,16,1,128]{3,1,0,2:T(8,128)S(1)} %get-tuple-element.109), channel_id=1, source_target_pairs={{1,0},{2,1},{3,2},{4,3},{5,4},{6,5},{7,6},{9,8},{10,9},{11,10},{12... | collective-permute-start | bytes 73736 | tf_op jit(solution)/shard_map/ppermute | solution.py:19
  240.9 10.9 %collective-permute-done.20 = f32[3,16,16,1]{3,1,0,2:T(8,128)S(1)} collective-permute-done((f32[3,16,16,1]{3,1,0,2:T(8,128)S(1)}, f32[3,16,16,1]{3,1,0,2:T(8,128)S(1)}, u32[]{:S(2)}, u32[]{:S(2)}) %collective-permute-start.20) | collective-permute-done | bytes 3104 | tf_op jit(solution)/shard_map/ppermute | solution.py:16
  255.0 1.0 broadcast_select_fusion.1
  256.0 5.0 %all-to-all-start.6 = ((f32[32,3,16,128]{3,2,1,0:T(8,128)}), f32[32,3,16,128]{3,2,1,0:T(8,128)}, u32[]{:S(2)}, u32[]{:S(2)}) async-start(f32[32,3,16,128]{3,2,1,0:T(8,128)} %broadcast_select_fusion.1), calls=%async_computation.6 | async-start | bytes 1572864 | tf_op jit(solution)/shard_map/all_to_all | solution.py:35
  261.5 5.2 %collective-permute-start.25 = (f32[3,16,16,1]{3,1,0,2:T(8,128)S(1)}, f32[3,16,16,1]{3,1,0,2:T(8,128)S(1)}, u32[]{:S(2)}, u32[]{:S(2)}) collective-permute-start(f32[3,16,16,1]{3,1,0,2:T(8,128)S(1)} %get-tuple-element.100), channel_id=1, source_target_pairs={{8,0},{16,8},{24,16},{32,24},{40,32},{48,40},{56,48},{64,56},{72,6... | collective-permute-start | bytes 9224 | tf_op jit(solution)/shard_map/ppermute | solution.py:19
  266.7 1.9 collective-permute-start.26
  268.6 6.3 %collective-permute-start.27 = (f32[3,16,1,128]{3,1,0,2:T(8,128)S(1)}, f32[3,16,1,128]{3,1,0,2:T(8,128)S(1)}, u32[]{:S(2)}, u32[]{:S(2)}) collective-permute-start(f32[3,16,1,128]{3,1,0,2:T(8,128)S(1)} %get-tuple-element.102), channel_id=1, source_target_pairs={{1,0},{2,1},{3,2},{4,3},{5,4},{6,5},{7,6},{9,8},{10,9},{11,10},{12... | collective-permute-start | bytes 73736 | tf_op jit(solution)/shard_map/ppermute | solution.py:19
  274.9 13.6 %collective-permute-done.24 = f32[3,16,16,1]{3,1,0,2:T(8,128)S(1)} collective-permute-done((f32[3,16,16,1]{3,1,0,2:T(8,128)S(1)}, f32[3,16,16,1]{3,1,0,2:T(8,128)S(1)}, u32[]{:S(2)}, u32[]{:S(2)}) %collective-permute-start.24) | collective-permute-done | bytes 3104 | tf_op jit(solution)/shard_map/ppermute | solution.py:16
  291.8 1.0 broadcast_select_fusion
  292.9 5.0 %all-to-all-start.7 = ((f32[32,3,16,128]{3,2,1,0:T(8,128)}), f32[32,3,16,128]{3,2,1,0:T(8,128)}, u32[]{:S(2)}, u32[]{:S(2)}) async-start(f32[32,3,16,128]{3,2,1,0:T(8,128)} %broadcast_select_fusion), calls=%async_computation.7 | async-start | bytes 1572864 | tf_op jit(solution)/shard_map/all_to_all | solution.py:35
  298.3 5.2 %collective-permute-start.29 = (f32[3,16,16,1]{3,1,0,2:T(8,128)S(1)}, f32[3,16,16,1]{3,1,0,2:T(8,128)S(1)}, u32[]{:S(2)}, u32[]{:S(2)}) collective-permute-start(f32[3,16,16,1]{3,1,0,2:T(8,128)S(1)} %get-tuple-element.93), channel_id=1, source_target_pairs={{8,0},{16,8},{24,16},{32,24},{40,32},{48,40},{56,48},{64,56},{72,6... | collective-permute-start | bytes 9224 | tf_op jit(solution)/shard_map/ppermute | solution.py:19
  303.6 1.9 collective-permute-start.30
  305.5 6.0 %collective-permute-start.31 = (f32[3,16,1,128]{3,1,0,2:T(8,128)S(1)}, f32[3,16,1,128]{3,1,0,2:T(8,128)S(1)}, u32[]{:S(2)}, u32[]{:S(2)}) collective-permute-start(f32[3,16,1,128]{3,1,0,2:T(8,128)S(1)} %get-tuple-element.95), channel_id=1, source_target_pairs={{1,0},{2,1},{3,2},{4,3},{5,4},{6,5},{7,6},{9,8},{10,9},{11,10},{12... | collective-permute-start | bytes 73736 | tf_op jit(solution)/shard_map/ppermute | solution.py:19
  311.5 13.8 %collective-permute-done.28 = f32[3,16,16,1]{3,1,0,2:T(8,128)S(1)} collective-permute-done((f32[3,16,16,1]{3,1,0,2:T(8,128)S(1)}, f32[3,16,16,1]{3,1,0,2:T(8,128)S(1)}, u32[]{:S(2)}, u32[]{:S(2)}) %collective-permute-start.28) | collective-permute-done | bytes 3104 | tf_op jit(solution)/shard_map/ppermute | solution.py:16
  329.2 1.4 broadcast_in_dim.189
  330.6 7.9 %all-to-all-start.8 = ((f32[256,1,1]{2,1,0:T(1,128)}), f32[256,1,1]{2,1,0:T(1,128)S(1)}, u32[]{:S(2)}, u32[]{:S(2)}) async-start(f32[256,1,1]{2,1,0:T(1,128)} %broadcast_in_dim.189), calls=%async_computation.8 | async-start | bytes 262144 | tf_op jit(solution)/shard_map/all_to_all | solution.py:46
  339.4 11.0 %all-to-all-done.8 = f32[256,1,1]{2,1,0:T(1,128)S(1)} async-done(((f32[256,1,1]{2,1,0:T(1,128)}), f32[256,1,1]{2,1,0:T(1,128)S(1)}, u32[]{:S(2)}, u32[]{:S(2)}) %all-to-all-start.8) | async-done | bytes 1056 | tf_op jit(solution)/shard_map/all_to_all | solution.py:46
  (215 shorter events, 36.4 us)
Async XLA Ops:
  2.5 0.9 copy-start.25
  3.5 1.0 copy-start.7
  5.1 1.3 copy-start.32
  6.4 10.6 %copy-start.8 = (f32[16,16,128]{2,1,0:T(8,128)S(1)}, f32[16,16,128]{2,1,0:T(8,128)}, u32[]{:S(2)}) copy-start(f32[16,16,128]{2,1,0:T(8,128)} %param.21) | copy-start | bytes 393220
  6.4 57.7 %all-to-all-start = ((f32[32,3,16,128]{3,2,1,0:T(8,128)}), f32[32,3,16,128]{3,2,1,0:T(8,128)S(1)}, u32[]{:S(2)}, u32[]{:S(2)}) async-start(f32[32,3,16,128]{3,2,1,0:T(8,128)} %get-tuple-element.130), calls=%async_computation | async-start | bytes 1572864 | tf_op jit(solution)/shard_map/all_to_all | solution.py:35
  17.1 52.6 %collective-permute-start.4 = (f32[4,16,1,128]{3,2,1,0:T(1,128)S(1)}, f32[4,16,1,128]{3,2,1,0:T(1,128)S(1)}, u32[]{:S(2)}, u32[]{:S(2)}) collective-permute-start(f32[4,16,1,128]{3,2,1,0:T(1,128)S(1)} %get-tuple-element.81), channel_id=1, source_target_pairs={{0,1},{1,2},{2,3},{3,4},{4,5},{5,6},{6,7},{8,9},{9,10},{10,11},{11... | collective-permute-start | bytes 98312 | tf_op jit(solution)/shard_map/ppermute | solution.py:16
  20.5 49.1 %collective-permute-start.5 = (f32[4,16,1,128]{3,2,1,0:T(1,128)S(1)}, f32[4,16,1,128]{3,2,1,0:T(1,128)S(1)}, u32[]{:S(2)}, u32[]{:S(2)}) collective-permute-start(f32[4,16,1,128]{3,2,1,0:T(1,128)S(1)} %get-tuple-element.82), channel_id=1, source_target_pairs={{1,0},{2,1},{3,2},{4,3},{5,4},{6,5},{7,6},{9,8},{10,9},{11,10},{12... | collective-permute-start | bytes 98312 | tf_op jit(solution)/shard_map/ppermute | solution.py:19
  25.0 45.6 %collective-permute-start.6 = (f32[3,16,1,128]{3,1,0,2:T(8,128)}, f32[3,16,1,128]{3,1,0,2:T(8,128)}, u32[]{:S(2)}, u32[]{:S(2)}) collective-permute-start(f32[3,16,1,128]{3,1,0,2:T(8,128)} %get-tuple-element.125), channel_id=1, source_target_pairs={{0,1},{1,2},{2,3},{3,4},{4,5},{5,6},{6,7},{8,9},{9,10},{10,11},{11... | collective-permute-start | bytes 73736 | tf_op jit(solution)/shard_map/ppermute | solution.py:16
  27.0 6.5 %copy-start.26 = (f32[16,16,128]{2,1,0:T(8,128)S(1)}, f32[16,16,128]{2,1,0:T(8,128)}, u32[]{:S(2)}) copy-start(f32[16,16,128]{2,1,0:T(8,128)} %param.23) | copy-start | bytes 393220
  28.1 18.0 %collective-permute-start = (f32[4,16,16,1]{3,2,1,0:T(8,128)}, f32[4,16,16,1]{3,2,1,0:T(8,128)}, u32[]{:S(2)}, u32[]{:S(2)}) collective-permute-start(f32[4,16,16,1]{3,2,1,0:T(8,128)} %get-tuple-element.79), channel_id=1, source_target_pairs={{0,8},{8,16},{16,24},{24,32},{32,40},{40,48},{48,56},{56,64},{64,7... | collective-permute-start | bytes 12296 | tf_op jit(solution)/shard_map/ppermute | solution.py:16
  28.1 18.0 %collective-permute-start.1 = (f32[4,16,16,1]{3,2,1,0:T(8,128)}, f32[4,16,16,1]{3,2,1,0:T(8,128)}, u32[]{:S(2)}, u32[]{:S(2)}) collective-permute-start(f32[4,16,16,1]{3,2,1,0:T(8,128)} %get-tuple-element.80), channel_id=1, source_target_pairs={{8,0},{16,8},{24,16},{32,24},{40,32},{48,40},{56,48},{64,56},{72,6... | collective-permute-start | bytes 12296 | tf_op jit(solution)/shard_map/ppermute | solution.py:19
  34.8 133.6 %copy-start = (f32[16,16,128]{2,0,1:T(8,128)}, f32[16,16,128]{2,0,1:T(8,128)S(1)}, u32[]{:S(2)}) copy-start(f32[16,16,128]{2,0,1:T(8,128)S(1)} %copy.205) | copy-start | bytes 393220
  46.1 11.0 %collective-permute-start.2 = (f32[3,16,16,1]{3,1,0,2:T(8,128)}, f32[3,16,16,1]{3,1,0,2:T(8,128)S(1)}, u32[]{:S(2)}, u32[]{:S(2)}) collective-permute-start(f32[3,16,16,1]{3,1,0,2:T(8,128)} %get-tuple-element.122), channel_id=1, source_target_pairs={{0,8},{8,16},{16,24},{24,32},{32,40},{40,48},{48,56},{56,64},{64,7... | collective-permute-start | bytes 9224 | tf_op jit(solution)/shard_map/ppermute | solution.py:16
  46.1 16.8 %collective-permute-start.3 = (f32[3,16,16,1]{3,1,0,2:T(8,128)}, f32[3,16,16,1]{3,1,0,2:T(8,128)S(1)}, u32[]{:S(2)}, u32[]{:S(2)}) collective-permute-start(f32[3,16,16,1]{3,1,0,2:T(8,128)} %get-tuple-element.121), channel_id=1, source_target_pairs={{8,0},{16,8},{24,16},{32,24},{40,32},{48,40},{56,48},{64,56},{72,6... | collective-permute-start | bytes 9224 | tf_op jit(solution)/shard_map/ppermute | solution.py:19
  57.2 13.4 %collective-permute-start.7 = (f32[3,16,1,128]{3,1,0,2:T(8,128)}, f32[3,16,1,128]{3,1,0,2:T(8,128)}, u32[]{:S(2)}, u32[]{:S(2)}) collective-permute-start(f32[3,16,1,128]{3,1,0,2:T(8,128)} %get-tuple-element.124), channel_id=1, source_target_pairs={{1,0},{2,1},{3,2},{4,3},{5,4},{6,5},{7,6},{9,8},{10,9},{11,10},{12... | collective-permute-start | bytes 73736 | tf_op jit(solution)/shard_map/ppermute | solution.py:19
  64.1 0.9 copy-start.22
  65.0 29.4 %all-to-all-start.1 = ((f32[32,3,16,128]{3,2,1,0:T(8,128)}), f32[32,3,16,128]{3,2,1,0:T(8,128)}, u32[]{:S(2)}, u32[]{:S(2)}) async-start(f32[32,3,16,128]{3,2,1,0:T(8,128)} %get-tuple-element.131), calls=%async_computation.1 | async-start | bytes 1572864 | tf_op jit(solution)/shard_map/all_to_all | solution.py:35
  69.9 1.7 copy-start.17
  70.5 1.2 copy-start.4
  70.6 1.3 copy-start.3
  70.6 1.3 copy-start.31
  74.6 98.6 %copy-start.23 = (f32[16,128]{1,0:T(8,128)}, f32[16,128]{1,0:T(8,128)S(1)}, u32[]{:S(2)}) copy-start(f32[16,128]{1,0:T(8,128)S(1)} %subtract_bitcast_fusion.2) | copy-start | bytes 24580
  97.8 4.8 %copy-start.18 = (f32[3,16,16,128]{3,1,0,2:T(8,128)S(1)}, f32[3,16,16,128]{3,1,0,2:T(8,128)}, u32[]{:S(2)}) copy-start(f32[3,16,16,128]{3,1,0,2:T(8,128)} %get-tuple-element.91) | copy-start | bytes 1179652
  97.8 34.9 %all-to-all-start.2 = ((f32[32,3,16,128]{3,2,1,0:T(8,128)}), f32[32,3,16,128]{3,2,1,0:T(8,128)}, u32[]{:S(2)}, u32[]{:S(2)}) async-start(f32[32,3,16,128]{3,2,1,0:T(8,128)} %broadcast_select_fusion.5), calls=%async_computation.2 | async-start | bytes 1572864 | tf_op jit(solution)/shard_map/all_to_all | solution.py:35
  102.6 27.8 %collective-permute-start.11 = (f32[3,16,1,128]{3,1,0,2:T(8,128)S(1)}, f32[3,16,1,128]{3,1,0,2:T(8,128)S(1)}, u32[]{:S(2)}, u32[]{:S(2)}) collective-permute-start(f32[3,16,1,128]{3,1,0,2:T(8,128)S(1)} %slice.817), channel_id=1, source_target_pairs={{1,0},{2,1},{3,2},{4,3},{5,4},{6,5},{7,6},{9,8},{10,9},{11,10},{12... | collective-permute-start | bytes 73736 | tf_op jit(solution)/shard_map/ppermute | solution.py:19
  105.3 25.2 %collective-permute-start.10 = (f32[3,16,1,128]{3,1,0,2:T(8,128)S(1)}, f32[3,16,1,128]{3,1,0,2:T(8,128)S(1)}, u32[]{:S(2)}, u32[]{:S(2)}) collective-permute-start(f32[3,16,1,128]{3,1,0,2:T(8,128)S(1)} %fusion.161), channel_id=1, source_target_pairs={{0,1},{1,2},{2,3},{3,4},{4,5},{5,6},{6,7},{8,9},{9,10},{10,11},{11... | collective-permute-start | bytes 73736 | tf_op jit(solution)/shard_map/ppermute | solution.py:16
  108.7 21.4 %collective-permute-start.8 = (f32[3,16,16,1]{3,1,0,2:T(8,128)S(1)}, f32[3,16,16,1]{3,1,0,2:T(8,128)S(1)}, u32[]{:S(2)}, u32[]{:S(2)}) collective-permute-start(f32[3,16,16,1]{3,1,0,2:T(8,128)S(1)} %get-tuple-element.119), channel_id=1, source_target_pairs={{0,8},{8,16},{16,24},{24,32},{32,40},{40,48},{48,56},{56,64},{64,7... | collective-permute-start | bytes 9224 | tf_op jit(solution)/shard_map/ppermute | solution.py:16
  108.8 21.3 %collective-permute-start.9 = (f32[3,16,16,1]{3,1,0,2:T(8,128)S(1)}, f32[3,16,16,1]{3,1,0,2:T(8,128)S(1)}, u32[]{:S(2)}, u32[]{:S(2)}) collective-permute-start(f32[3,16,16,1]{3,1,0,2:T(8,128)S(1)} %get-tuple-element.118), channel_id=1, source_target_pairs={{8,0},{16,8},{24,16},{32,24},{40,32},{48,40},{56,48},{64,56},{72,6... | collective-permute-start | bytes 9224 | tf_op jit(solution)/shard_map/ppermute | solution.py:19
  135.4 37.0 %all-to-all-start.3 = ((f32[32,3,16,128]{3,2,1,0:T(8,128)}), f32[32,3,16,128]{3,2,1,0:T(8,128)}, u32[]{:S(2)}, u32[]{:S(2)}) async-start(f32[32,3,16,128]{3,2,1,0:T(8,128)} %broadcast_select_fusion.4), calls=%async_computation.3 | async-start | bytes 1572864 | tf_op jit(solution)/shard_map/all_to_all | solution.py:35
  140.5 27.8 %collective-permute-start.15 = (f32[3,16,1,128]{3,1,0,2:T(8,128)S(1)}, f32[3,16,1,128]{3,1,0,2:T(8,128)S(1)}, u32[]{:S(2)}, u32[]{:S(2)}) collective-permute-start(f32[3,16,1,128]{3,1,0,2:T(8,128)S(1)} %slice.838), channel_id=1, source_target_pairs={{1,0},{2,1},{3,2},{4,3},{5,4},{6,5},{7,6},{9,8},{10,9},{11,10},{12... | collective-permute-start | bytes 73736 | tf_op jit(solution)/shard_map/ppermute | solution.py:19
  143.1 25.2 %collective-permute-start.14 = (f32[3,16,1,128]{3,1,0,2:T(8,128)S(1)}, f32[3,16,1,128]{3,1,0,2:T(8,128)S(1)}, u32[]{:S(2)}, u32[]{:S(2)}) collective-permute-start(f32[3,16,1,128]{3,1,0,2:T(8,128)S(1)} %fusion.159), channel_id=1, source_target_pairs={{0,1},{1,2},{2,3},{3,4},{4,5},{5,6},{6,7},{8,9},{9,10},{10,11},{11... | collective-permute-start | bytes 73736 | tf_op jit(solution)/shard_map/ppermute | solution.py:16
  146.5 21.4 %collective-permute-start.12 = (f32[3,16,16,1]{3,1,0,2:T(8,128)S(1)}, f32[3,16,16,1]{3,1,0,2:T(8,128)S(1)}, u32[]{:S(2)}, u32[]{:S(2)}) collective-permute-start(f32[3,16,16,1]{3,1,0,2:T(8,128)S(1)} %get-tuple-element.117), channel_id=1, source_target_pairs={{0,8},{8,16},{16,24},{24,32},{32,40},{40,48},{48,56},{56,64},{64,7... | collective-permute-start | bytes 9224 | tf_op jit(solution)/shard_map/ppermute | solution.py:16
  146.8 21.2 %collective-permute-start.13 = (f32[3,16,16,1]{3,1,0,2:T(8,128)S(1)}, f32[3,16,16,1]{3,1,0,2:T(8,128)S(1)}, u32[]{:S(2)}, u32[]{:S(2)}) collective-permute-start(f32[3,16,16,1]{3,1,0,2:T(8,128)S(1)} %get-tuple-element.116), channel_id=1, source_target_pairs={{8,0},{16,8},{24,16},{32,24},{40,32},{48,40},{56,48},{64,56},{72,6... | collective-permute-start | bytes 9224 | tf_op jit(solution)/shard_map/ppermute | solution.py:19
  168.3 1.5 copy-start.5
  169.8 42.8 %collective-permute-start.19 = (f32[3,16,1,128]{3,1,0,2:T(8,128)S(1)}, f32[3,16,1,128]{3,1,0,2:T(8,128)S(1)}, u32[]{:S(2)}, u32[]{:S(2)}) collective-permute-start(f32[3,16,1,128]{3,1,0,2:T(8,128)S(1)} %slice.859), channel_id=1, source_target_pairs={{1,0},{2,1},{3,2},{4,3},{5,4},{6,5},{7,6},{9,8},{10,9},{11,10},{12... | collective-permute-start | bytes 73736 | tf_op jit(solution)/shard_map/ppermute | solution.py:19
  174.2 38.4 %collective-permute-start.18 = (f32[3,16,1,128]{3,1,0,2:T(8,128)S(1)}, f32[3,16,1,128]{3,1,0,2:T(8,128)S(1)}, u32[]{:S(2)}, u32[]{:S(2)}) collective-permute-start(f32[3,16,1,128]{3,1,0,2:T(8,128)S(1)} %fusion.157), channel_id=1, source_target_pairs={{0,1},{1,2},{2,3},{3,4},{4,5},{5,6},{6,7},{8,9},{9,10},{10,11},{11... | collective-permute-start | bytes 73736 | tf_op jit(solution)/shard_map/ppermute | solution.py:16
  179.6 35.0 %all-to-all-start.4 = ((f32[32,3,16,128]{3,2,1,0:T(8,128)}), f32[32,3,16,128]{3,2,1,0:T(8,128)}, u32[]{:S(2)}, u32[]{:S(2)}) async-start(f32[32,3,16,128]{3,2,1,0:T(8,128)} %broadcast_select_fusion.3), calls=%async_computation.4 | async-start | bytes 1572864 | tf_op jit(solution)/shard_map/all_to_all | solution.py:35
  184.8 27.3 %collective-permute-start.16 = (f32[3,16,16,1]{3,1,0,2:T(8,128)S(1)}, f32[3,16,16,1]{3,1,0,2:T(8,128)S(1)}, u32[]{:S(2)}, u32[]{:S(2)}) collective-permute-start(f32[3,16,16,1]{3,1,0,2:T(8,128)S(1)} %get-tuple-element.115), channel_id=1, source_target_pairs={{0,8},{8,16},{16,24},{24,32},{32,40},{40,48},{48,56},{56,64},{64,7... | collective-permute-start | bytes 9224 | tf_op jit(solution)/shard_map/ppermute | solution.py:16
  185.1 27.0 %collective-permute-start.17 = (f32[3,16,16,1]{3,1,0,2:T(8,128)S(1)}, f32[3,16,16,1]{3,1,0,2:T(8,128)S(1)}, u32[]{:S(2)}, u32[]{:S(2)}) collective-permute-start(f32[3,16,16,1]{3,1,0,2:T(8,128)S(1)} %get-tuple-element.114), channel_id=1, source_target_pairs={{8,0},{16,8},{24,16},{32,24},{40,32},{48,40},{56,48},{64,56},{72,6... | collective-permute-start | bytes 9224 | tf_op jit(solution)/shard_map/ppermute | solution.py:19
  212.7 1.1 copy-start.19
  213.7 1.7 copy-start.24
  214.6 1.7 copy-start.20
  215.4 0.9 copy-start.1
  219.2 34.0 %all-to-all-start.5 = ((f32[32,3,16,128]{3,2,1,0:T(8,128)}), f32[32,3,16,128]{3,2,1,0:T(8,128)}, u32[]{:S(2)}, u32[]{:S(2)}) async-start(f32[32,3,16,128]{3,2,1,0:T(8,128)} %broadcast_select_fusion.2), calls=%async_computation.5 | async-start | bytes 1572864 | tf_op jit(solution)/shard_map/all_to_all | solution.py:35
  224.2 1.0 copy-start.10
  226.2 0.9 slice-start.2
  227.4 24.4 %collective-permute-start.20 = (f32[3,16,16,1]{3,1,0,2:T(8,128)S(1)}, f32[3,16,16,1]{3,1,0,2:T(8,128)S(1)}, u32[]{:S(2)}, u32[]{:S(2)}) collective-permute-start(f32[3,16,16,1]{3,1,0,2:T(8,128)S(1)} %get-tuple-element.108), channel_id=1, source_target_pairs={{0,8},{8,16},{16,24},{24,32},{32,40},{40,48},{48,56},{56,64},{64,7... | collective-permute-start | bytes 9224 | tf_op jit(solution)/shard_map/ppermute | solution.py:16
  227.7 24.1 %collective-permute-start.21 = (f32[3,16,16,1]{3,1,0,2:T(8,128)S(1)}, f32[3,16,16,1]{3,1,0,2:T(8,128)S(1)}, u32[]{:S(2)}, u32[]{:S(2)}) collective-permute-start(f32[3,16,16,1]{3,1,0,2:T(8,128)S(1)} %get-tuple-element.107), channel_id=1, source_target_pairs={{8,0},{16,8},{24,16},{32,24},{40,32},{48,40},{56,48},{64,56},{72,6... | collective-permute-start | bytes 9224 | tf_op jit(solution)/shard_map/ppermute | solution.py:19
  232.9 19.1 %collective-permute-start.22 = (f32[3,16,1,128]{3,1,0,2:T(8,128)S(1)}, f32[3,16,1,128]{3,1,0,2:T(8,128)S(1)}, u32[]{:S(2)}, u32[]{:S(2)}) collective-permute-start(f32[3,16,1,128]{3,1,0,2:T(8,128)S(1)} %get-tuple-element.111), channel_id=1, source_target_pairs={{0,1},{1,2},{2,3},{3,4},{4,5},{5,6},{6,7},{8,9},{9,10},{10,11},{11... | collective-permute-start | bytes 73736 | tf_op jit(solution)/shard_map/ppermute | solution.py:16
  234.8 17.2 %collective-permute-start.23 = (f32[3,16,1,128]{3,1,0,2:T(8,128)S(1)}, f32[3,16,1,128]{3,1,0,2:T(8,128)S(1)}, u32[]{:S(2)}, u32[]{:S(2)}) collective-permute-start(f32[3,16,1,128]{3,1,0,2:T(8,128)S(1)} %get-tuple-element.109), channel_id=1, source_target_pairs={{1,0},{2,1},{3,2},{4,3},{5,4},{6,5},{7,6},{9,8},{10,9},{11,10},{12... | collective-permute-start | bytes 73736 | tf_op jit(solution)/shard_map/ppermute | solution.py:19
  252.1 1.0 copy-start.16
  256.0 34.1 %all-to-all-start.6 = ((f32[32,3,16,128]{3,2,1,0:T(8,128)}), f32[32,3,16,128]{3,2,1,0:T(8,128)}, u32[]{:S(2)}, u32[]{:S(2)}) async-start(f32[32,3,16,128]{3,2,1,0:T(8,128)} %broadcast_select_fusion.1), calls=%async_computation.6 | async-start | bytes 1572864 | tf_op jit(solution)/shard_map/all_to_all | solution.py:35
  261.2 27.3 %collective-permute-start.24 = (f32[3,16,16,1]{3,1,0,2:T(8,128)S(1)}, f32[3,16,16,1]{3,1,0,2:T(8,128)S(1)}, u32[]{:S(2)}, u32[]{:S(2)}) collective-permute-start(f32[3,16,16,1]{3,1,0,2:T(8,128)S(1)} %get-tuple-element.101), channel_id=1, source_target_pairs={{0,8},{8,16},{16,24},{24,32},{32,40},{40,48},{48,56},{56,64},{64,7... | collective-permute-start | bytes 9224 | tf_op jit(solution)/shard_map/ppermute | solution.py:16
  261.5 27.0 %collective-permute-start.25 = (f32[3,16,16,1]{3,1,0,2:T(8,128)S(1)}, f32[3,16,16,1]{3,1,0,2:T(8,128)S(1)}, u32[]{:S(2)}, u32[]{:S(2)}) collective-permute-start(f32[3,16,16,1]{3,1,0,2:T(8,128)S(1)} %get-tuple-element.100), channel_id=1, source_target_pairs={{8,0},{16,8},{24,16},{32,24},{40,32},{48,40},{56,48},{64,56},{72,6... | collective-permute-start | bytes 9224 | tf_op jit(solution)/shard_map/ppermute | solution.py:19
  266.7 22.1 %collective-permute-start.26 = (f32[3,16,1,128]{3,1,0,2:T(8,128)S(1)}, f32[3,16,1,128]{3,1,0,2:T(8,128)S(1)}, u32[]{:S(2)}, u32[]{:S(2)}) collective-permute-start(f32[3,16,1,128]{3,1,0,2:T(8,128)S(1)} %get-tuple-element.104), channel_id=1, source_target_pairs={{0,1},{1,2},{2,3},{3,4},{4,5},{5,6},{6,7},{8,9},{9,10},{10,11},{11... | collective-permute-start | bytes 73736 | tf_op jit(solution)/shard_map/ppermute | solution.py:16
  268.6 20.2 %collective-permute-start.27 = (f32[3,16,1,128]{3,1,0,2:T(8,128)S(1)}, f32[3,16,1,128]{3,1,0,2:T(8,128)S(1)}, u32[]{:S(2)}, u32[]{:S(2)}) collective-permute-start(f32[3,16,1,128]{3,1,0,2:T(8,128)S(1)} %get-tuple-element.102), channel_id=1, source_target_pairs={{1,0},{2,1},{3,2},{4,3},{5,4},{6,5},{7,6},{9,8},{10,9},{11,10},{12... | collective-permute-start | bytes 73736 | tf_op jit(solution)/shard_map/ppermute | solution.py:19
  288.8 1.0 copy-start.13
  292.9 34.0 %all-to-all-start.7 = ((f32[32,3,16,128]{3,2,1,0:T(8,128)}), f32[32,3,16,128]{3,2,1,0:T(8,128)}, u32[]{:S(2)}, u32[]{:S(2)}) async-start(f32[32,3,16,128]{3,2,1,0:T(8,128)} %broadcast_select_fusion), calls=%async_computation.7 | async-start | bytes 1572864 | tf_op jit(solution)/shard_map/all_to_all | solution.py:35
  298.0 27.3 %collective-permute-start.28 = (f32[3,16,16,1]{3,1,0,2:T(8,128)S(1)}, f32[3,16,16,1]{3,1,0,2:T(8,128)S(1)}, u32[]{:S(2)}, u32[]{:S(2)}) collective-permute-start(f32[3,16,16,1]{3,1,0,2:T(8,128)S(1)} %get-tuple-element.94), channel_id=1, source_target_pairs={{0,8},{8,16},{16,24},{24,32},{32,40},{40,48},{48,56},{56,64},{64,7... | collective-permute-start | bytes 9224 | tf_op jit(solution)/shard_map/ppermute | solution.py:16
  298.3 27.0 %collective-permute-start.29 = (f32[3,16,16,1]{3,1,0,2:T(8,128)S(1)}, f32[3,16,16,1]{3,1,0,2:T(8,128)S(1)}, u32[]{:S(2)}, u32[]{:S(2)}) collective-permute-start(f32[3,16,16,1]{3,1,0,2:T(8,128)S(1)} %get-tuple-element.93), channel_id=1, source_target_pairs={{8,0},{16,8},{24,16},{32,24},{40,32},{48,40},{56,48},{64,56},{72,6... | collective-permute-start | bytes 9224 | tf_op jit(solution)/shard_map/ppermute | solution.py:19
  303.6 22.1 %collective-permute-start.30 = (f32[3,16,1,128]{3,1,0,2:T(8,128)S(1)}, f32[3,16,1,128]{3,1,0,2:T(8,128)S(1)}, u32[]{:S(2)}, u32[]{:S(2)}) collective-permute-start(f32[3,16,1,128]{3,1,0,2:T(8,128)S(1)} %get-tuple-element.96), channel_id=1, source_target_pairs={{0,1},{1,2},{2,3},{3,4},{4,5},{5,6},{6,7},{8,9},{9,10},{10,11},{11... | collective-permute-start | bytes 73736 | tf_op jit(solution)/shard_map/ppermute | solution.py:16
  305.5 20.2 %collective-permute-start.31 = (f32[3,16,1,128]{3,1,0,2:T(8,128)S(1)}, f32[3,16,1,128]{3,1,0,2:T(8,128)S(1)}, u32[]{:S(2)}, u32[]{:S(2)}) collective-permute-start(f32[3,16,1,128]{3,1,0,2:T(8,128)S(1)} %get-tuple-element.95), channel_id=1, source_target_pairs={{1,0},{2,1},{3,2},{4,3},{5,4},{6,5},{7,6},{9,8},{10,9},{11,10},{12... | collective-permute-start | bytes 73736 | tf_op jit(solution)/shard_map/ppermute | solution.py:19
  325.7 1.0 copy-start.12
  330.6 19.8 %all-to-all-start.8 = ((f32[256,1,1]{2,1,0:T(1,128)}), f32[256,1,1]{2,1,0:T(1,128)S(1)}, u32[]{:S(2)}, u32[]{:S(2)}) async-start(f32[256,1,1]{2,1,0:T(1,128)} %broadcast_in_dim.189), calls=%async_computation.8 | async-start | bytes 262144 | tf_op jit(solution)/shard_map/all_to_all | solution.py:46
  (16 other events, 11.9 us)

commit v5 on v3

--- a/solution.py
+++ b/solution.py
@@ -67,8 +67,14 @@
 ):
     ocean = sea_mask.astype(jnp.float32)
     statics = jnp.stack([east_vel, north_vel, diffusivity, ocean])
-    wide_static = with_halo(statics, (("lon", 3),), 1, True)
-    tall_static = with_halo(statics, (("lat", 2),), 1, False)
+    count_static = statics.shape[0]
+    joined = jnp.concatenate([statics, tracer_start])
+    wide_joined = with_halo(joined, (("lon", 3),), 1, True)
+    tall_joined = with_halo(joined, (("lat", 2),), 1, False)
+    wide_static = wide_joined[:count_static]
+    tall_static = tall_joined[:count_static]
+    start_east_west = wide_joined[count_static:]
+    start_south_north = tall_joined[count_static:]
     west_cell = wide_static[..., :-1]
     east_cell = wide_static[..., 1:]
     east_own, east_next = upwind_pair(
@@ -83,7 +89,10 @@
         vertical_vel[:-1], 0.5 * (diffusivity[:-1] + diffusivity[1:]), ocean[:-1] * ocean[1:]
     )
     top_static = jnp.stack([north_vel[:, -1, :], diffusivity[:, -1, :], ocean[:, -1, :]])
-    across = fold_row(top_static, fold_partner)
+    top_joined = jnp.concatenate([top_static, tracer_start[:, :, -1, :]])
+    across_joined = fold_row(top_joined, fold_partner)
+    across = across_joined[: top_static.shape[0]]
+    start_partner_row = across_joined[top_static.shape[0] :]
     north_top = (lax.axis_index("lat") == lax.axis_size("lat") - 1).astype(jnp.float32)
     fold_own, fold_next = upwind_pair(
         0.5 * (top_static[0] - across[0]),
@@ -103,9 +112,14 @@
     for repeat in range(STEPS):
         advance_quantity = kept_states[-1]
         uptake = decay_rate * advance_quantity / jnp.sqrt(1.0 + advance_quantity * advance_quantity)
-        divergence_east_west, divergence_south_north, divergence_partner_row = neighbours(
-            advance_quantity
-        )
+        if repeat == 0:
+            divergence_east_west = start_east_west
+            divergence_south_north = start_south_north
+            divergence_partner_row = start_partner_row
+        else:
+            divergence_east_west, divergence_south_north, divergence_partner_row = neighbours(
+                advance_quantity
+            )
         east_flux = (
             east_own * divergence_east_west[..., :-1] + east_next * divergence_east_west[..., 1:]
         )

time: 356 us -> 326 us (0.916)
  blocking collectives: 21.5 us -> 0 us
  starting transfers between devices: 152 us -> 144 us
  local copies, waits for them, and re-layouts: 27.2 us -> 20.5 us
  waiting for transfers between devices: 108 us -> 112 us
    ppermute x16 -> x14, waiting for transfers between devices: 76.8 us -> 101 us  [with_halo(): lax.ppermute(lax.slice_in_dim(block, block.shape[dim] - width, None, axis...]
    all_to_all x1 -> x0, blocking collectives: 21.5 us -> none  [tree_sum(): got = lax.all_to_all(jnp.broadcast_to(value, (count,)), axes, 0, 0)]
    all_to_all x8 -> x7, waiting for transfers between devices: 19.2 us -> 0.02 us  [fold_row(): got = lax.all_to_all(sent, 'lon', 0, 0)]
    ppermute x16 -> x14, waiting for transfers between devices: 11.7 us -> 0.04 us  [with_halo(): lax.ppermute(lax.slice_in_dim(block, 0, width, axis=dim), axis, backward)]
    all_to_all x0 -> x1, waiting for transfers between devices: none -> 11 us  [tree_sum(): got = lax.all_to_all(jnp.broadcast_to(value, (count,)), axes, 0, 0)]
    ppermute x16 -> x14, starting transfers between devices: 77.2 us -> 67.6 us  [with_halo(): lax.ppermute(lax.slice_in_dim(block, 0, width, axis=dim), axis, backward)]
    all_to_all x0 -> x1, starting transfers between devices: none -> 9.16 us  [tree_sum(): got = lax.all_to_all(jnp.broadcast_to(value, (count,)), axes, 0, 0)]
    div x3 -> x0, other arithmetic: 8.63 us -> none  [on_device(): decay_rate / (spread * jnp.sqrt(spread)) * weight]
  transfers between devices with their start and end apart: 40 -> 36, of which waited for: 10 -> 8; matrix products, arithmetic and copies ran while one was open for 7% -> 7% of each run, Pallas kernels for 0% -> 0%
where the time goes in v5:
time: 326 us; the launch traced here: 322 us
  starting transfers between devices  144 us (44%)
  waiting for transfers between devices  112 us (34%)
  other arithmetic  41.5 us (13%)
  local copies, waits for them, and re-layouts  20.5 us (6%)
  between operations  4 us (1%)
    ppermute x14, waiting for transfers between devices, with_halo(): lax.ppermute(lax.slice_in_dim(block, block.shape[dim] - width, None, axis...  101 us
    ppermute x14, starting transfers between devices, with_halo(): lax.ppermute(lax.slice_in_dim(block, 0, width, axis=dim), axis, backward)  67.6 us
    all_to_all x7, starting transfers between devices, fold_row(): got = lax.all_to_all(sent, 'lon', 0, 0)  40.5 us
    ppermute x14, starting transfers between devices, with_halo(): lax.ppermute(lax.slice_in_dim(block, block.shape[dim] - width, None, axis...  26.3 us
    all_to_all x1, waiting for transfers between devices, tree_sum(): got = lax.all_to_all(jnp.broadcast_to(value, (count,)), axes, 0, 0)  11 us
    all_to_all x1, starting transfers between devices, tree_sum(): got = lax.all_to_all(jnp.broadcast_to(value, (count,)), axes, 0, 0)  9.16 us
    select_n x7, other arithmetic, fold_row(): sent = jnp.where(wanted, flipped[None], 0.0)  7.39 us
  transfers between devices with their start and end apart: 36, of which 8 were waited for; matrix products, arithmetic and copies ran while one was open for 7% of the time, Pallas kernels for 0%

profile of v5, /device:TPU:2, one launch (start us, length us, event | category | flops | bytes accessed | tf_op | source)
XLA Modules:
  0.0 322.0 jit_solution(1685492145274791051)
XLA Ops:
  2.4 1.0 copy.239
  5.2 1.0 bitcast_dynamic-update-slice_fusion.2
  7.6 1.3 broadcast_select_fusion
  8.9 10.5 %all-to-all-start = ((f32[32,6,16,128]{3,2,1,0:T(8,128)}), f32[32,6,16,128]{3,2,1,0:T(8,128)}, u32[]{:S(2)}, u32[]{:S(2)}) async-start(f32[32,6,16,128]{3,2,1,0:T(8,128)} %broadcast_select_fusion), calls=%async_computation | async-start | bytes 3145728 | tf_op jit(solution)/shard_map/all_to_all | solution.py:35
  20.1 3.5 %collective-permute-start.2 = (f32[7,16,1,128]{3,1,0,2:T(8,128)}, f32[7,16,1,128]{3,1,0,2:T(8,128)}, u32[]{:S(2)}, u32[]{:S(2)}) collective-permute-start(f32[7,16,1,128]{3,1,0,2:T(8,128)} %get-tuple-element.109), channel_id=1, source_target_pairs={{0,1},{1,2},{2,3},{3,4},{4,5},{5,6},{6,7},{8,9},{9,10},{10,11},{11... | collective-permute-start | bytes 172040 | tf_op jit(solution)/shard_map/ppermute | solution.py:16
  23.6 4.5 %collective-permute-start.3 = (f32[7,16,1,128]{3,1,0,2:T(8,128)}, f32[7,16,1,128]{3,1,0,2:T(8,128)}, u32[]{:S(2)}, u32[]{:S(2)}) collective-permute-start(f32[7,16,1,128]{3,1,0,2:T(8,128)} %get-tuple-element.110), channel_id=1, source_target_pairs={{1,0},{2,1},{3,2},{4,3},{5,4},{6,5},{7,6},{9,8},{10,9},{11,10},{12... | collective-permute-start | bytes 172040 | tf_op jit(solution)/shard_map/ppermute | solution.py:19
  28.0 1.2 fusion.126
  29.3 1.9 copy.241
  32.0 5.4 %collective-permute-start.1 = (f32[7,16,16,1]{2,1,3,0:T(8,128)S(1)}, f32[7,16,16,1]{2,1,3,0:T(8,128)S(1)}, u32[]{:S(2)}, u32[]{:S(2)}) collective-permute-start(f32[7,16,16,1]{2,1,3,0:T(8,128)S(1)} %copy.243), channel_id=1, source_target_pairs={{8,0},{16,8},{24,16},{32,24},{40,32},{48,40},{56,48},{64,56},{72,6... | collective-permute-start | bytes 21512 | tf_op jit(solution)/shard_map/ppermute | solution.py:19
  38.3 21.9 %collective-permute-done = f32[7,16,16,1]{2,1,3,0:T(8,128)S(1)} collective-permute-done((f32[7,16,16,1]{2,1,3,0:T(8,128)S(1)}, f32[7,16,16,1]{2,1,3,0:T(8,128)S(1)}, u32[]{:S(2)}, u32[]{:S(2)}) %collective-permute-start) | collective-permute-done | bytes 7200 | tf_op jit(solution)/shard_map/ppermute | solution.py:16
  62.0 1.2 fusion.1
  67.4 1.9 fusion.64
  69.4 1.0 broadcast_select_fusion.6
  70.4 5.0 %all-to-all-start.1 = ((f32[32,3,16,128]{3,2,1,0:T(8,128)}), f32[32,3,16,128]{3,2,1,0:T(8,128)}, u32[]{:S(2)}, u32[]{:S(2)}) async-start(f32[32,3,16,128]{3,2,1,0:T(8,128)} %broadcast_select_fusion.6), calls=%async_computation.1 | async-start | bytes 1572864 | tf_op jit(solution)/shard_map/all_to_all | solution.py:35
  75.9 5.2 %collective-permute-start.5 = (f32[3,16,16,1]{3,1,0,2:T(8,128)S(1)}, f32[3,16,16,1]{3,1,0,2:T(8,128)S(1)}, u32[]{:S(2)}, u32[]{:S(2)}) collective-permute-start(f32[3,16,16,1]{3,1,0,2:T(8,128)S(1)} %get-tuple-element.154), channel_id=1, source_target_pairs={{8,0},{16,8},{24,16},{32,24},{40,32},{48,40},{56,48},{64,56},{72,6... | collective-permute-start | bytes 9224 | tf_op jit(solution)/shard_map/ppermute | solution.py:19
  81.1 3.5 %collective-permute-start.6 = (f32[3,16,1,128]{3,1,0,2:T(8,128)S(1)}, f32[3,16,1,128]{3,1,0,2:T(8,128)S(1)}, u32[]{:S(2)}, u32[]{:S(2)}) collective-permute-start(f32[3,16,1,128]{3,1,0,2:T(8,128)S(1)} %get-tuple-element.158), channel_id=1, source_target_pairs={{0,1},{1,2},{2,3},{3,4},{4,5},{5,6},{6,7},{8,9},{9,10},{10,11},{11... | collective-permute-start | bytes 73736 | tf_op jit(solution)/shard_map/ppermute | solution.py:16
  84.6 4.5 %collective-permute-start.7 = (f32[3,16,1,128]{3,1,0,2:T(8,128)S(1)}, f32[3,16,1,128]{3,1,0,2:T(8,128)S(1)}, u32[]{:S(2)}, u32[]{:S(2)}) collective-permute-start(f32[3,16,1,128]{3,1,0,2:T(8,128)S(1)} %get-tuple-element.157), channel_id=1, source_target_pairs={{1,0},{2,1},{3,2},{4,3},{5,4},{6,5},{7,6},{9,8},{10,9},{11,10},{12... | collective-permute-start | bytes 73736 | tf_op jit(solution)/shard_map/ppermute | solution.py:19
  89.1 13.8 %collective-permute-done.4 = f32[3,16,16,1]{3,1,0,2:T(8,128)S(1)} collective-permute-done((f32[3,16,16,1]{3,1,0,2:T(8,128)S(1)}, f32[3,16,16,1]{3,1,0,2:T(8,128)S(1)}, u32[]{:S(2)}, u32[]{:S(2)}) %collective-permute-start.4) | collective-permute-done | bytes 3104 | tf_op jit(solution)/shard_map/ppermute | solution.py:16
  102.9 1.2 fusion.3
  105.1 1.7 fusion.14
  106.8 1.0 broadcast_select_fusion.5
  107.8 5.0 %all-to-all-start.2 = ((f32[32,3,16,128]{3,2,1,0:T(8,128)}), f32[32,3,16,128]{3,2,1,0:T(8,128)}, u32[]{:S(2)}, u32[]{:S(2)}) async-start(f32[32,3,16,128]{3,2,1,0:T(8,128)} %broadcast_select_fusion.5), calls=%async_computation.2 | async-start | bytes 1572864 | tf_op jit(solution)/shard_map/all_to_all | solution.py:35
  113.3 5.2 %collective-permute-start.9 = (f32[3,16,16,1]{3,1,0,2:T(8,128)S(1)}, f32[3,16,16,1]{3,1,0,2:T(8,128)S(1)}, u32[]{:S(2)}, u32[]{:S(2)}) collective-permute-start(f32[3,16,16,1]{3,1,0,2:T(8,128)S(1)} %get-tuple-element.149), channel_id=1, source_target_pairs={{8,0},{16,8},{24,16},{32,24},{40,32},{48,40},{56,48},{64,56},{72,6... | collective-permute-start | bytes 9224 | tf_op jit(solution)/shard_map/ppermute | solution.py:19
  118.6 3.5 %collective-permute-start.10 = (f32[3,16,1,128]{3,1,0,2:T(8,128)S(1)}, f32[3,16,1,128]{3,1,0,2:T(8,128)S(1)}, u32[]{:S(2)}, u32[]{:S(2)}) collective-permute-start(f32[3,16,1,128]{3,1,0,2:T(8,128)S(1)} %get-tuple-element.153), channel_id=1, source_target_pairs={{0,1},{1,2},{2,3},{3,4},{4,5},{5,6},{6,7},{8,9},{9,10},{10,11},{11... | collective-permute-start | bytes 73736 | tf_op jit(solution)/shard_map/ppermute | solution.py:16
  122.1 4.5 %collective-permute-start.11 = (f32[3,16,1,128]{3,1,0,2:T(8,128)S(1)}, f32[3,16,1,128]{3,1,0,2:T(8,128)S(1)}, u32[]{:S(2)}, u32[]{:S(2)}) collective-permute-start(f32[3,16,1,128]{3,1,0,2:T(8,128)S(1)} %get-tuple-element.152), channel_id=1, source_target_pairs={{1,0},{2,1},{3,2},{4,3},{5,4},{6,5},{7,6},{9,8},{10,9},{11,10},{12... | collective-permute-start | bytes 73736 | tf_op jit(solution)/shard_map/ppermute | solution.py:19
  126.6 13.8 %collective-permute-done.8 = f32[3,16,16,1]{3,1,0,2:T(8,128)S(1)} collective-permute-done((f32[3,16,16,1]{3,1,0,2:T(8,128)S(1)}, f32[3,16,16,1]{3,1,0,2:T(8,128)S(1)}, u32[]{:S(2)}, u32[]{:S(2)}) %collective-permute-start.8) | collective-permute-done | bytes 3104 | tf_op jit(solution)/shard_map/ppermute | solution.py:16
  140.3 1.2 fusion.4
  143.2 1.4 fusion.103
  144.6 1.9 fusion.22
  146.6 1.0 broadcast_select_fusion.4
  147.6 5.0 %all-to-all-start.3 = ((f32[32,3,16,128]{3,2,1,0:T(8,128)}), f32[32,3,16,128]{3,2,1,0:T(8,128)}, u32[]{:S(2)}, u32[]{:S(2)}) async-start(f32[32,3,16,128]{3,2,1,0:T(8,128)} %broadcast_select_fusion.4), calls=%async_computation.3 | async-start | bytes 1572864 | tf_op jit(solution)/shard_map/all_to_all | solution.py:35
  153.1 5.2 %collective-permute-start.13 = (f32[3,16,16,1]{3,1,0,2:T(8,128)S(1)}, f32[3,16,16,1]{3,1,0,2:T(8,128)S(1)}, u32[]{:S(2)}, u32[]{:S(2)}) collective-permute-start(f32[3,16,16,1]{3,1,0,2:T(8,128)S(1)} %get-tuple-element.144), channel_id=1, source_target_pairs={{8,0},{16,8},{24,16},{32,24},{40,32},{48,40},{56,48},{64,56},{72,6... | collective-permute-start | bytes 9224 | tf_op jit(solution)/shard_map/ppermute | solution.py:19
  159.0 3.5 %collective-permute-start.14 = (f32[3,16,1,128]{3,1,0,2:T(8,128)S(1)}, f32[3,16,1,128]{3,1,0,2:T(8,128)S(1)}, u32[]{:S(2)}, u32[]{:S(2)}) collective-permute-start(f32[3,16,1,128]{3,1,0,2:T(8,128)S(1)} %get-tuple-element.148), channel_id=1, source_target_pairs={{0,1},{1,2},{2,3},{3,4},{4,5},{5,6},{6,7},{8,9},{9,10},{10,11},{11... | collective-permute-start | bytes 73736 | tf_op jit(solution)/shard_map/ppermute | solution.py:16
  162.5 4.5 %collective-permute-start.15 = (f32[3,16,1,128]{3,1,0,2:T(8,128)S(1)}, f32[3,16,1,128]{3,1,0,2:T(8,128)S(1)}, u32[]{:S(2)}, u32[]{:S(2)}) collective-permute-start(f32[3,16,1,128]{3,1,0,2:T(8,128)S(1)} %get-tuple-element.147), channel_id=1, source_target_pairs={{1,0},{2,1},{3,2},{4,3},{5,4},{6,5},{7,6},{9,8},{10,9},{11,10},{12... | collective-permute-start | bytes 73736 | tf_op jit(solution)/shard_map/ppermute | solution.py:19
  167.0 13.1 %collective-permute-done.12 = f32[3,16,16,1]{3,1,0,2:T(8,128)S(1)} collective-permute-done((f32[3,16,16,1]{3,1,0,2:T(8,128)S(1)}, f32[3,16,16,1]{3,1,0,2:T(8,128)S(1)}, u32[]{:S(2)}, u32[]{:S(2)}) %collective-permute-start.12) | collective-permute-done | bytes 3104 | tf_op jit(solution)/shard_map/ppermute | solution.py:16
  180.1 1.2 fusion.5
  182.9 1.4 fusion.97
  184.3 2.4 fusion.32
  186.9 1.0 broadcast_select_fusion.3
  187.9 5.0 %all-to-all-start.4 = ((f32[32,3,16,128]{3,2,1,0:T(8,128)}), f32[32,3,16,128]{3,2,1,0:T(8,128)}, u32[]{:S(2)}, u32[]{:S(2)}) async-start(f32[32,3,16,128]{3,2,1,0:T(8,128)} %broadcast_select_fusion.3), calls=%async_computation.4 | async-start | bytes 1572864 | tf_op jit(solution)/shard_map/all_to_all | solution.py:35
  193.5 5.2 %collective-permute-start.17 = (f32[3,16,16,1]{3,1,0,2:T(8,128)S(1)}, f32[3,16,16,1]{3,1,0,2:T(8,128)S(1)}, u32[]{:S(2)}, u32[]{:S(2)}) collective-permute-start(f32[3,16,16,1]{3,1,0,2:T(8,128)S(1)} %get-tuple-element.142), channel_id=1, source_target_pairs={{8,0},{16,8},{24,16},{32,24},{40,32},{48,40},{56,48},{64,56},{72,6... | collective-permute-start | bytes 9224 | tf_op jit(solution)/shard_map/ppermute | solution.py:19
  198.7 1.0 broadcast_multiply_fusion.5
  199.6 3.5 %collective-permute-start.18 = (f32[3,16,1,128]{3,1,0,2:T(8,128)S(1)}, f32[3,16,1,128]{3,1,0,2:T(8,128)S(1)}, u32[]{:S(2)}, u32[]{:S(2)}) collective-permute-start(f32[3,16,1,128]{3,1,0,2:T(8,128)S(1)} %get-tuple-element.141), channel_id=1, source_target_pairs={{0,1},{1,2},{2,3},{3,4},{4,5},{5,6},{6,7},{8,9},{9,10},{10,11},{11... | collective-permute-start | bytes 73736 | tf_op jit(solution)/shard_map/ppermute | solution.py:16
  203.1 4.5 %collective-permute-start.19 = (f32[3,16,1,128]{3,1,0,2:T(8,128)S(1)}, f32[3,16,1,128]{3,1,0,2:T(8,128)S(1)}, u32[]{:S(2)}, u32[]{:S(2)}) collective-permute-start(f32[3,16,1,128]{3,1,0,2:T(8,128)S(1)} %get-tuple-element.140), channel_id=1, source_target_pairs={{1,0},{2,1},{3,2},{4,3},{5,4},{6,5},{7,6},{9,8},{10,9},{11,10},{12... | collective-permute-start | bytes 73736 | tf_op jit(solution)/shard_map/ppermute | solution.py:19
  207.6 12.8 %collective-permute-done.16 = f32[3,16,16,1]{3,1,0,2:T(8,128)S(1)} collective-permute-done((f32[3,16,16,1]{3,1,0,2:T(8,128)S(1)}, f32[3,16,16,1]{3,1,0,2:T(8,128)S(1)}, u32[]{:S(2)}, u32[]{:S(2)}) %collective-permute-start.16) | collective-permute-done | bytes 3104 | tf_op jit(solution)/shard_map/ppermute | solution.py:16
  221.9 1.4 fusion.36
  223.4 1.0 broadcast_select_fusion.2
  224.4 5.0 %all-to-all-start.5 = ((f32[32,3,16,128]{3,2,1,0:T(8,128)}), f32[32,3,16,128]{3,2,1,0:T(8,128)}, u32[]{:S(2)}, u32[]{:S(2)}) async-start(f32[32,3,16,128]{3,2,1,0:T(8,128)} %broadcast_select_fusion.2), calls=%async_computation.5 | async-start | bytes 1572864 | tf_op jit(solution)/shard_map/all_to_all | solution.py:35
  229.9 5.2 %collective-permute-start.21 = (f32[3,16,16,1]{3,1,0,2:T(8,128)S(1)}, f32[3,16,16,1]{3,1,0,2:T(8,128)S(1)}, u32[]{:S(2)}, u32[]{:S(2)}) collective-permute-start(f32[3,16,16,1]{3,1,0,2:T(8,128)S(1)} %get-tuple-element.135), channel_id=1, source_target_pairs={{8,0},{16,8},{24,16},{32,24},{40,32},{48,40},{56,48},{64,56},{72,6... | collective-permute-start | bytes 9224 | tf_op jit(solution)/shard_map/ppermute | solution.py:19
  235.1 1.0 broadcast_multiply_fusion.4
  236.0 3.5 %collective-permute-start.22 = (f32[3,16,1,128]{3,1,0,2:T(8,128)S(1)}, f32[3,16,1,128]{3,1,0,2:T(8,128)S(1)}, u32[]{:S(2)}, u32[]{:S(2)}) collective-permute-start(f32[3,16,1,128]{3,1,0,2:T(8,128)S(1)} %get-tuple-element.134), channel_id=1, source_target_pairs={{0,1},{1,2},{2,3},{3,4},{4,5},{5,6},{6,7},{8,9},{9,10},{10,11},{11... | collective-permute-start | bytes 73736 | tf_op jit(solution)/shard_map/ppermute | solution.py:16
  239.5 4.5 %collective-permute-start.23 = (f32[3,16,1,128]{3,1,0,2:T(8,128)S(1)}, f32[3,16,1,128]{3,1,0,2:T(8,128)S(1)}, u32[]{:S(2)}, u32[]{:S(2)}) collective-permute-start(f32[3,16,1,128]{3,1,0,2:T(8,128)S(1)} %get-tuple-element.133), channel_id=1, source_target_pairs={{1,0},{2,1},{3,2},{4,3},{5,4},{6,5},{7,6},{9,8},{10,9},{11,10},{12... | collective-permute-start | bytes 73736 | tf_op jit(solution)/shard_map/ppermute | solution.py:19
  244.0 13.0 %collective-permute-done.20 = f32[3,16,16,1]{3,1,0,2:T(8,128)S(1)} collective-permute-done((f32[3,16,16,1]{3,1,0,2:T(8,128)S(1)}, f32[3,16,16,1]{3,1,0,2:T(8,128)S(1)}, u32[]{:S(2)}, u32[]{:S(2)}) %collective-permute-start.20) | collective-permute-done | bytes 3104 | tf_op jit(solution)/shard_map/ppermute | solution.py:16
  258.4 1.4 fusion.26
  259.9 1.0 broadcast_select_fusion.1
  260.9 5.0 %all-to-all-start.6 = ((f32[32,3,16,128]{3,2,1,0:T(8,128)}), f32[32,3,16,128]{3,2,1,0:T(8,128)}, u32[]{:S(2)}, u32[]{:S(2)}) async-start(f32[32,3,16,128]{3,2,1,0:T(8,128)} %broadcast_select_fusion.1), calls=%async_computation.6 | async-start | bytes 1572864 | tf_op jit(solution)/shard_map/all_to_all | solution.py:35
  266.6 5.2 %collective-permute-start.25 = (f32[3,16,16,1]{3,1,0,2:T(8,128)S(1)}, f32[3,16,16,1]{3,1,0,2:T(8,128)S(1)}, u32[]{:S(2)}, u32[]{:S(2)}) collective-permute-start(f32[3,16,16,1]{3,1,0,2:T(8,128)S(1)} %get-tuple-element.128), channel_id=1, source_target_pairs={{8,0},{16,8},{24,16},{32,24},{40,32},{48,40},{56,48},{64,56},{72,6... | collective-permute-start | bytes 9224 | tf_op jit(solution)/shard_map/ppermute | solution.py:19
  272.6 3.5 %collective-permute-start.26 = (f32[3,16,1,128]{3,1,0,2:T(8,128)S(1)}, f32[3,16,1,128]{3,1,0,2:T(8,128)S(1)}, u32[]{:S(2)}, u32[]{:S(2)}) collective-permute-start(f32[3,16,1,128]{3,1,0,2:T(8,128)S(1)} %get-tuple-element.127), channel_id=1, source_target_pairs={{0,1},{1,2},{2,3},{3,4},{4,5},{5,6},{6,7},{8,9},{9,10},{10,11},{11... | collective-permute-start | bytes 73736 | tf_op jit(solution)/shard_map/ppermute | solution.py:16
  276.1 4.5 %collective-permute-start.27 = (f32[3,16,1,128]{3,1,0,2:T(8,128)S(1)}, f32[3,16,1,128]{3,1,0,2:T(8,128)S(1)}, u32[]{:S(2)}, u32[]{:S(2)}) collective-permute-start(f32[3,16,1,128]{3,1,0,2:T(8,128)S(1)} %get-tuple-element.126), channel_id=1, source_target_pairs={{1,0},{2,1},{3,2},{4,3},{5,4},{6,5},{7,6},{9,8},{10,9},{11,10},{12... | collective-permute-start | bytes 73736 | tf_op jit(solution)/shard_map/ppermute | solution.py:19
  280.6 12.9 %collective-permute-done.24 = f32[3,16,16,1]{3,1,0,2:T(8,128)S(1)} collective-permute-done((f32[3,16,16,1]{3,1,0,2:T(8,128)S(1)}, f32[3,16,16,1]{3,1,0,2:T(8,128)S(1)}, u32[]{:S(2)}, u32[]{:S(2)}) %collective-permute-start.24) | collective-permute-done | bytes 3104 | tf_op jit(solution)/shard_map/ppermute | solution.py:16
  294.9 2.0 multiply_reduce_fusion
  296.9 1.4 broadcast_in_dim.101
  298.2 9.2 %all-to-all-start.7 = ((f32[256,1,1]{2,1,0:T(1,128)}), f32[256,1,1]{2,1,0:T(1,128)S(1)}, u32[]{:S(2)}, u32[]{:S(2)}) async-start(f32[256,1,1]{2,1,0:T(1,128)} %broadcast_in_dim.101), calls=%async_computation.7 | async-start | bytes 262144 | tf_op jit(solution)/shard_map/all_to_all | solution.py:46
  308.3 11.0 %all-to-all-done.7 = f32[256,1,1]{2,1,0:T(1,128)S(1)} async-done(((f32[256,1,1]{2,1,0:T(1,128)}), f32[256,1,1]{2,1,0:T(1,128)S(1)}, u32[]{:S(2)}, u32[]{:S(2)}) %all-to-all-start.7) | async-done | bytes 1056 | tf_op jit(solution)/shard_map/all_to_all | solution.py:46
  (143 shorter events, 28.0 us)
Async XLA Ops:
  0.6 6.6 %copy-start.8 = (s32[16,16,128]{2,1,0:T(8,128)S(1)}, s32[16,16,128]{2,1,0:T(8,128)}, u32[]{:S(2)}) copy-start(s32[16,16,128]{2,1,0:T(8,128)} %param.31) | copy-start | bytes 393220
  0.6 6.6 %copy-start.4 = (f32[3,16,16,128]{3,2,1,0:T(8,128)S(1)}, f32[3,16,16,128]{3,2,1,0:T(8,128)}, u32[]{:S(2)}) copy-start(f32[3,16,16,128]{3,2,1,0:T(8,128)} %param.24) | copy-start | bytes 1179652
  5.2 2.2 copy-start.9
  7.4 30.1 %copy-start.3 = (f32[3,16,16,128]{3,1,0,2:T(8,128)}, f32[3,16,16,128]{3,1,0,2:T(8,128)S(1)}, u32[]{:S(2)}) copy-start(f32[3,16,16,128]{3,1,0,2:T(8,128)S(1)} %get-tuple-element.159) | copy-start | bytes 1179652
  7.6 179.3 %copy-start.12 = (pred[32]{0:T(512)(128)(4,1)}, pred[32]{0:T(512)(128)(4,1)S(1)}, u32[]{:S(2)}) copy-start(pred[32]{0:T(512)(128)(4,1)S(1)} %compare_or_fusion) | copy-start | bytes 100
  8.9 56.1 %all-to-all-start = ((f32[32,6,16,128]{3,2,1,0:T(8,128)}), f32[32,6,16,128]{3,2,1,0:T(8,128)}, u32[]{:S(2)}, u32[]{:S(2)}) async-start(f32[32,6,16,128]{3,2,1,0:T(8,128)} %broadcast_select_fusion), calls=%async_computation | async-start | bytes 3145728 | tf_op jit(solution)/shard_map/all_to_all | solution.py:35
  20.1 43.1 %collective-permute-start.2 = (f32[7,16,1,128]{3,1,0,2:T(8,128)}, f32[7,16,1,128]{3,1,0,2:T(8,128)}, u32[]{:S(2)}, u32[]{:S(2)}) collective-permute-start(f32[7,16,1,128]{3,1,0,2:T(8,128)} %get-tuple-element.109), channel_id=1, source_target_pairs={{0,1},{1,2},{2,3},{3,4},{4,5},{5,6},{6,7},{8,9},{9,10},{10,11},{11... | collective-permute-start | bytes 172040 | tf_op jit(solution)/shard_map/ppermute | solution.py:16
  23.6 39.6 %collective-permute-start.3 = (f32[7,16,1,128]{3,1,0,2:T(8,128)}, f32[7,16,1,128]{3,1,0,2:T(8,128)}, u32[]{:S(2)}, u32[]{:S(2)}) collective-permute-start(f32[7,16,1,128]{3,1,0,2:T(8,128)} %get-tuple-element.110), channel_id=1, source_target_pairs={{1,0},{2,1},{3,2},{4,3},{5,4},{6,5},{7,6},{9,8},{10,9},{11,10},{12... | collective-permute-start | bytes 172040 | tf_op jit(solution)/shard_map/ppermute | solution.py:19
  29.3 8.1 %slice-start = ((f32[16,16,128]{2,1,0:T(8,128)}), f32[15,16,128]{2,1,0:T(8,128)S(1)}, s32[]{:S(2)}) async-start(f32[16,16,128]{2,1,0:T(8,128)} %param.29), calls=%async_computation.8 | async-start | bytes 245760 | tf_op jit(solution)/shard_map/slice | solution.py:89
  31.2 29.0 %collective-permute-start = (f32[7,16,16,1]{2,1,3,0:T(8,128)S(1)}, f32[7,16,16,1]{2,1,3,0:T(8,128)S(1)}, u32[]{:S(2)}, u32[]{:S(2)}) collective-permute-start(f32[7,16,16,1]{2,1,3,0:T(8,128)S(1)} %copy.241), channel_id=1, source_target_pairs={{0,8},{8,16},{16,24},{24,32},{32,40},{40,48},{48,56},{56,64},{64,7... | collective-permute-start | bytes 21512 | tf_op jit(solution)/shard_map/ppermute | solution.py:16
  32.0 28.9 %collective-permute-start.1 = (f32[7,16,16,1]{2,1,3,0:T(8,128)S(1)}, f32[7,16,16,1]{2,1,3,0:T(8,128)S(1)}, u32[]{:S(2)}, u32[]{:S(2)}) collective-permute-start(f32[7,16,16,1]{2,1,3,0:T(8,128)S(1)} %copy.243), channel_id=1, source_target_pairs={{8,0},{16,8},{24,16},{32,24},{40,32},{48,40},{56,48},{64,56},{72,6... | collective-permute-start | bytes 21512 | tf_op jit(solution)/shard_map/ppermute | solution.py:19
  62.0 1.2 copy-start
  64.0 3.4 %copy-start.2 = (f32[3,16,16,128]{3,2,1,0:T(8,128)S(1)}, f32[3,16,16,128]{3,2,1,0:T(8,128)}, u32[]{:S(2)}) copy-start(f32[3,16,16,128]{3,2,1,0:T(8,128)} %param.25) | copy-start | bytes 1179652
  64.0 3.4 %copy-start.5 = (f32[3,16,16,128]{3,2,1,0:T(8,128)S(1)}, f32[3,16,16,128]{3,2,1,0:T(8,128)}, u32[]{:S(2)}) copy-start(f32[3,16,16,128]{3,2,1,0:T(8,128)} %param.24) | copy-start | bytes 1179652
  64.0 3.4 %copy-start.10 = (f32[3,16]{1,0:T(4,128)S(1)}, f32[3,16]{1,0:T(4,128)}, u32[]{:S(2)}) copy-start(f32[3,16]{1,0:T(4,128)} %param.32) | copy-start | bytes 580
  66.6 116.3 %copy-start.6 = (f32[16,128]{1,0:T(8,128)}, f32[16,128]{1,0:T(8,128)S(1)}, u32[]{:S(2)}) copy-start(f32[16,128]{1,0:T(8,128)S(1)} %get-tuple-element.99) | copy-start | bytes 24580
  70.4 33.8 %all-to-all-start.1 = ((f32[32,3,16,128]{3,2,1,0:T(8,128)}), f32[32,3,16,128]{3,2,1,0:T(8,128)}, u32[]{:S(2)}, u32[]{:S(2)}) async-start(f32[32,3,16,128]{3,2,1,0:T(8,128)} %broadcast_select_fusion.6), calls=%async_computation.1 | async-start | bytes 1572864 | tf_op jit(solution)/shard_map/all_to_all | solution.py:35
  75.4 27.5 %copy-start.1 = (f32[16,16,129]{2,0,1:T(8,128)S(1)}, f32[16,16,129]{2,0,1:T(8,128)}, u32[]{:S(2)}) copy-start(f32[16,16,129]{2,0,1:T(8,128)} %copy-done) | copy-start | bytes 396292
  75.6 27.3 %collective-permute-start.4 = (f32[3,16,16,1]{3,1,0,2:T(8,128)S(1)}, f32[3,16,16,1]{3,1,0,2:T(8,128)S(1)}, u32[]{:S(2)}, u32[]{:S(2)}) collective-permute-start(f32[3,16,16,1]{3,1,0,2:T(8,128)S(1)} %get-tuple-element.155), channel_id=1, source_target_pairs={{0,8},{8,16},{16,24},{24,32},{32,40},{40,48},{48,56},{56,64},{64,7... | collective-permute-start | bytes 9224 | tf_op jit(solution)/shard_map/ppermute | solution.py:16
  75.9 27.0 %collective-permute-start.5 = (f32[3,16,16,1]{3,1,0,2:T(8,128)S(1)}, f32[3,16,16,1]{3,1,0,2:T(8,128)S(1)}, u32[]{:S(2)}, u32[]{:S(2)}) collective-permute-start(f32[3,16,16,1]{3,1,0,2:T(8,128)S(1)} %get-tuple-element.154), channel_id=1, source_target_pairs={{8,0},{16,8},{24,16},{32,24},{40,32},{48,40},{56,48},{64,56},{72,6... | collective-permute-start | bytes 9224 | tf_op jit(solution)/shard_map/ppermute | solution.py:19
  81.1 23.0 %collective-permute-start.6 = (f32[3,16,1,128]{3,1,0,2:T(8,128)S(1)}, f32[3,16,1,128]{3,1,0,2:T(8,128)S(1)}, u32[]{:S(2)}, u32[]{:S(2)}) collective-permute-start(f32[3,16,1,128]{3,1,0,2:T(8,128)S(1)} %get-tuple-element.158), channel_id=1, source_target_pairs={{0,1},{1,2},{2,3},{3,4},{4,5},{5,6},{6,7},{8,9},{9,10},{10,11},{11... | collective-permute-start | bytes 73736 | tf_op jit(solution)/shard_map/ppermute | solution.py:16
  84.6 19.5 %collective-permute-start.7 = (f32[3,16,1,128]{3,1,0,2:T(8,128)S(1)}, f32[3,16,1,128]{3,1,0,2:T(8,128)S(1)}, u32[]{:S(2)}, u32[]{:S(2)}) collective-permute-start(f32[3,16,1,128]{3,1,0,2:T(8,128)S(1)} %get-tuple-element.157), channel_id=1, source_target_pairs={{1,0},{2,1},{3,2},{4,3},{5,4},{6,5},{7,6},{9,8},{10,9},{11,10},{12... | collective-permute-start | bytes 73736 | tf_op jit(solution)/shard_map/ppermute | solution.py:19
  107.8 34.6 %all-to-all-start.2 = ((f32[32,3,16,128]{3,2,1,0:T(8,128)}), f32[32,3,16,128]{3,2,1,0:T(8,128)}, u32[]{:S(2)}, u32[]{:S(2)}) async-start(f32[32,3,16,128]{3,2,1,0:T(8,128)} %broadcast_select_fusion.5), calls=%async_computation.2 | async-start | bytes 1572864 | tf_op jit(solution)/shard_map/all_to_all | solution.py:35
  113.0 27.3 %collective-permute-start.8 = (f32[3,16,16,1]{3,1,0,2:T(8,128)S(1)}, f32[3,16,16,1]{3,1,0,2:T(8,128)S(1)}, u32[]{:S(2)}, u32[]{:S(2)}) collective-permute-start(f32[3,16,16,1]{3,1,0,2:T(8,128)S(1)} %get-tuple-element.150), channel_id=1, source_target_pairs={{0,8},{8,16},{16,24},{24,32},{32,40},{40,48},{48,56},{56,64},{64,7... | collective-permute-start | bytes 9224 | tf_op jit(solution)/shard_map/ppermute | solution.py:16
  113.3 27.0 %collective-permute-start.9 = (f32[3,16,16,1]{3,1,0,2:T(8,128)S(1)}, f32[3,16,16,1]{3,1,0,2:T(8,128)S(1)}, u32[]{:S(2)}, u32[]{:S(2)}) collective-permute-start(f32[3,16,16,1]{3,1,0,2:T(8,128)S(1)} %get-tuple-element.149), channel_id=1, source_target_pairs={{8,0},{16,8},{24,16},{32,24},{40,32},{48,40},{56,48},{64,56},{72,6... | collective-permute-start | bytes 9224 | tf_op jit(solution)/shard_map/ppermute | solution.py:19
  118.6 23.0 %collective-permute-start.10 = (f32[3,16,1,128]{3,1,0,2:T(8,128)S(1)}, f32[3,16,1,128]{3,1,0,2:T(8,128)S(1)}, u32[]{:S(2)}, u32[]{:S(2)}) collective-permute-start(f32[3,16,1,128]{3,1,0,2:T(8,128)S(1)} %get-tuple-element.153), channel_id=1, source_target_pairs={{0,1},{1,2},{2,3},{3,4},{4,5},{5,6},{6,7},{8,9},{9,10},{10,11},{11... | collective-permute-start | bytes 73736 | tf_op jit(solution)/shard_map/ppermute | solution.py:16
  122.1 19.5 %collective-permute-start.11 = (f32[3,16,1,128]{3,1,0,2:T(8,128)S(1)}, f32[3,16,1,128]{3,1,0,2:T(8,128)S(1)}, u32[]{:S(2)}, u32[]{:S(2)}) collective-permute-start(f32[3,16,1,128]{3,1,0,2:T(8,128)S(1)} %get-tuple-element.152), channel_id=1, source_target_pairs={{1,0},{2,1},{3,2},{4,3},{5,4},{6,5},{7,6},{9,8},{10,9},{11,10},{12... | collective-permute-start | bytes 73736 | tf_op jit(solution)/shard_map/ppermute | solution.py:19
  147.6 34.6 %all-to-all-start.3 = ((f32[32,3,16,128]{3,2,1,0:T(8,128)}), f32[32,3,16,128]{3,2,1,0:T(8,128)}, u32[]{:S(2)}, u32[]{:S(2)}) async-start(f32[32,3,16,128]{3,2,1,0:T(8,128)} %broadcast_select_fusion.4), calls=%async_computation.3 | async-start | bytes 1572864 | tf_op jit(solution)/shard_map/all_to_all | solution.py:35
  152.8 27.3 %collective-permute-start.12 = (f32[3,16,16,1]{3,1,0,2:T(8,128)S(1)}, f32[3,16,16,1]{3,1,0,2:T(8,128)S(1)}, u32[]{:S(2)}, u32[]{:S(2)}) collective-permute-start(f32[3,16,16,1]{3,1,0,2:T(8,128)S(1)} %get-tuple-element.145), channel_id=1, source_target_pairs={{0,8},{8,16},{16,24},{24,32},{32,40},{40,48},{48,56},{56,64},{64,7... | collective-permute-start | bytes 9224 | tf_op jit(solution)/shard_map/ppermute | solution.py:16
  153.1 27.0 %collective-permute-start.13 = (f32[3,16,16,1]{3,1,0,2:T(8,128)S(1)}, f32[3,16,16,1]{3,1,0,2:T(8,128)S(1)}, u32[]{:S(2)}, u32[]{:S(2)}) collective-permute-start(f32[3,16,16,1]{3,1,0,2:T(8,128)S(1)} %get-tuple-element.144), channel_id=1, source_target_pairs={{8,0},{16,8},{24,16},{32,24},{40,32},{48,40},{56,48},{64,56},{72,6... | collective-permute-start | bytes 9224 | tf_op jit(solution)/shard_map/ppermute | solution.py:19
  159.0 22.3 %collective-permute-start.14 = (f32[3,16,1,128]{3,1,0,2:T(8,128)S(1)}, f32[3,16,1,128]{3,1,0,2:T(8,128)S(1)}, u32[]{:S(2)}, u32[]{:S(2)}) collective-permute-start(f32[3,16,1,128]{3,1,0,2:T(8,128)S(1)} %get-tuple-element.148), channel_id=1, source_target_pairs={{0,1},{1,2},{2,3},{3,4},{4,5},{5,6},{6,7},{8,9},{9,10},{10,11},{11... | collective-permute-start | bytes 73736 | tf_op jit(solution)/shard_map/ppermute | solution.py:16
  162.5 18.8 %collective-permute-start.15 = (f32[3,16,1,128]{3,1,0,2:T(8,128)S(1)}, f32[3,16,1,128]{3,1,0,2:T(8,128)S(1)}, u32[]{:S(2)}, u32[]{:S(2)}) collective-permute-start(f32[3,16,1,128]{3,1,0,2:T(8,128)S(1)} %get-tuple-element.147), channel_id=1, source_target_pairs={{1,0},{2,1},{3,2},{4,3},{5,4},{6,5},{7,6},{9,8},{10,9},{11,10},{12... | collective-permute-start | bytes 73736 | tf_op jit(solution)/shard_map/ppermute | solution.py:19
  187.9 33.1 %all-to-all-start.4 = ((f32[32,3,16,128]{3,2,1,0:T(8,128)}), f32[32,3,16,128]{3,2,1,0:T(8,128)}, u32[]{:S(2)}, u32[]{:S(2)}) async-start(f32[32,3,16,128]{3,2,1,0:T(8,128)} %broadcast_select_fusion.3), calls=%async_computation.4 | async-start | bytes 1572864 | tf_op jit(solution)/shard_map/all_to_all | solution.py:35
  193.2 27.2 %collective-permute-start.16 = (f32[3,16,16,1]{3,1,0,2:T(8,128)S(1)}, f32[3,16,16,1]{3,1,0,2:T(8,128)S(1)}, u32[]{:S(2)}, u32[]{:S(2)}) collective-permute-start(f32[3,16,16,1]{3,1,0,2:T(8,128)S(1)} %get-tuple-element.143), channel_id=1, source_target_pairs={{0,8},{8,16},{16,24},{24,32},{32,40},{40,48},{48,56},{56,64},{64,7... | collective-permute-start | bytes 9224 | tf_op jit(solution)/shard_map/ppermute | solution.py:16
  193.5 26.9 %collective-permute-start.17 = (f32[3,16,16,1]{3,1,0,2:T(8,128)S(1)}, f32[3,16,16,1]{3,1,0,2:T(8,128)S(1)}, u32[]{:S(2)}, u32[]{:S(2)}) collective-permute-start(f32[3,16,16,1]{3,1,0,2:T(8,128)S(1)} %get-tuple-element.142), channel_id=1, source_target_pairs={{8,0},{16,8},{24,16},{32,24},{40,32},{48,40},{56,48},{64,56},{72,6... | collective-permute-start | bytes 9224 | tf_op jit(solution)/shard_map/ppermute | solution.py:19
  199.6 21.1 %collective-permute-start.18 = (f32[3,16,1,128]{3,1,0,2:T(8,128)S(1)}, f32[3,16,1,128]{3,1,0,2:T(8,128)S(1)}, u32[]{:S(2)}, u32[]{:S(2)}) collective-permute-start(f32[3,16,1,128]{3,1,0,2:T(8,128)S(1)} %get-tuple-element.141), channel_id=1, source_target_pairs={{0,1},{1,2},{2,3},{3,4},{4,5},{5,6},{6,7},{8,9},{9,10},{10,11},{11... | collective-permute-start | bytes 73736 | tf_op jit(solution)/shard_map/ppermute | solution.py:16
  203.1 17.6 %collective-permute-start.19 = (f32[3,16,1,128]{3,1,0,2:T(8,128)S(1)}, f32[3,16,1,128]{3,1,0,2:T(8,128)S(1)}, u32[]{:S(2)}, u32[]{:S(2)}) collective-permute-start(f32[3,16,1,128]{3,1,0,2:T(8,128)S(1)} %get-tuple-element.140), channel_id=1, source_target_pairs={{1,0},{2,1},{3,2},{4,3},{5,4},{6,5},{7,6},{9,8},{10,9},{11,10},{12... | collective-permute-start | bytes 73736 | tf_op jit(solution)/shard_map/ppermute | solution.py:19
  220.7 1.1 copy-start.7
  220.8 1.2 copy-start.11
  221.0 2.4 copy-start.13
  224.4 33.1 %all-to-all-start.5 = ((f32[32,3,16,128]{3,2,1,0:T(8,128)}), f32[32,3,16,128]{3,2,1,0:T(8,128)}, u32[]{:S(2)}, u32[]{:S(2)}) async-start(f32[32,3,16,128]{3,2,1,0:T(8,128)} %broadcast_select_fusion.2), calls=%async_computation.5 | async-start | bytes 1572864 | tf_op jit(solution)/shard_map/all_to_all | solution.py:35
  229.6 27.3 %collective-permute-start.20 = (f32[3,16,16,1]{3,1,0,2:T(8,128)S(1)}, f32[3,16,16,1]{3,1,0,2:T(8,128)S(1)}, u32[]{:S(2)}, u32[]{:S(2)}) collective-permute-start(f32[3,16,16,1]{3,1,0,2:T(8,128)S(1)} %get-tuple-element.136), channel_id=1, source_target_pairs={{0,8},{8,16},{16,24},{24,32},{32,40},{40,48},{48,56},{56,64},{64,7... | collective-permute-start | bytes 9224 | tf_op jit(solution)/shard_map/ppermute | solution.py:16
  229.9 27.0 %collective-permute-start.21 = (f32[3,16,16,1]{3,1,0,2:T(8,128)S(1)}, f32[3,16,16,1]{3,1,0,2:T(8,128)S(1)}, u32[]{:S(2)}, u32[]{:S(2)}) collective-permute-start(f32[3,16,16,1]{3,1,0,2:T(8,128)S(1)} %get-tuple-element.135), channel_id=1, source_target_pairs={{8,0},{16,8},{24,16},{32,24},{40,32},{48,40},{56,48},{64,56},{72,6... | collective-permute-start | bytes 9224 | tf_op jit(solution)/shard_map/ppermute | solution.py:19
  236.0 21.2 %collective-permute-start.22 = (f32[3,16,1,128]{3,1,0,2:T(8,128)S(1)}, f32[3,16,1,128]{3,1,0,2:T(8,128)S(1)}, u32[]{:S(2)}, u32[]{:S(2)}) collective-permute-start(f32[3,16,1,128]{3,1,0,2:T(8,128)S(1)} %get-tuple-element.134), channel_id=1, source_target_pairs={{0,1},{1,2},{2,3},{3,4},{4,5},{5,6},{6,7},{8,9},{9,10},{10,11},{11... | collective-permute-start | bytes 73736 | tf_op jit(solution)/shard_map/ppermute | solution.py:16
  239.5 17.7 %collective-permute-start.23 = (f32[3,16,1,128]{3,1,0,2:T(8,128)S(1)}, f32[3,16,1,128]{3,1,0,2:T(8,128)S(1)}, u32[]{:S(2)}, u32[]{:S(2)}) collective-permute-start(f32[3,16,1,128]{3,1,0,2:T(8,128)S(1)} %get-tuple-element.133), channel_id=1, source_target_pairs={{1,0},{2,1},{3,2},{4,3},{5,4},{6,5},{7,6},{9,8},{10,9},{11,10},{12... | collective-permute-start | bytes 73736 | tf_op jit(solution)/shard_map/ppermute | solution.py:19
  260.9 33.1 %all-to-all-start.6 = ((f32[32,3,16,128]{3,2,1,0:T(8,128)}), f32[32,3,16,128]{3,2,1,0:T(8,128)}, u32[]{:S(2)}, u32[]{:S(2)}) async-start(f32[32,3,16,128]{3,2,1,0:T(8,128)} %broadcast_select_fusion.1), calls=%async_computation.6 | async-start | bytes 1572864 | tf_op jit(solution)/shard_map/all_to_all | solution.py:35
  266.1 27.3 %collective-permute-start.24 = (f32[3,16,16,1]{3,1,0,2:T(8,128)S(1)}, f32[3,16,16,1]{3,1,0,2:T(8,128)S(1)}, u32[]{:S(2)}, u32[]{:S(2)}) collective-permute-start(f32[3,16,16,1]{3,1,0,2:T(8,128)S(1)} %get-tuple-element.129), channel_id=1, source_target_pairs={{0,8},{8,16},{16,24},{24,32},{32,40},{40,48},{48,56},{56,64},{64,7... | collective-permute-start | bytes 9224 | tf_op jit(solution)/shard_map/ppermute | solution.py:16
  266.6 26.8 %collective-permute-start.25 = (f32[3,16,16,1]{3,1,0,2:T(8,128)S(1)}, f32[3,16,16,1]{3,1,0,2:T(8,128)S(1)}, u32[]{:S(2)}, u32[]{:S(2)}) collective-permute-start(f32[3,16,16,1]{3,1,0,2:T(8,128)S(1)} %get-tuple-element.128), channel_id=1, source_target_pairs={{8,0},{16,8},{24,16},{32,24},{40,32},{48,40},{56,48},{64,56},{72,6... | collective-permute-start | bytes 9224 | tf_op jit(solution)/shard_map/ppermute | solution.py:19
  272.6 21.1 %collective-permute-start.26 = (f32[3,16,1,128]{3,1,0,2:T(8,128)S(1)}, f32[3,16,1,128]{3,1,0,2:T(8,128)S(1)}, u32[]{:S(2)}, u32[]{:S(2)}) collective-permute-start(f32[3,16,1,128]{3,1,0,2:T(8,128)S(1)} %get-tuple-element.127), channel_id=1, source_target_pairs={{0,1},{1,2},{2,3},{3,4},{4,5},{5,6},{6,7},{8,9},{9,10},{10,11},{11... | collective-permute-start | bytes 73736 | tf_op jit(solution)/shard_map/ppermute | solution.py:16
  276.1 17.7 %collective-permute-start.27 = (f32[3,16,1,128]{3,1,0,2:T(8,128)S(1)}, f32[3,16,1,128]{3,1,0,2:T(8,128)S(1)}, u32[]{:S(2)}, u32[]{:S(2)}) collective-permute-start(f32[3,16,1,128]{3,1,0,2:T(8,128)S(1)} %get-tuple-element.126), channel_id=1, source_target_pairs={{1,0},{2,1},{3,2},{4,3},{5,4},{6,5},{7,6},{9,8},{10,9},{11,10},{12... | collective-permute-start | bytes 73736 | tf_op jit(solution)/shard_map/ppermute | solution.py:19
  298.2 21.0 %all-to-all-start.7 = ((f32[256,1,1]{2,1,0:T(1,128)}), f32[256,1,1]{2,1,0:T(1,128)S(1)}, u32[]{:S(2)}, u32[]{:S(2)}) async-start(f32[256,1,1]{2,1,0:T(1,128)} %broadcast_in_dim.101), calls=%async_computation.7 | async-start | bytes 262144 | tf_op jit(solution)/shard_map/all_to_all | solution.py:46

commit v6 on v5

--- a/solution.py
+++ b/solution.py
@@ -108,6 +108,19 @@
         partner_row = fold_row(top_row, fold_partner)
         return (east_west, south_north, partner_row)
 
+    def combine(quantity, east_flux, north_flux, vertical_part, uptake, forcing, sea):
+        return sea * (
+            quantity
+            - (
+                east_flux[..., 1:]
+                - east_flux[..., :-1]
+                + (north_flux[:, :, 1:, :] - north_flux[:, :, :-1, :])
+                + vertical_part
+            )
+            - uptake
+            + forcing
+        )
+
     kept_states = [tracer_start]
     for repeat in range(STEPS):
         advance_quantity = kept_states[-1]
@@ -127,28 +140,27 @@
             north_own * divergence_south_north[:, :, :-1, :]
             + north_next * divergence_south_north[:, :, 1:, :]
         )
-        divergence_top_row = advance_quantity[:, :, -1, :]
-        fold_flux = fold_own * divergence_top_row + fold_next * divergence_partner_row
-        north_flux = north_flux.at[:, :, -1, :].add(fold_flux)
         up_flux = up_own * advance_quantity[:, :-1] + up_next * advance_quantity[:, 1:]
         zero_level = jnp.zeros_like(advance_quantity[:, :1])
         vertical_part = jnp.concatenate([up_flux, zero_level], 1) - jnp.concatenate(
             [zero_level, up_flux], 1
         )
-        kept_states.append(
-            ocean
-            * (
-                advance_quantity
-                - (
-                    east_flux[..., 1:]
-                    - east_flux[..., :-1]
-                    + (north_flux[:, :, 1:, :] - north_flux[:, :, :-1, :])
-                    + vertical_part
-                )
-                - uptake
-                + source
-            )
-        )
+        main = combine(
+            advance_quantity, east_flux, north_flux, vertical_part, uptake, source, ocean
+        )
+        divergence_top_row = advance_quantity[:, :, -1, :]
+        fold_flux = fold_own * divergence_top_row + fold_next * divergence_partner_row
+        top_north = north_flux[:, :, -2:, :].at[:, :, -1, :].add(fold_flux)
+        top = combine(
+            advance_quantity[:, :, -1:],
+            east_flux[:, :, -1:],
+            top_north,
+            vertical_part[:, :, -1:],
+            uptake[:, :, -1:],
+            source[:, :, -1:],
+            ocean[:, -1:],
+        )
+        kept_states.append(jnp.concatenate([main[:, :, :-1], top], axis=2))
     last_state = kept_states[-1]
     adjoint = ocean * (last_state - target)
     source_grad = ocean * adjoint
@@ -164,16 +176,22 @@
             north_own[:, 1:, :] * north_diff[:, :, 1:, :]
             + north_next[:, :-1, :] * north_diff[:, :, :-1, :]
         )
-        result = result.at[:, :, -1, :].add(
+        transposed_zero_level = jnp.zeros_like(weight[:, :1])
+        up_part = jnp.concatenate([up_own * up_diff, transposed_zero_level], 1) + jnp.concatenate(
+            [transposed_zero_level, up_next * up_diff], 1
+        )
+        spread = 1.0 + current * current
+        damping = decay_rate / (spread * jnp.sqrt(spread))
+        main = weight - (result + up_part) - damping * weight
+        top_result = result[:, :, -1:, :] + (
             fold_own * (weight[:, :, -1, :] - transposed_partner_row)
-        )
-        transposed_zero_level = jnp.zeros_like(weight[:, :1])
-        result = result + (
-            jnp.concatenate([up_own * up_diff, transposed_zero_level], 1)
-            + jnp.concatenate([transposed_zero_level, up_next * up_diff], 1)
-        )
-        spread = 1.0 + current * current
-        adjoint = weight - result - decay_rate / (spread * jnp.sqrt(spread)) * weight
+        )[:, :, None, :]
+        top = (
+            weight[:, :, -1:]
+            - (top_result + up_part[:, :, -1:])
+            - damping[:, :, -1:] * weight[:, :, -1:]
+        )
+        adjoint = jnp.concatenate([main[:, :, :-1], top], axis=2)
         source_grad = source_grad + ocean * adjoint
     squares = tree_sum(jnp.sum(source_grad * source_grad), ("lon", "lat"))
     return (source_grad, jnp.sqrt(squares))

time: 326 us -> 331 us (1.015)
  waiting for transfers between devices: 112 us -> 125 us
  other arithmetic: 41.5 us -> 33.3 us
  local copies, waits for them, and re-layouts: 20.5 us -> 24.8 us
  starting transfers between devices: 144 us -> 140 us
    ppermute x14, waiting for transfers between devices: 0.04 us -> 56.3 us  [with_halo(): lax.ppermute(lax.slice_in_dim(block, 0, width, axis=dim), axis, backward)]
    ppermute x14, waiting for transfers between devices: 101 us -> 57.3 us  [with_halo(): lax.ppermute(lax.slice_in_dim(block, block.shape[dim] - width, None, axis...]
    ppermute x14, starting transfers between devices: 26.3 us -> 15.1 us  [with_halo(): lax.ppermute(lax.slice_in_dim(block, block.shape[dim] - width, None, axis...]
    ppermute x14, starting transfers between devices: 67.6 us -> 75.2 us  [with_halo(): lax.ppermute(lax.slice_in_dim(block, 0, width, axis=dim), axis, backward)]
    unnamed x35 -> x58, local copies, waits for them, and re-layouts: 5.87 us -> 10 us
    scatter-add x7 -> x0, other arithmetic: 3.95 us -> none  [the longest x4 3.69 us: on_device(): north_flux = north_flux.at[:, :, -1, :].add(fold_flux)]
    div x0 -> x3, other arithmetic: none -> 3.72 us  [on_device(): damping = decay_rate / (spread * jnp.sqrt(spread))]
    add x4, other arithmetic: 4.69 us -> 1.21 us  [on_device(): east_own * divergence_east_west[..., :-1]]
  transfers between devices with their start and end apart: 36 -> 36, of which waited for: 8 -> 14; matrix products, arithmetic and copies ran while one was open for 7% -> 8% of each run, Pallas kernels for 0% -> 0%
where the time goes in v6:
time: 331 us; the launch traced here: 327 us
  starting transfers between devices  140 us (42%)
  waiting for transfers between devices  125 us (38%)
  other arithmetic  33.3 us (10%)
  local copies, waits for them, and re-layouts  24.8 us (7%)
  between operations  4.25 us (1%)
    ppermute x14, starting transfers between devices, with_halo(): lax.ppermute(lax.slice_in_dim(block, 0, width, axis=dim), axis, backward)  75.2 us
    ppermute x14, waiting for transfers between devices, with_halo(): lax.ppermute(lax.slice_in_dim(block, block.shape[dim] - width, None, axis...  57.3 us
    ppermute x14, waiting for transfers between devices, with_halo(): lax.ppermute(lax.slice_in_dim(block, 0, width, axis=dim), axis, backward)  56.3 us
    all_to_all x7, starting transfers between devices, fold_row(): got = lax.all_to_all(sent, 'lon', 0, 0)  40.1 us
    ppermute x14, starting transfers between devices, with_halo(): lax.ppermute(lax.slice_in_dim(block, block.shape[dim] - width, None, axis...  15.1 us
    all_to_all x1, waiting for transfers between devices, tree_sum(): got = lax.all_to_all(jnp.broadcast_to(value, (count,)), axes, 0, 0)  11 us
    unnamed x58, local copies, waits for them, and re-layouts  10 us
    all_to_all x1, starting transfers between devices, tree_sum(): got = lax.all_to_all(jnp.broadcast_to(value, (count,)), axes, 0, 0)  9.59 us
  transfers between devices with their start and end apart: 36, of which 14 were waited for; matrix products, arithmetic and copies ran while one was open for 8% of the time, Pallas kernels for 0%

profile of v6, /device:TPU:2, one launch (start us, length us, event | category | flops | bytes accessed | tf_op | source)
XLA Modules:
  0.0 326.9 jit_solution(10736040513000494729)
XLA Ops:
  2.4 1.0 copy.239
  3.4 1.0 copy.238
  4.4 1.0 bitcast_dynamic-update-slice_fusion.3
  7.7 1.3 broadcast_select_fusion
  9.0 10.5 %all-to-all-start = ((f32[32,6,16,128]{3,2,1,0:T(8,128)}), f32[32,6,16,128]{3,2,1,0:T(8,128)}, u32[]{:S(2)}, u32[]{:S(2)}) async-start(f32[32,6,16,128]{3,2,1,0:T(8,128)} %broadcast_select_fusion), calls=%async_computation | async-start | bytes 3145728 | tf_op jit(solution)/shard_map/all_to_all | solution.py:35
  20.2 3.5 %collective-permute-start.2 = (f32[7,16,1,128]{3,1,0,2:T(8,128)}, f32[7,16,1,128]{3,1,0,2:T(8,128)}, u32[]{:S(2)}, u32[]{:S(2)}) collective-permute-start(f32[7,16,1,128]{3,1,0,2:T(8,128)} %get-tuple-element.73), channel_id=1, source_target_pairs={{0,1},{1,2},{2,3},{3,4},{4,5},{5,6},{6,7},{8,9},{9,10},{10,11},{11... | collective-permute-start | bytes 172040 | tf_op jit(solution)/shard_map/ppermute | solution.py:16
  23.7 4.5 %collective-permute-start.3 = (f32[7,16,1,128]{3,1,0,2:T(8,128)}, f32[7,16,1,128]{3,1,0,2:T(8,128)}, u32[]{:S(2)}, u32[]{:S(2)}) collective-permute-start(f32[7,16,1,128]{3,1,0,2:T(8,128)} %get-tuple-element.74), channel_id=1, source_target_pairs={{1,0},{2,1},{3,2},{4,3},{5,4},{6,5},{7,6},{9,8},{10,9},{11,10},{12... | collective-permute-start | bytes 172040 | tf_op jit(solution)/shard_map/ppermute | solution.py:19
  28.5 1.3 copy.243
  29.8 4.6 %collective-permute-start.1 = (f32[7,16,16,1]{2,1,3,0:T(8,128)}, f32[7,16,16,1]{2,1,3,0:T(8,128)S(1)}, u32[]{:S(2)}, u32[]{:S(2)}) collective-permute-start(f32[7,16,16,1]{2,1,3,0:T(8,128)} %copy.243), channel_id=1, source_target_pairs={{8,0},{16,8},{24,16},{32,24},{40,32},{48,40},{56,48},{64,56},{72,6... | collective-permute-start | bytes 21512 | tf_op jit(solution)/shard_map/ppermute | solution.py:19
  35.2 1.1 maximum_add_fusion.2
  37.1 23.2 %collective-permute-done = f32[7,16,16,1]{2,1,3,0:T(8,128)S(1)} collective-permute-done((f32[7,16,16,1]{2,1,3,0:T(8,128)S(1)}, f32[7,16,16,1]{2,1,3,0:T(8,128)S(1)}, u32[]{:S(2)}, u32[]{:S(2)}) %collective-permute-start) | collective-permute-done | bytes 7200 | tf_op jit(solution)/shard_map/ppermute | solution.py:16
  62.9 1.1 add_bitcast_fusion.1
  64.9 1.3 fusion.63
  69.0 1.0 broadcast_select_fusion.6
  70.0 5.0 %all-to-all-start.1 = ((f32[32,3,16,128]{3,2,1,0:T(8,128)}), f32[32,3,16,128]{3,2,1,0:T(8,128)}, u32[]{:S(2)}, u32[]{:S(2)}) async-start(f32[32,3,16,128]{3,2,1,0:T(8,128)} %broadcast_select_fusion.6), calls=%async_computation.1 | async-start | bytes 1572864 | tf_op jit(solution)/shard_map/all_to_all | solution.py:35
  75.8 1.0 slice.826
  76.8 5.8 %collective-permute-start.7 = (f32[3,16,1,128]{3,1,0,2:T(8,128)S(1)}, f32[3,16,1,128]{3,1,0,2:T(8,128)S(1)}, u32[]{:S(2)}, u32[]{:S(2)}) collective-permute-start(f32[3,16,1,128]{3,1,0,2:T(8,128)S(1)} %slice.849), channel_id=1, source_target_pairs={{1,0},{2,1},{3,2},{4,3},{5,4},{6,5},{7,6},{9,8},{10,9},{11,10},{12... | collective-permute-start | bytes 73736 | tf_op jit(solution)/shard_map/ppermute | solution.py:19
  82.6 1.9 collective-permute-start.6
  84.7 4.3 %collective-permute-start.5 = (f32[3,16,16,1]{3,1,0,2:T(8,128)S(1)}, f32[3,16,16,1]{3,1,0,2:T(8,128)S(1)}, u32[]{:S(2)}, u32[]{:S(2)}) collective-permute-start(f32[3,16,16,1]{3,1,0,2:T(8,128)S(1)} %get-tuple-element.122), channel_id=1, source_target_pairs={{8,0},{16,8},{24,16},{32,24},{40,32},{48,40},{56,48},{64,56},{72,6... | collective-permute-start | bytes 9224 | tf_op jit(solution)/shard_map/ppermute | solution.py:19
  89.1 7.7 %collective-permute-done.5 = f32[3,16,16,1]{3,1,0,2:T(8,128)S(1)} collective-permute-done((f32[3,16,16,1]{3,1,0,2:T(8,128)S(1)}, f32[3,16,16,1]{3,1,0,2:T(8,128)S(1)}, u32[]{:S(2)}, u32[]{:S(2)}) %collective-permute-start.5) | collective-permute-done | bytes 3104 | tf_op jit(solution)/shard_map/ppermute | solution.py:19
  96.8 5.7 %collective-permute-done.4 = f32[3,16,16,1]{3,1,0,2:T(8,128)S(1)} collective-permute-done((f32[3,16,16,1]{3,1,0,2:T(8,128)S(1)}, f32[3,16,16,1]{3,1,0,2:T(8,128)S(1)}, u32[]{:S(2)}, u32[]{:S(2)}) %collective-permute-start.4) | collective-permute-done | bytes 3104 | tf_op jit(solution)/shard_map/ppermute | solution.py:16
  103.7 1.4 fusion.12
  106.8 1.0 broadcast_select_fusion.5
  107.8 5.0 %all-to-all-start.2 = ((f32[32,3,16,128]{3,2,1,0:T(8,128)}), f32[32,3,16,128]{3,2,1,0:T(8,128)}, u32[]{:S(2)}, u32[]{:S(2)}) async-start(f32[32,3,16,128]{3,2,1,0:T(8,128)} %broadcast_select_fusion.5), calls=%async_computation.2 | async-start | bytes 1572864 | tf_op jit(solution)/shard_map/all_to_all | solution.py:35
  112.9 5.8 %collective-permute-start.11 = (f32[3,16,1,128]{3,1,0,2:T(8,128)S(1)}, f32[3,16,1,128]{3,1,0,2:T(8,128)S(1)}, u32[]{:S(2)}, u32[]{:S(2)}) collective-permute-start(f32[3,16,1,128]{3,1,0,2:T(8,128)S(1)} %slice.870), channel_id=1, source_target_pairs={{1,0},{2,1},{3,2},{4,3},{5,4},{6,5},{7,6},{9,8},{10,9},{11,10},{12... | collective-permute-start | bytes 73736 | tf_op jit(solution)/shard_map/ppermute | solution.py:19
  118.7 1.9 collective-permute-start.10
  120.8 4.3 %collective-permute-start.9 = (f32[3,16,16,1]{3,1,0,2:T(8,128)S(1)}, f32[3,16,16,1]{3,1,0,2:T(8,128)S(1)}, u32[]{:S(2)}, u32[]{:S(2)}) collective-permute-start(f32[3,16,16,1]{3,1,0,2:T(8,128)S(1)} %get-tuple-element.120), channel_id=1, source_target_pairs={{8,0},{16,8},{24,16},{32,24},{40,32},{48,40},{56,48},{64,56},{72,6... | collective-permute-start | bytes 9224 | tf_op jit(solution)/shard_map/ppermute | solution.py:19
  125.2 9.4 %collective-permute-done.9 = f32[3,16,16,1]{3,1,0,2:T(8,128)S(1)} collective-permute-done((f32[3,16,16,1]{3,1,0,2:T(8,128)S(1)}, f32[3,16,16,1]{3,1,0,2:T(8,128)S(1)}, u32[]{:S(2)}, u32[]{:S(2)}) %collective-permute-start.9) | collective-permute-done | bytes 3104 | tf_op jit(solution)/shard_map/ppermute | solution.py:19
  134.7 5.7 %collective-permute-done.8 = f32[3,16,16,1]{3,1,0,2:T(8,128)S(1)} collective-permute-done((f32[3,16,16,1]{3,1,0,2:T(8,128)S(1)}, f32[3,16,16,1]{3,1,0,2:T(8,128)S(1)}, u32[]{:S(2)}, u32[]{:S(2)}) %collective-permute-start.8) | collective-permute-done | bytes 3104 | tf_op jit(solution)/shard_map/ppermute | solution.py:16
  140.8 1.4 fusion.13
  142.2 5.8 %collective-permute-start.15 = (f32[3,16,1,128]{3,1,0,2:T(8,128)S(1)}, f32[3,16,1,128]{3,1,0,2:T(8,128)S(1)}, u32[]{:S(2)}, u32[]{:S(2)}) collective-permute-start(f32[3,16,1,128]{3,1,0,2:T(8,128)S(1)} %slice.891), channel_id=1, source_target_pairs={{1,0},{2,1},{3,2},{4,3},{5,4},{6,5},{7,6},{9,8},{10,9},{11,10},{12... | collective-permute-start | bytes 73736 | tf_op jit(solution)/shard_map/ppermute | solution.py:19
  149.7 1.9 collective-permute-start.14
  151.7 1.0 broadcast_select_fusion.4
  152.7 4.6 %all-to-all-start.3 = ((f32[32,3,16,128]{3,2,1,0:T(8,128)}), f32[32,3,16,128]{3,2,1,0:T(8,128)}, u32[]{:S(2)}, u32[]{:S(2)}) async-start(f32[32,3,16,128]{3,2,1,0:T(8,128)} %broadcast_select_fusion.4), calls=%async_computation.3 | async-start | bytes 1572864 | tf_op jit(solution)/shard_map/all_to_all | solution.py:35
  157.4 1.0 fusion.14
  158.5 5.2 %collective-permute-start.13 = (f32[3,16,16,1]{3,1,0,2:T(8,128)S(1)}, f32[3,16,16,1]{3,1,0,2:T(8,128)S(1)}, u32[]{:S(2)}, u32[]{:S(2)}) collective-permute-start(f32[3,16,16,1]{3,1,0,2:T(8,128)S(1)} %get-tuple-element.118), channel_id=1, source_target_pairs={{8,0},{16,8},{24,16},{32,24},{40,32},{48,40},{56,48},{64,56},{72,6... | collective-permute-start | bytes 9224 | tf_op jit(solution)/shard_map/ppermute | solution.py:19
  163.8 15.3 %collective-permute-done.13 = f32[3,16,16,1]{3,1,0,2:T(8,128)S(1)} collective-permute-done((f32[3,16,16,1]{3,1,0,2:T(8,128)S(1)}, f32[3,16,16,1]{3,1,0,2:T(8,128)S(1)}, u32[]{:S(2)}, u32[]{:S(2)}) %collective-permute-start.13) | collective-permute-done | bytes 3104 | tf_op jit(solution)/shard_map/ppermute | solution.py:19
  179.1 5.7 %collective-permute-done.12 = f32[3,16,16,1]{3,1,0,2:T(8,128)S(1)} collective-permute-done((f32[3,16,16,1]{3,1,0,2:T(8,128)S(1)}, f32[3,16,16,1]{3,1,0,2:T(8,128)S(1)}, u32[]{:S(2)}, u32[]{:S(2)}) %collective-permute-start.12) | collective-permute-done | bytes 3104 | tf_op jit(solution)/shard_map/ppermute | solution.py:16
  186.5 1.0 fusion.72
  189.2 1.2 fusion.65
  190.5 1.0 broadcast_select_fusion.3
  191.5 5.0 %all-to-all-start.4 = ((f32[32,3,16,128]{3,2,1,0:T(8,128)}), f32[32,3,16,128]{3,2,1,0:T(8,128)}, u32[]{:S(2)}, u32[]{:S(2)}) async-start(f32[32,3,16,128]{3,2,1,0:T(8,128)} %broadcast_select_fusion.3), calls=%async_computation.4 | async-start | bytes 1572864 | tf_op jit(solution)/shard_map/all_to_all | solution.py:35
  196.8 5.2 %collective-permute-start.17 = (f32[3,16,16,1]{3,1,0,2:T(8,128)S(1)}, f32[3,16,16,1]{3,1,0,2:T(8,128)S(1)}, u32[]{:S(2)}, u32[]{:S(2)}) collective-permute-start(f32[3,16,16,1]{3,1,0,2:T(8,128)S(1)} %get-tuple-element.111), channel_id=1, source_target_pairs={{8,0},{16,8},{24,16},{32,24},{40,32},{48,40},{56,48},{64,56},{72,6... | collective-permute-start | bytes 9224 | tf_op jit(solution)/shard_map/ppermute | solution.py:19
  202.2 6.4 %collective-permute-start.19 = (f32[3,16,1,128]{3,1,0,2:T(8,128)S(1)}, f32[3,16,1,128]{3,1,0,2:T(8,128)S(1)}, u32[]{:S(2)}, u32[]{:S(2)}) collective-permute-start(f32[3,16,1,128]{3,1,0,2:T(8,128)S(1)} %get-tuple-element.113), channel_id=1, source_target_pairs={{1,0},{2,1},{3,2},{4,3},{5,4},{6,5},{7,6},{9,8},{10,9},{11,10},{12... | collective-permute-start | bytes 73736 | tf_op jit(solution)/shard_map/ppermute | solution.py:19
  208.6 1.9 collective-permute-start.18
  210.5 7.9 %collective-permute-done.17 = f32[3,16,16,1]{3,1,0,2:T(8,128)S(1)} collective-permute-done((f32[3,16,16,1]{3,1,0,2:T(8,128)S(1)}, f32[3,16,16,1]{3,1,0,2:T(8,128)S(1)}, u32[]{:S(2)}, u32[]{:S(2)}) %collective-permute-start.17) | collective-permute-done | bytes 3104 | tf_op jit(solution)/shard_map/ppermute | solution.py:19
  218.4 5.7 %collective-permute-done.16 = f32[3,16,16,1]{3,1,0,2:T(8,128)S(1)} collective-permute-done((f32[3,16,16,1]{3,1,0,2:T(8,128)S(1)}, f32[3,16,16,1]{3,1,0,2:T(8,128)S(1)}, u32[]{:S(2)}, u32[]{:S(2)}) %collective-permute-start.16) | collective-permute-done | bytes 3104 | tf_op jit(solution)/shard_map/ppermute | solution.py:16
  227.2 1.0 broadcast_select_fusion.2
  228.2 5.0 %all-to-all-start.5 = ((f32[32,3,16,128]{3,2,1,0:T(8,128)}), f32[32,3,16,128]{3,2,1,0:T(8,128)}, u32[]{:S(2)}, u32[]{:S(2)}) async-start(f32[32,3,16,128]{3,2,1,0:T(8,128)} %broadcast_select_fusion.2), calls=%async_computation.5 | async-start | bytes 1572864 | tf_op jit(solution)/shard_map/all_to_all | solution.py:35
  233.4 5.2 %collective-permute-start.21 = (f32[3,16,16,1]{3,1,0,2:T(8,128)S(1)}, f32[3,16,16,1]{3,1,0,2:T(8,128)S(1)}, u32[]{:S(2)}, u32[]{:S(2)}) collective-permute-start(f32[3,16,16,1]{3,1,0,2:T(8,128)S(1)} %get-tuple-element.104), channel_id=1, source_target_pairs={{8,0},{16,8},{24,16},{32,24},{40,32},{48,40},{56,48},{64,56},{72,6... | collective-permute-start | bytes 9224 | tf_op jit(solution)/shard_map/ppermute | solution.py:19
  238.7 6.4 %collective-permute-start.23 = (f32[3,16,1,128]{3,1,0,2:T(8,128)S(1)}, f32[3,16,1,128]{3,1,0,2:T(8,128)S(1)}, u32[]{:S(2)}, u32[]{:S(2)}) collective-permute-start(f32[3,16,1,128]{3,1,0,2:T(8,128)S(1)} %get-tuple-element.106), channel_id=1, source_target_pairs={{1,0},{2,1},{3,2},{4,3},{5,4},{6,5},{7,6},{9,8},{10,9},{11,10},{12... | collective-permute-start | bytes 73736 | tf_op jit(solution)/shard_map/ppermute | solution.py:19
  245.1 1.9 collective-permute-start.22
  247.0 8.0 %collective-permute-done.21 = f32[3,16,16,1]{3,1,0,2:T(8,128)S(1)} collective-permute-done((f32[3,16,16,1]{3,1,0,2:T(8,128)S(1)}, f32[3,16,16,1]{3,1,0,2:T(8,128)S(1)}, u32[]{:S(2)}, u32[]{:S(2)}) %collective-permute-start.21) | collective-permute-done | bytes 3104 | tf_op jit(solution)/shard_map/ppermute | solution.py:19
  255.0 5.7 %collective-permute-done.20 = f32[3,16,16,1]{3,1,0,2:T(8,128)S(1)} collective-permute-done((f32[3,16,16,1]{3,1,0,2:T(8,128)S(1)}, f32[3,16,16,1]{3,1,0,2:T(8,128)S(1)}, u32[]{:S(2)}, u32[]{:S(2)}) %collective-permute-start.20) | collective-permute-done | bytes 3104 | tf_op jit(solution)/shard_map/ppermute | solution.py:16
  264.0 1.0 broadcast_select_fusion.1
  265.0 5.0 %all-to-all-start.6 = ((f32[32,3,16,128]{3,2,1,0:T(8,128)}), f32[32,3,16,128]{3,2,1,0:T(8,128)}, u32[]{:S(2)}, u32[]{:S(2)}) async-start(f32[32,3,16,128]{3,2,1,0:T(8,128)} %broadcast_select_fusion.1), calls=%async_computation.6 | async-start | bytes 1572864 | tf_op jit(solution)/shard_map/all_to_all | solution.py:35
  270.2 5.2 %collective-permute-start.25 = (f32[3,16,16,1]{3,1,0,2:T(8,128)S(1)}, f32[3,16,16,1]{3,1,0,2:T(8,128)S(1)}, u32[]{:S(2)}, u32[]{:S(2)}) collective-permute-start(f32[3,16,16,1]{3,1,0,2:T(8,128)S(1)} %get-tuple-element.97), channel_id=1, source_target_pairs={{8,0},{16,8},{24,16},{32,24},{40,32},{48,40},{56,48},{64,56},{72,6... | collective-permute-start | bytes 9224 | tf_op jit(solution)/shard_map/ppermute | solution.py:19
  275.5 6.4 %collective-permute-start.27 = (f32[3,16,1,128]{3,1,0,2:T(8,128)S(1)}, f32[3,16,1,128]{3,1,0,2:T(8,128)S(1)}, u32[]{:S(2)}, u32[]{:S(2)}) collective-permute-start(f32[3,16,1,128]{3,1,0,2:T(8,128)S(1)} %get-tuple-element.99), channel_id=1, source_target_pairs={{1,0},{2,1},{3,2},{4,3},{5,4},{6,5},{7,6},{9,8},{10,9},{11,10},{12... | collective-permute-start | bytes 73736 | tf_op jit(solution)/shard_map/ppermute | solution.py:19
  281.9 1.9 collective-permute-start.26
  283.9 8.0 %collective-permute-done.25 = f32[3,16,16,1]{3,1,0,2:T(8,128)S(1)} collective-permute-done((f32[3,16,16,1]{3,1,0,2:T(8,128)S(1)}, f32[3,16,16,1]{3,1,0,2:T(8,128)S(1)}, u32[]{:S(2)}, u32[]{:S(2)}) %collective-permute-start.25) | collective-permute-done | bytes 3104 | tf_op jit(solution)/shard_map/ppermute | solution.py:19
  291.9 5.7 %collective-permute-done.24 = f32[3,16,16,1]{3,1,0,2:T(8,128)S(1)} collective-permute-done((f32[3,16,16,1]{3,1,0,2:T(8,128)S(1)}, f32[3,16,16,1]{3,1,0,2:T(8,128)S(1)}, u32[]{:S(2)}, u32[]{:S(2)}) %collective-permute-start.24) | collective-permute-done | bytes 3104 | tf_op jit(solution)/shard_map/ppermute | solution.py:16
  301.4 1.4 broadcast_in_dim.191
  302.8 9.6 %all-to-all-start.7 = ((f32[256,1,1]{2,1,0:T(1,128)}), f32[256,1,1]{2,1,0:T(1,128)S(1)}, u32[]{:S(2)}, u32[]{:S(2)}) async-start(f32[256,1,1]{2,1,0:T(1,128)} %broadcast_in_dim.191), calls=%async_computation.7 | async-start | bytes 262144 | tf_op jit(solution)/shard_map/all_to_all | solution.py:46
  313.3 11.0 %all-to-all-done.7 = f32[256,1,1]{2,1,0:T(1,128)S(1)} async-done(((f32[256,1,1]{2,1,0:T(1,128)}), f32[256,1,1]{2,1,0:T(1,128)S(1)}, u32[]{:S(2)}, u32[]{:S(2)}) %all-to-all-start.7) | async-done | bytes 1056 | tf_op jit(solution)/shard_map/all_to_all | solution.py:46
  (178 shorter events, 34.6 us)
Async XLA Ops:
  0.6 6.7 %copy-start.22 = (s32[16,16,128]{2,1,0:T(8,128)S(1)}, s32[16,16,128]{2,1,0:T(8,128)}, u32[]{:S(2)}) copy-start(s32[16,16,128]{2,1,0:T(8,128)} %param.25) | copy-start | bytes 393220
  0.6 6.7 %copy-start.18 = (f32[3,16,16,128]{3,2,1,0:T(8,128)S(1)}, f32[3,16,16,128]{3,2,1,0:T(8,128)}, u32[]{:S(2)}) copy-start(f32[3,16,16,128]{3,2,1,0:T(8,128)} %param.18) | copy-start | bytes 1179652
  2.4 138.4 %copy-start = (f32[16,16,128]{2,0,1:T(8,128)}, f32[16,16,128]{2,0,1:T(8,128)S(1)}, u32[]{:S(2)}) copy-start(f32[16,16,128]{2,0,1:T(8,128)S(1)} %copy_convert_fusion) | copy-start | bytes 393220
  3.4 5.6 %copy-start.21 = (f32[16,16,128]{2,0,1:T(8,128)}, f32[16,16,128]{2,0,1:T(8,128)S(1)}, u32[]{:S(2)}) copy-start(f32[16,16,128]{2,0,1:T(8,128)S(1)} %copy.239) | copy-start | bytes 393220
  4.4 4.6 %copy-start.23 = (f32[16,16,128]{2,0,1:T(8,128)}, f32[16,16,128]{2,0,1:T(8,128)S(1)}, u32[]{:S(2)}) copy-start(f32[16,16,128]{2,0,1:T(8,128)S(1)} %copy.238) | copy-start | bytes 393220
  7.5 28.8 %copy-start.4 = (f32[3,16,16,128]{3,1,0,2:T(8,128)}, f32[3,16,16,128]{3,1,0,2:T(8,128)S(1)}, u32[]{:S(2)}) copy-start(f32[3,16,16,128]{3,1,0,2:T(8,128)S(1)} %get-tuple-element.126) | copy-start | bytes 1179652
  9.0 57.2 %all-to-all-start = ((f32[32,6,16,128]{3,2,1,0:T(8,128)}), f32[32,6,16,128]{3,2,1,0:T(8,128)}, u32[]{:S(2)}, u32[]{:S(2)}) async-start(f32[32,6,16,128]{3,2,1,0:T(8,128)} %broadcast_select_fusion), calls=%async_computation | async-start | bytes 3145728 | tf_op jit(solution)/shard_map/all_to_all | solution.py:35
  20.2 42.7 %collective-permute-start.2 = (f32[7,16,1,128]{3,1,0,2:T(8,128)}, f32[7,16,1,128]{3,1,0,2:T(8,128)}, u32[]{:S(2)}, u32[]{:S(2)}) collective-permute-start(f32[7,16,1,128]{3,1,0,2:T(8,128)} %get-tuple-element.73), channel_id=1, source_target_pairs={{0,1},{1,2},{2,3},{3,4},{4,5},{5,6},{6,7},{8,9},{9,10},{10,11},{11... | collective-permute-start | bytes 172040 | tf_op jit(solution)/shard_map/ppermute | solution.py:16
  23.7 39.2 %collective-permute-start.3 = (f32[7,16,1,128]{3,1,0,2:T(8,128)}, f32[7,16,1,128]{3,1,0,2:T(8,128)}, u32[]{:S(2)}, u32[]{:S(2)}) collective-permute-start(f32[7,16,1,128]{3,1,0,2:T(8,128)} %get-tuple-element.74), channel_id=1, source_target_pairs={{1,0},{2,1},{3,2},{4,3},{5,4},{6,5},{7,6},{9,8},{10,9},{11,10},{12... | collective-permute-start | bytes 172040 | tf_op jit(solution)/shard_map/ppermute | solution.py:19
  28.5 6.8 %copy-start.24 = (f32[16,16,128]{2,1,0:T(8,128)S(1)}, f32[16,16,128]{2,1,0:T(8,128)}, u32[]{:S(2)}) copy-start(f32[16,16,128]{2,1,0:T(8,128)} %param.23) | copy-start | bytes 393220
  29.8 31.2 %collective-permute-start.1 = (f32[7,16,16,1]{2,1,3,0:T(8,128)}, f32[7,16,16,1]{2,1,3,0:T(8,128)S(1)}, u32[]{:S(2)}, u32[]{:S(2)}) collective-permute-start(f32[7,16,16,1]{2,1,3,0:T(8,128)} %copy.243), channel_id=1, source_target_pairs={{8,0},{16,8},{24,16},{32,24},{40,32},{48,40},{56,48},{64,56},{72,6... | collective-permute-start | bytes 21512 | tf_op jit(solution)/shard_map/ppermute | solution.py:19
  35.1 25.1 %collective-permute-start = (f32[7,16,16,1]{2,1,3,0:T(8,128)S(1)}, f32[7,16,16,1]{2,1,3,0:T(8,128)S(1)}, u32[]{:S(2)}, u32[]{:S(2)}) collective-permute-start(f32[7,16,16,1]{2,1,3,0:T(8,128)S(1)} %copy.241), channel_id=1, source_target_pairs={{0,8},{8,16},{16,24},{24,32},{32,40},{40,48},{48,56},{56,64},{64,7... | collective-permute-start | bytes 21512 | tf_op jit(solution)/shard_map/ppermute | solution.py:16
  62.1 0.7 copy-start.2
  62.8 2.0 copy-start.10
  62.8 2.0 copy-start.5
  62.8 2.0 copy-start.6
  62.8 2.0 copy-start.19
  62.8 2.0 copy-start.25
  66.2 3.8 %copy-start.11 = (f32[3,16,16,128]{3,1,0,2:T(8,128)}, f32[3,16,16,128]{3,1,0,2:T(8,128)S(1)}, u32[]{:S(2)}) copy-start(f32[3,16,16,128]{3,1,0,2:T(8,128)S(1)} %get-tuple-element.124) | copy-start | bytes 1179652
  70.0 35.1 %all-to-all-start.1 = ((f32[32,3,16,128]{3,2,1,0:T(8,128)}), f32[32,3,16,128]{3,2,1,0:T(8,128)}, u32[]{:S(2)}, u32[]{:S(2)}) async-start(f32[32,3,16,128]{3,2,1,0:T(8,128)} %broadcast_select_fusion.6), calls=%async_computation.1 | async-start | bytes 1572864 | tf_op jit(solution)/shard_map/all_to_all | solution.py:35
  75.0 27.5 %copy-start.3 = (f32[16,16,129]{2,0,1:T(8,128)S(1)}, f32[16,16,129]{2,0,1:T(8,128)}, u32[]{:S(2)}) copy-start(f32[16,16,129]{2,0,1:T(8,128)} %copy-done.2) | copy-start | bytes 396292
  76.8 26.0 %collective-permute-start.7 = (f32[3,16,1,128]{3,1,0,2:T(8,128)S(1)}, f32[3,16,1,128]{3,1,0,2:T(8,128)S(1)}, u32[]{:S(2)}, u32[]{:S(2)}) collective-permute-start(f32[3,16,1,128]{3,1,0,2:T(8,128)S(1)} %slice.849), channel_id=1, source_target_pairs={{1,0},{2,1},{3,2},{4,3},{5,4},{6,5},{7,6},{9,8},{10,9},{11,10},{12... | collective-permute-start | bytes 73736 | tf_op jit(solution)/shard_map/ppermute | solution.py:19
  82.6 20.3 %collective-permute-start.6 = (f32[3,16,1,128]{3,1,0,2:T(8,128)S(1)}, f32[3,16,1,128]{3,1,0,2:T(8,128)S(1)}, u32[]{:S(2)}, u32[]{:S(2)}) collective-permute-start(f32[3,16,1,128]{3,1,0,2:T(8,128)S(1)} %fusion.156), channel_id=1, source_target_pairs={{0,1},{1,2},{2,3},{3,4},{4,5},{5,6},{6,7},{8,9},{9,10},{10,11},{11... | collective-permute-start | bytes 73736 | tf_op jit(solution)/shard_map/ppermute | solution.py:16
  84.7 12.1 %collective-permute-start.5 = (f32[3,16,16,1]{3,1,0,2:T(8,128)S(1)}, f32[3,16,16,1]{3,1,0,2:T(8,128)S(1)}, u32[]{:S(2)}, u32[]{:S(2)}) collective-permute-start(f32[3,16,16,1]{3,1,0,2:T(8,128)S(1)} %get-tuple-element.122), channel_id=1, source_target_pairs={{8,0},{16,8},{24,16},{32,24},{40,32},{48,40},{56,48},{64,56},{72,6... | collective-permute-start | bytes 9224 | tf_op jit(solution)/shard_map/ppermute | solution.py:19
  89.1 13.4 %collective-permute-start.4 = (f32[3,16,16,1]{3,1,0,2:T(8,128)S(1)}, f32[3,16,16,1]{3,1,0,2:T(8,128)S(1)}, u32[]{:S(2)}, u32[]{:S(2)}) collective-permute-start(f32[3,16,16,1]{3,1,0,2:T(8,128)S(1)} %get-tuple-element.123), channel_id=1, source_target_pairs={{0,8},{8,16},{16,24},{24,32},{32,40},{40,48},{48,56},{56,64},{64,7... | collective-permute-start | bytes 9224 | tf_op jit(solution)/shard_map/ppermute | solution.py:16
  102.8 0.9 copy-start.9
  107.8 40.2 %all-to-all-start.2 = ((f32[32,3,16,128]{3,2,1,0:T(8,128)}), f32[32,3,16,128]{3,2,1,0:T(8,128)}, u32[]{:S(2)}, u32[]{:S(2)}) async-start(f32[32,3,16,128]{3,2,1,0:T(8,128)} %broadcast_select_fusion.5), calls=%async_computation.2 | async-start | bytes 1572864 | tf_op jit(solution)/shard_map/all_to_all | solution.py:35
  112.9 27.8 %collective-permute-start.11 = (f32[3,16,1,128]{3,1,0,2:T(8,128)S(1)}, f32[3,16,1,128]{3,1,0,2:T(8,128)S(1)}, u32[]{:S(2)}, u32[]{:S(2)}) collective-permute-start(f32[3,16,1,128]{3,1,0,2:T(8,128)S(1)} %slice.870), channel_id=1, source_target_pairs={{1,0},{2,1},{3,2},{4,3},{5,4},{6,5},{7,6},{9,8},{10,9},{11,10},{12... | collective-permute-start | bytes 73736 | tf_op jit(solution)/shard_map/ppermute | solution.py:19
  118.7 22.0 %collective-permute-start.10 = (f32[3,16,1,128]{3,1,0,2:T(8,128)S(1)}, f32[3,16,1,128]{3,1,0,2:T(8,128)S(1)}, u32[]{:S(2)}, u32[]{:S(2)}) collective-permute-start(f32[3,16,1,128]{3,1,0,2:T(8,128)S(1)} %fusion.154), channel_id=1, source_target_pairs={{0,1},{1,2},{2,3},{3,4},{4,5},{5,6},{6,7},{8,9},{9,10},{10,11},{11... | collective-permute-start | bytes 73736 | tf_op jit(solution)/shard_map/ppermute | solution.py:16
  120.8 13.9 %collective-permute-start.9 = (f32[3,16,16,1]{3,1,0,2:T(8,128)S(1)}, f32[3,16,16,1]{3,1,0,2:T(8,128)S(1)}, u32[]{:S(2)}, u32[]{:S(2)}) collective-permute-start(f32[3,16,16,1]{3,1,0,2:T(8,128)S(1)} %get-tuple-element.120), channel_id=1, source_target_pairs={{8,0},{16,8},{24,16},{32,24},{40,32},{48,40},{56,48},{64,56},{72,6... | collective-permute-start | bytes 9224 | tf_op jit(solution)/shard_map/ppermute | solution.py:19
  125.2 15.2 %collective-permute-start.8 = (f32[3,16,16,1]{3,1,0,2:T(8,128)S(1)}, f32[3,16,16,1]{3,1,0,2:T(8,128)S(1)}, u32[]{:S(2)}, u32[]{:S(2)}) collective-permute-start(f32[3,16,16,1]{3,1,0,2:T(8,128)S(1)} %get-tuple-element.121), channel_id=1, source_target_pairs={{0,8},{8,16},{16,24},{24,32},{32,40},{40,48},{48,56},{56,64},{64,7... | collective-permute-start | bytes 9224 | tf_op jit(solution)/shard_map/ppermute | solution.py:16
  140.7 1.5 copy-start.7
  142.2 43.2 %collective-permute-start.15 = (f32[3,16,1,128]{3,1,0,2:T(8,128)S(1)}, f32[3,16,1,128]{3,1,0,2:T(8,128)S(1)}, u32[]{:S(2)}, u32[]{:S(2)}) collective-permute-start(f32[3,16,1,128]{3,1,0,2:T(8,128)S(1)} %slice.891), channel_id=1, source_target_pairs={{1,0},{2,1},{3,2},{4,3},{5,4},{6,5},{7,6},{9,8},{10,9},{11,10},{12... | collective-permute-start | bytes 73736 | tf_op jit(solution)/shard_map/ppermute | solution.py:19
  149.7 35.7 %collective-permute-start.14 = (f32[3,16,1,128]{3,1,0,2:T(8,128)S(1)}, f32[3,16,1,128]{3,1,0,2:T(8,128)S(1)}, u32[]{:S(2)}, u32[]{:S(2)}) collective-permute-start(f32[3,16,1,128]{3,1,0,2:T(8,128)S(1)} %fusion.152), channel_id=1, source_target_pairs={{0,1},{1,2},{2,3},{3,4},{4,5},{5,6},{6,7},{8,9},{9,10},{10,11},{11... | collective-permute-start | bytes 73736 | tf_op jit(solution)/shard_map/ppermute | solution.py:16
  152.7 34.7 %all-to-all-start.3 = ((f32[32,3,16,128]{3,2,1,0:T(8,128)}), f32[32,3,16,128]{3,2,1,0:T(8,128)}, u32[]{:S(2)}, u32[]{:S(2)}) async-start(f32[32,3,16,128]{3,2,1,0:T(8,128)} %broadcast_select_fusion.4), calls=%async_computation.3 | async-start | bytes 1572864 | tf_op jit(solution)/shard_map/all_to_all | solution.py:35
  158.3 27.7 %copy-start.20 = (f32[3,16,16,128]{3,1,0,2:T(8,128)}, f32[3,16,16,128]{3,1,0,2:T(8,128)S(1)}, u32[]{:S(2)}) copy-start(f32[3,16,16,128]{3,1,0,2:T(8,128)S(1)} %get-tuple-element.94) | copy-start | bytes 1179652
  158.5 20.6 %collective-permute-start.13 = (f32[3,16,16,1]{3,1,0,2:T(8,128)S(1)}, f32[3,16,16,1]{3,1,0,2:T(8,128)S(1)}, u32[]{:S(2)}, u32[]{:S(2)}) collective-permute-start(f32[3,16,16,1]{3,1,0,2:T(8,128)S(1)} %get-tuple-element.118), channel_id=1, source_target_pairs={{8,0},{16,8},{24,16},{32,24},{40,32},{48,40},{56,48},{64,56},{72,6... | collective-permute-start | bytes 9224 | tf_op jit(solution)/shard_map/ppermute | solution.py:19
  163.8 21.1 %collective-permute-start.12 = (f32[3,16,16,1]{3,1,0,2:T(8,128)S(1)}, f32[3,16,16,1]{3,1,0,2:T(8,128)S(1)}, u32[]{:S(2)}, u32[]{:S(2)}) collective-permute-start(f32[3,16,16,1]{3,1,0,2:T(8,128)S(1)} %get-tuple-element.119), channel_id=1, source_target_pairs={{0,8},{8,16},{16,24},{24,32},{32,40},{40,48},{48,56},{56,64},{64,7... | collective-permute-start | bytes 9224 | tf_op jit(solution)/shard_map/ppermute | solution.py:16
  185.2 0.9 copy-start.8
  185.2 1.0 slice-start
  185.2 1.3 copy-start.12
  186.5 2.6 copy-start.1
  191.5 33.9 %all-to-all-start.4 = ((f32[32,3,16,128]{3,2,1,0:T(8,128)}), f32[32,3,16,128]{3,2,1,0:T(8,128)}, u32[]{:S(2)}, u32[]{:S(2)}) async-start(f32[32,3,16,128]{3,2,1,0:T(8,128)} %broadcast_select_fusion.3), calls=%async_computation.4 | async-start | bytes 1572864 | tf_op jit(solution)/shard_map/all_to_all | solution.py:35
  196.8 21.5 %collective-permute-start.17 = (f32[3,16,16,1]{3,1,0,2:T(8,128)S(1)}, f32[3,16,16,1]{3,1,0,2:T(8,128)S(1)}, u32[]{:S(2)}, u32[]{:S(2)}) collective-permute-start(f32[3,16,16,1]{3,1,0,2:T(8,128)S(1)} %get-tuple-element.111), channel_id=1, source_target_pairs={{8,0},{16,8},{24,16},{32,24},{40,32},{48,40},{56,48},{64,56},{72,6... | collective-permute-start | bytes 9224 | tf_op jit(solution)/shard_map/ppermute | solution.py:19
  202.1 21.9 %collective-permute-start.16 = (f32[3,16,16,1]{3,1,0,2:T(8,128)S(1)}, f32[3,16,16,1]{3,1,0,2:T(8,128)S(1)}, u32[]{:S(2)}, u32[]{:S(2)}) collective-permute-start(f32[3,16,16,1]{3,1,0,2:T(8,128)S(1)} %get-tuple-element.112), channel_id=1, source_target_pairs={{0,8},{8,16},{16,24},{24,32},{32,40},{40,48},{48,56},{56,64},{64,7... | collective-permute-start | bytes 9224 | tf_op jit(solution)/shard_map/ppermute | solution.py:16
  202.2 22.2 %collective-permute-start.19 = (f32[3,16,1,128]{3,1,0,2:T(8,128)S(1)}, f32[3,16,1,128]{3,1,0,2:T(8,128)S(1)}, u32[]{:S(2)}, u32[]{:S(2)}) collective-permute-start(f32[3,16,1,128]{3,1,0,2:T(8,128)S(1)} %get-tuple-element.113), channel_id=1, source_target_pairs={{1,0},{2,1},{3,2},{4,3},{5,4},{6,5},{7,6},{9,8},{10,9},{11,10},{12... | collective-permute-start | bytes 73736 | tf_op jit(solution)/shard_map/ppermute | solution.py:19
  208.6 15.8 %collective-permute-start.18 = (f32[3,16,1,128]{3,1,0,2:T(8,128)S(1)}, f32[3,16,1,128]{3,1,0,2:T(8,128)S(1)}, u32[]{:S(2)}, u32[]{:S(2)}) collective-permute-start(f32[3,16,1,128]{3,1,0,2:T(8,128)S(1)} %get-tuple-element.115), channel_id=1, source_target_pairs={{0,1},{1,2},{2,3},{3,4},{4,5},{5,6},{6,7},{8,9},{9,10},{10,11},{11... | collective-permute-start | bytes 73736 | tf_op jit(solution)/shard_map/ppermute | solution.py:16
  224.3 1.0 copy-start.17
  228.2 34.0 %all-to-all-start.5 = ((f32[32,3,16,128]{3,2,1,0:T(8,128)}), f32[32,3,16,128]{3,2,1,0:T(8,128)}, u32[]{:S(2)}, u32[]{:S(2)}) async-start(f32[32,3,16,128]{3,2,1,0:T(8,128)} %broadcast_select_fusion.2), calls=%async_computation.5 | async-start | bytes 1572864 | tf_op jit(solution)/shard_map/all_to_all | solution.py:35
  233.4 21.7 %collective-permute-start.21 = (f32[3,16,16,1]{3,1,0,2:T(8,128)S(1)}, f32[3,16,16,1]{3,1,0,2:T(8,128)S(1)}, u32[]{:S(2)}, u32[]{:S(2)}) collective-permute-start(f32[3,16,16,1]{3,1,0,2:T(8,128)S(1)} %get-tuple-element.104), channel_id=1, source_target_pairs={{8,0},{16,8},{24,16},{32,24},{40,32},{48,40},{56,48},{64,56},{72,6... | collective-permute-start | bytes 9224 | tf_op jit(solution)/shard_map/ppermute | solution.py:19
  238.6 22.1 %collective-permute-start.20 = (f32[3,16,16,1]{3,1,0,2:T(8,128)S(1)}, f32[3,16,16,1]{3,1,0,2:T(8,128)S(1)}, u32[]{:S(2)}, u32[]{:S(2)}) collective-permute-start(f32[3,16,16,1]{3,1,0,2:T(8,128)S(1)} %get-tuple-element.105), channel_id=1, source_target_pairs={{0,8},{8,16},{16,24},{24,32},{32,40},{40,48},{48,56},{56,64},{64,7... | collective-permute-start | bytes 9224 | tf_op jit(solution)/shard_map/ppermute | solution.py:16
  238.7 22.3 %collective-permute-start.23 = (f32[3,16,1,128]{3,1,0,2:T(8,128)S(1)}, f32[3,16,1,128]{3,1,0,2:T(8,128)S(1)}, u32[]{:S(2)}, u32[]{:S(2)}) collective-permute-start(f32[3,16,1,128]{3,1,0,2:T(8,128)S(1)} %get-tuple-element.106), channel_id=1, source_target_pairs={{1,0},{2,1},{3,2},{4,3},{5,4},{6,5},{7,6},{9,8},{10,9},{11,10},{12... | collective-permute-start | bytes 73736 | tf_op jit(solution)/shard_map/ppermute | solution.py:19
  245.1 15.9 %collective-permute-start.22 = (f32[3,16,1,128]{3,1,0,2:T(8,128)S(1)}, f32[3,16,1,128]{3,1,0,2:T(8,128)S(1)}, u32[]{:S(2)}, u32[]{:S(2)}) collective-permute-start(f32[3,16,1,128]{3,1,0,2:T(8,128)S(1)} %get-tuple-element.107), channel_id=1, source_target_pairs={{0,1},{1,2},{2,3},{3,4},{4,5},{5,6},{6,7},{8,9},{9,10},{10,11},{11... | collective-permute-start | bytes 73736 | tf_op jit(solution)/shard_map/ppermute | solution.py:16
  261.0 1.1 copy-start.14
  261.3 0.8 copy-start.16
  265.0 34.0 %all-to-all-start.6 = ((f32[32,3,16,128]{3,2,1,0:T(8,128)}), f32[32,3,16,128]{3,2,1,0:T(8,128)}, u32[]{:S(2)}, u32[]{:S(2)}) async-start(f32[32,3,16,128]{3,2,1,0:T(8,128)} %broadcast_select_fusion.1), calls=%async_computation.6 | async-start | bytes 1572864 | tf_op jit(solution)/shard_map/all_to_all | solution.py:35
  270.2 21.7 %collective-permute-start.25 = (f32[3,16,16,1]{3,1,0,2:T(8,128)S(1)}, f32[3,16,16,1]{3,1,0,2:T(8,128)S(1)}, u32[]{:S(2)}, u32[]{:S(2)}) collective-permute-start(f32[3,16,16,1]{3,1,0,2:T(8,128)S(1)} %get-tuple-element.97), channel_id=1, source_target_pairs={{8,0},{16,8},{24,16},{32,24},{40,32},{48,40},{56,48},{64,56},{72,6... | collective-permute-start | bytes 9224 | tf_op jit(solution)/shard_map/ppermute | solution.py:19
  275.4 22.1 %collective-permute-start.24 = (f32[3,16,16,1]{3,1,0,2:T(8,128)S(1)}, f32[3,16,16,1]{3,1,0,2:T(8,128)S(1)}, u32[]{:S(2)}, u32[]{:S(2)}) collective-permute-start(f32[3,16,16,1]{3,1,0,2:T(8,128)S(1)} %get-tuple-element.98), channel_id=1, source_target_pairs={{0,8},{8,16},{16,24},{24,32},{32,40},{40,48},{48,56},{56,64},{64,7... | collective-permute-start | bytes 9224 | tf_op jit(solution)/shard_map/ppermute | solution.py:16
  275.5 22.3 %collective-permute-start.27 = (f32[3,16,1,128]{3,1,0,2:T(8,128)S(1)}, f32[3,16,1,128]{3,1,0,2:T(8,128)S(1)}, u32[]{:S(2)}, u32[]{:S(2)}) collective-permute-start(f32[3,16,1,128]{3,1,0,2:T(8,128)S(1)} %get-tuple-element.99), channel_id=1, source_target_pairs={{1,0},{2,1},{3,2},{4,3},{5,4},{6,5},{7,6},{9,8},{10,9},{11,10},{12... | collective-permute-start | bytes 73736 | tf_op jit(solution)/shard_map/ppermute | solution.py:19
  281.9 15.9 %collective-permute-start.26 = (f32[3,16,1,128]{3,1,0,2:T(8,128)S(1)}, f32[3,16,1,128]{3,1,0,2:T(8,128)S(1)}, u32[]{:S(2)}, u32[]{:S(2)}) collective-permute-start(f32[3,16,1,128]{3,1,0,2:T(8,128)S(1)} %get-tuple-element.100), channel_id=1, source_target_pairs={{0,1},{1,2},{2,3},{3,4},{4,5},{5,6},{6,7},{8,9},{9,10},{10,11},{11... | collective-permute-start | bytes 73736 | tf_op jit(solution)/shard_map/ppermute | solution.py:16
  297.8 1.1 copy-start.13
  298.1 0.8 copy-start.15
  302.8 21.5 %all-to-all-start.7 = ((f32[256,1,1]{2,1,0:T(1,128)}), f32[256,1,1]{2,1,0:T(1,128)S(1)}, u32[]{:S(2)}, u32[]{:S(2)}) async-start(f32[256,1,1]{2,1,0:T(1,128)} %broadcast_in_dim.191), calls=%async_computation.7 | async-start | bytes 262144 | tf_op jit(solution)/shard_map/all_to_all | solution.py:46
